TPU v7x, 256 devices: a whole 4x4x8 slice. The times are simulated.
256 devices in a mesh: ctx: 64 (over z, y, core), tp: 4 (over x).
Axes of the slice: x: 4, y: 4, z: 8, core: 2. Of those that a mesh axis runs over, the one named last changes fastest.
Arguments:
- queries: bfloat16 [8192, 32, 128], P('ctx', 'tp'), may hold values from -25 to 25
- key_vectors: bfloat16 [8192, 4, 128], P('ctx', 'tp'), may hold values from -6 to 6
- value_vectors: bfloat16 [8192, 4, 128], P('ctx', 'tp'), may hold values from -6 to 6
- attention_out: bfloat16 [8192, 32, 128], P('ctx', 'tp'), may hold values from -6 to 6
- grad_attention: bfloat16 [8192, 32, 128], P('ctx', 'tp'), may hold values from -6 to 6
- mix_input: bfloat16 [8192, 8192], P('ctx', 'tp'), may hold values from -0.0625 to 0.0625
- grad_mix: bfloat16 [8192, 8192], P('ctx', 'tp'), may hold values from -6 to 6
- input_map: float32 [8192, 16], P('ctx'), may hold values from -0.375 to 0.375
- output_map: float32 [8192, 16], P('ctx'), may hold values from -0.375 to 0.375
- decay_log: float32 [8192, 128], P('ctx', 'tp'), may hold values from -0.6 to 0
Outputs:
- grad_queries: bfloat16 [8192, 32, 128], P('ctx', 'tp')
- grad_keys: bfloat16 [8192, 4, 128], P('ctx', 'tp')
- grad_values: bfloat16 [8192, 4, 128], P('ctx', 'tp')
- grad_input: bfloat16 [8192, 8192], P('ctx', 'tp')
- grad_input_map: float32 [8192, 16], P('ctx')
- grad_output_map: float32 [8192, 16], P('ctx')
- grad_decay: float32 [8192, 128], P('ctx', 'tp')
All inputs are finite; a program needn't handle non-finite values.
Results may differ from a plain program's by a relative error of at most 0.0052.
Values may be sent and summed in bfloat16 or wider, within the bound.
No kernel may reach another device: no remote copies, remote signals or barrier semaphores. Data moves between devices by JAX's collectives and lax.ppermute only.
A program may use at most 128 MiB of HBM per device.

v0:
```python
import math

import jax
import jax.numpy as jnp
from jax import lax
from jax.sharding import PartitionSpec as P


def carried_in(x, axis, combine, identity, reverse):
    length, here = (lax.axis_size(axis), lax.axis_index(axis))
    everything = jax.tree.map(lambda part: lax.all_gather(part, axis), x)
    start = jax.tree.map(
        lambda part, zero: jnp.broadcast_to(jnp.asarray(zero, part.dtype), part.shape), x, identity
    )

    def turn(k, before):
        at = length - 1 - k if reverse else k
        reached = at > here if reverse else at < here
        new = combine(before, jax.tree.map(lambda part: part[at], everything))
        return jax.tree.map(lambda a, b: jnp.where(reached, a, b), new, before)

    return lax.fori_loop(0, length, turn, start)


def blend_states(earlier, later):
    decay_early, state_early = earlier
    decay_later, state_later = later
    return (decay_early * decay_later, decay_later[..., None, None] * state_early + state_later)


def attention_grads(queries, key_vectors, value_vectors, attention_out, grad_attention):
    local_rows, local_heads, head_width = queries.shape
    local_groups = key_vectors.shape[1]
    repeats = local_heads // local_groups
    score_scale = 1.0 / math.sqrt(head_width)
    whole_keys, whole_values = (
        lax.all_gather(key_vectors, "ctx", axis=0, tiled=True),
        lax.all_gather(value_vectors, "ctx", axis=0, tiled=True),
    )
    all_tokens = whole_keys.shape[0]
    key_block = math.gcd(all_tokens, 1024)
    here = lax.axis_index("ctx")

    def scores_of(entry, first_row, length):
        query_grp, query_pos = (entry[0], entry[3])
        key_part = lax.dynamic_slice_in_dim(whole_keys, first_row, length, 0)
        scores = (
            jnp.einsum("tgrd,kgd->gtrk", query_grp, key_part, preferred_element_type=jnp.float32)
            * score_scale
        )
        key_pos = first_row + jnp.arange(length)
        allowed = key_pos[None, :] <= query_pos[:, None]
        return (jnp.where(allowed[None, :, None, :], scores, -jnp.inf), key_part)

    first_pos = here * local_rows
    row_count = queries.shape[0]
    query_grp = queries.reshape(row_count, local_groups, repeats, head_width)
    grad_grp = grad_attention.reshape(row_count, local_groups, repeats, head_width)
    out_dots = jnp.sum(
        grad_attention.astype(jnp.float32) * attention_out.astype(jnp.float32), axis=-1
    )
    out_dots = out_dots.reshape(row_count, local_groups, repeats).transpose(1, 0, 2)
    query_pos = first_pos + jnp.arange(row_count)
    last_query = first_pos + row_count - 1
    live_blocks = last_query // key_block + 1
    partial_entry = (query_grp, grad_grp, out_dots, query_pos)

    def stats_step(block_index, carry):
        run_max, run_total = carry
        scores, unused_keys = scores_of(partial_entry, block_index * key_block, key_block)
        new_max = jnp.maximum(run_max, jnp.max(scores, axis=-1))
        run_total = run_total * jnp.exp(run_max - new_max) + jnp.sum(
            jnp.exp(scores - new_max[..., None]), axis=-1
        )
        return (new_max, run_total)

    start_max = jnp.full((local_groups, row_count, repeats), -jnp.inf, jnp.float32)
    start_total = jnp.zeros((local_groups, row_count, repeats), jnp.float32)
    run_max, run_total = lax.fori_loop(0, live_blocks, stats_step, (start_max, start_total))
    log_total = run_max + jnp.log(run_total)
    entries = (query_grp, grad_grp, out_dots, query_pos, last_query, live_blocks, log_total)

    def block_terms(entry, first_row, length):
        query_grp, grad_grp, out_dots, log_total = (entry[0], entry[1], entry[2], entry[6])
        scores, key_part = scores_of(entry, first_row, length)
        value_part = lax.dynamic_slice_in_dim(whole_values, first_row, length, 0)
        probs = jnp.exp(scores - log_total[..., None])
        grad_probs = jnp.einsum(
            "tgrd,kgd->gtrk", grad_grp, value_part, preferred_element_type=jnp.float32
        )
        grad_scores = (probs * (grad_probs - out_dots[..., None]) * score_scale).astype(
            jnp.bfloat16
        )
        query_add = None
        key_term = None
        query_add = jnp.einsum(
            "gtrk,kgd->tgrd", grad_scores, key_part, preferred_element_type=jnp.float32
        )
        probs_low = probs.astype(jnp.bfloat16)
        value_term = jnp.einsum(
            "gtrk,tgrd->kgd", probs_low, grad_grp, preferred_element_type=jnp.float32
        )
        keys_term = jnp.einsum(
            "gtrk,tgrd->kgd", grad_scores, query_grp, preferred_element_type=jnp.float32
        )
        key_term = jnp.stack([keys_term, value_term], axis=1)
        return (query_add, key_term)

    buffer = jnp.zeros((all_tokens, 2, local_groups, head_width), jnp.float32)
    entry = entries

    def joint_step(block_index, carry, entry=entry):
        query_acc, acc = carry
        first_row = block_index * key_block
        query_add, key_term = block_terms(entry, first_row, key_block)
        current = lax.dynamic_slice_in_dim(acc, first_row, key_block, 0)
        return (
            query_acc + query_add,
            lax.dynamic_update_slice_in_dim(acc, current + key_term, first_row, 0),
        )

    query_start = jnp.zeros(entry[0].shape, jnp.float32)
    query_acc, buffer = lax.fori_loop(0, entry[5], joint_step, (query_start, buffer))
    key_rows = lax.psum_scatter(buffer, "ctx", scatter_dimension=0, tiled=True)
    grad_queries = query_acc.reshape(local_rows, local_heads, head_width).astype(jnp.bfloat16)
    return (grad_queries, key_rows[:, 0].astype(jnp.bfloat16), key_rows[:, 1].astype(jnp.bfloat16))


def mixer_grads(mix_input, grad_mix, input_map, output_map, decay_log):
    local_rows, channels = mix_input.shape
    local_heads = decay_log.shape[1]
    head_width = channels // local_heads
    state_size = input_map.shape[1]
    span_len = math.gcd(local_rows, 128)
    span_count = local_rows // span_len
    highest = lax.Precision.HIGHEST
    inputs_f = mix_input.astype(jnp.float32).reshape(span_count, span_len, local_heads, head_width)
    grads_f = grad_mix.astype(jnp.float32).reshape(span_count, span_len, local_heads, head_width)
    in_maps = input_map.reshape(span_count, span_len, state_size)
    out_maps = output_map.reshape(span_count, span_len, state_size)
    cum_log = jnp.cumsum(decay_log.reshape(span_count, span_len, local_heads), axis=1)
    total_log = cum_log[:, -1]
    to_end = jnp.exp(total_log[:, None, :] - cum_log)
    from_start = jnp.exp(cum_log)
    span_decay = jnp.exp(total_log)
    ends = jnp.einsum("cshp,csn->chpn", inputs_f * to_end[..., None], in_maps, precision=highest)
    pulls = jnp.einsum(
        "cshp,csn->chpn", grads_f * from_start[..., None], out_maps, precision=highest
    )
    fwd_decay, fwd_state = lax.associative_scan(blend_states, (span_decay, ends), axis=0)
    bwd_decay, bwd_state = lax.associative_scan(
        blend_states, (span_decay[::-1], pulls[::-1]), axis=0
    )
    bwd_decay = bwd_decay[::-1]
    bwd_state = bwd_state[::-1]
    identity = (
        jnp.ones((local_heads,), jnp.float32),
        jnp.zeros((local_heads, head_width, state_size), jnp.float32),
    )
    unused_a, state_in = carried_in(
        (fwd_decay[-1], fwd_state[-1]), "ctx", blend_states, identity, False
    )
    unused_b, pull_out = carried_in(
        (bwd_decay[0], bwd_state[0]), "ctx", blend_states, identity, True
    )
    ones_row = jnp.ones((1, local_heads), jnp.float32)
    zero_row = jnp.zeros((1, local_heads, head_width, state_size), jnp.float32)
    prev_decay = jnp.concatenate([ones_row, fwd_decay[:-1]], axis=0)
    prev_state = jnp.concatenate([zero_row, fwd_state[:-1]], axis=0)
    start_states = prev_decay[..., None, None] * state_in[None] + prev_state
    next_decay = jnp.concatenate([bwd_decay[1:], ones_row], axis=0)
    next_pull = jnp.concatenate([bwd_state[1:], zero_row], axis=0)
    end_pulls = next_decay[..., None, None] * pull_out[None] + next_pull
    token_positions = jnp.arange(span_len)
    lower = token_positions[:, None] >= token_positions[None, :]
    cum_heads = cum_log.transpose(0, 2, 1)
    log_gap = cum_heads[:, :, :, None] - cum_heads[:, :, None, :]
    decay_mat = jnp.exp(jnp.where(lower[None, None], log_gap, -jnp.inf))
    map_dots = jnp.einsum("ctn,csn->cts", out_maps, in_maps, precision=highest)
    weights = decay_mat * map_dots[:, None]
    grad_in_f = jnp.einsum("chts,cthp->cshp", weights, grads_f, precision=highest)
    grad_in_f = grad_in_f + to_end[..., None] * jnp.einsum(
        "chpn,csn->cshp", end_pulls, in_maps, precision=highest
    )
    pair_dots = jnp.einsum("cthp,cshp->chts", grads_f, inputs_f, precision=highest)
    kernel = decay_mat * pair_dots
    kernel_sum = jnp.sum(kernel, axis=1)
    in_map_part = jnp.einsum("cts,ctn->csn", kernel_sum, out_maps, precision=highest)
    in_map_part = in_map_part + jnp.einsum(
        "csh,cshp,chpn->csn", to_end, inputs_f, end_pulls, precision=highest
    )
    out_map_part = jnp.einsum("cts,csn->ctn", kernel_sum, in_maps, precision=highest)
    out_map_part = out_map_part + jnp.einsum(
        "cth,cthp,chpn->ctn", from_start, grads_f, start_states, precision=highest
    )
    grad_in_map, grad_out_map = lax.psum(
        (in_map_part.reshape(local_rows, state_size), out_map_part.reshape(local_rows, state_size)),
        "tp",
    )
    mixed = kernel * map_dots[:, None]
    row_part = jnp.sum(mixed, axis=-1).transpose(0, 2, 1)
    col_part = jnp.sum(mixed, axis=-2).transpose(0, 2, 1)
    start_part = from_start * jnp.einsum(
        "cthp,chpn,ctn->cth", grads_f, start_states, out_maps, precision=highest
    )
    end_part = to_end * jnp.einsum(
        "cshp,chpn,csn->csh", inputs_f, end_pulls, in_maps, precision=highest
    )
    end_total = jnp.sum(end_part, axis=1) + span_decay * jnp.sum(
        end_pulls * start_states, axis=(2, 3)
    )
    per_log = row_part - col_part + start_part - end_part
    suffix = jnp.cumsum(per_log[:, ::-1], axis=1)[:, ::-1]
    grad_decay = (suffix + end_total[:, None, :]).reshape(local_rows, local_heads)
    grad_input = grad_in_f.reshape(local_rows, channels).astype(jnp.bfloat16)
    return (grad_input, grad_in_map, grad_out_map, grad_decay)


def local(
    queries,
    key_vectors,
    value_vectors,
    attention_out,
    grad_attention,
    mix_input,
    grad_mix,
    input_map,
    output_map,
    decay_log,
):
    grad_queries, grad_keys, grad_values = attention_grads(
        queries, key_vectors, value_vectors, attention_out, grad_attention
    )
    grad_input, grad_in_map, grad_out_map, grad_decay = mixer_grads(
        mix_input, grad_mix, input_map, output_map, decay_log
    )
    return (grad_queries, grad_keys, grad_values, grad_input, grad_in_map, grad_out_map, grad_decay)


def solution(mesh):
    in_specs = (
        P("ctx", "tp", None),
        P("ctx", "tp", None),
        P("ctx", "tp", None),
        P("ctx", "tp", None),
        P("ctx", "tp", None),
        P("ctx", "tp"),
        P("ctx", "tp"),
        P("ctx", None),
        P("ctx", None),
        P("ctx", "tp"),
    )
    out_specs = (
        P("ctx", "tp", None),
        P("ctx", "tp", None),
        P("ctx", "tp", None),
        P("ctx", "tp"),
        P("ctx", None),
        P("ctx", None),
        P("ctx", "tp"),
    )
    return jax.shard_map(local, mesh=mesh, in_specs=in_specs, out_specs=out_specs, check_vma=False)
```

profile of v0, /device:TPU:2, one launch (start us, length us, event | category | flops | bytes accessed | tf_op | source)
XLA Modules:
  0.0 618.6 jit_solution(8449157056863351498)
XLA Ops:
  9.6 1.3 copy.80
  11.2 4.0 fusion.65
  15.9 42.9 %all-gather = f32[64,1,32]{2,1,0:T(1,128)S(1)} all-gather(f32[1,1,32]{2,1,0:T(1,128)S(1)} %get-tuple-element.533), channel_id=2, replica_groups=mesh['ctx'=64,'tp'=4] {'ctx'}, dimensions={0}, use_global_device_ids=true | all-gather | bytes 8320 | tf_op jit(solution)/shard_map/all_gather | solution.py:11
  58.9 32.2 %all-gather.8.cloned.1.call-done = bf16[8192,1,128]{2,0,1:T(8,128)(2,1)} async-done(((bf16[128,1,128]{2,0,1:T(8,128)(2,1)}), bf16[8192,1,128]{2,0,1:T(8,128)(2,1)}) %all-gather.8.cloned.1.call-update) | async-done | bytes 2097168 | tf_op jit(solution)/shard_map/all_gather | solution.py:37
  91.1 2.8 while.56
  91.3 1.7 fusion.108
  93.9 74.9 %all-gather.10.cloned.1.call-done = bf16[8192,1,128]{2,0,1:T(8,128)(2,1)} async-done(((bf16[128,1,128]{2,0,1:T(8,128)(2,1)}), bf16[8192,1,128]{2,0,1:T(8,128)(2,1)}) %all-gather.10.cloned.1.call-update) | async-done | bytes 2097168 | tf_op jit(solution)/shard_map/all_gather | solution.py:38
  168.9 3.8 broadcast_in_dim.69
  172.6 9.8 %while.57 = (s32[]{:T(128)}, f32[128,1,8,128]{0,3,2,1:T(8,128)S(1)}, f32[8192,2,1,128]{3,0,2,1:T(8,128)}, s32[]{:T(128)}, bf16[8192,1,128]{2,0,1:T(8,128)(2,1)},...) while((s32[]{:T(128)}, ...), condition=%wide.region_6.7_spmd.clone, body=%wide.region_5.6_spmd.clone.sunk | while | flops 1354499200 | bytes 26367196 | solution.py:123
  172.6 1.7 fusion.119
  174.5 2.5 fusion.120
  177.0 1.5 fusion.121
  180.2 2.3 fusion.123
  182.8 86.9 %all-gather.12.cloned.1.call-done = f32[2048,64,16]{1,2,0:T(8,128)} async-done(((f32[32,64,16]{1,2,0:T(8,128)}), f32[2048,64,16]{1,2,0:T(8,128)}) %all-gather.12.cloned.1.call-update) | async-done | bytes 8388624 | tf_op jit(solution)/shard_map/all_gather | solution.py:11
  269.6 73.0 %while.58 = (s32[]{:T(128)}, f32[32,64,16]{1,2,0:T(8,128)S(1)}, s32[]{:T(128)}, f32[64,32]{1,0:T(8,128)S(1)}, f32[64,32,64,16]{2,3,1,0:T(8,128)}, /*index=5*/s32[]{:T(128)}, s32[]{:T(128)}, s32[]{:T(128)}, s32[]{:T(128)}) while((s32[]{:T(128)}, f32[32,64,16]{1,2,0:T(8,128)S(1)}, s32[]{:T(128)}, f32[64,32]{1,0:T(8,128)S(1)}, ...), condition=%wide.region_10.11_spmd.clone, body=%wide.region_9.10_spmd.clone.sunk | while | flops 131080 | bytes 393775 | solution.py:22
  281.0 1.1 fusion.124
  282.1 1.1 fusion.124
  283.3 1.1 fusion.124
  284.4 1.1 fusion.124
  285.6 1.1 fusion.124
  289.0 1.1 fusion.124
  290.1 1.1 fusion.124
  291.3 1.1 fusion.124
  292.4 1.1 fusion.124
  293.6 1.1 fusion.124
  294.7 1.1 fusion.124
  295.8 1.1 fusion.124
  297.0 1.1 fusion.124
  298.1 1.1 fusion.124
  299.3 1.1 fusion.124
  300.4 1.1 fusion.124
  302.7 1.1 fusion.124
  303.9 1.1 fusion.124
  305.0 1.1 fusion.124
  306.1 1.1 fusion.124
  307.3 1.1 fusion.124
  308.4 1.1 fusion.124
  309.6 1.1 fusion.124
  311.8 1.1 fusion.124
  313.0 1.1 fusion.124
  314.1 1.1 fusion.124
  315.3 1.1 fusion.124
  316.4 1.1 fusion.124
  317.5 1.1 fusion.124
  319.8 1.1 fusion.124
  321.0 1.1 fusion.124
  324.4 1.1 fusion.124
  325.5 1.1 fusion.124
  326.7 1.1 fusion.124
  327.8 1.1 fusion.124
  329.0 1.1 fusion.124
  330.1 1.1 fusion.124
  331.3 1.1 fusion.124
  332.4 1.1 fusion.124
  333.6 1.1 fusion.124
  334.7 1.1 fusion.124
  343.4 3.3 fusion.62
  347.1 1.7 multiply_reduce_fusion
  349.8 1.8 fusion.48
  351.6 1.8 fusion.52
  354.6 67.8 %reduce-scatter.2.cloned.1.call-done = f32[128,2,1,128]{3,0,2,1:T(8,128)} async-done(((f32[8192,2,1,128]{3,0,2,1:T(8,128)}), f32[128,2,1,128]{3,0,2,1:T(8,128)}) %reduce-scatter.2.cloned.1.call-update) | async-done | bytes 131088 | tf_op jit(solution)/shard_map/reduce_scatter | solution.py:124
  424.0 99.6 %all-gather.14.cloned.1.call-done = f32[2048,64,16]{1,2,0:T(8,128)} async-done(((f32[32,64,16]{1,2,0:T(8,128)}), f32[2048,64,16]{1,2,0:T(8,128)}) %all-gather.14.cloned.1.call-update) | async-done | bytes 8388624 | tf_op jit(solution)/shard_map/all_gather | solution.py:11
  523.5 71.8 %while.59 = (s32[]{:T(128)}, f32[32,64,16]{1,2,0:T(8,128)S(1)}, s32[]{:T(128)}, f32[64,32]{1,0:T(8,128)S(1)}, f32[64,32,64,16]{2,3,1,0:T(8,128)}, /*index=5*/s32[]{:T(128)}, s32[]{:T(128)}) while((s32[]{:T(128)}, f32[32,64,16]{1,2,0:T(8,128)S(1)}, s32[]{:T(128)}, f32[64,32]{1,0:T(8,128)S(1)}, f32[64,32,64,16]{2,3,1,0:T(8,128)}, ...), condition=%wide.region_14.15_spmd.clone, body=%wide.region_13.14_spmd.clone.sunk | while | flops 131076 | bytes 393713 | solution.py:22
  597.6 14.5 %all-reduce = (f32[128,16]{0,1:T(8,128)}, f32[128,16]{0,1:T(8,128)}) all-reduce(f32[128,16]{0,1:T(8,128)S(1)} %convolution_add_fusion.1, f32[128,16]{0,1:T(8,128)S(1)} %convolution_add_fusion), channel_id=1, replica_groups=mesh['ctx'=64,'tp'=4] {'tp'}, use_global_device_ids=true, to_apply=%region_12.13 | all-reduce | flops 4096 | bytes 32768 | tf_op jit(solution)/shard_map/psum | solution.py:196
  (289 shorter events, 108.7 us)
Async XLA Ops:
  7.2 8.1 %copy-start = (bf16[128,8,128]{2,1,0:T(8,128)(2,1)S(1)}, bf16[128,8,128]{2,1,0:T(8,128)(2,1)}, u32[]{:S(2)}) copy-start(bf16[128,8,128]{2,1,0:T(8,128)(2,1)} %param.22) | copy-start | bytes 786436
  7.2 8.1 %copy-start.2 = (bf16[128,8,128]{2,1,0:T(8,128)(2,1)S(1)}, bf16[128,8,128]{2,1,0:T(8,128)(2,1)}, u32[]{:S(2)}) copy-start(bf16[128,8,128]{2,1,0:T(8,128)(2,1)} %param.21) | copy-start | bytes 786436
  7.2 8.4 %copy-start.1 = (bf16[128,2048]{1,0:T(8,128)(2,1)S(1)}, bf16[128,2048]{1,0:T(8,128)(2,1)}, u32[]{:S(2)}) copy-start(bf16[128,2048]{1,0:T(8,128)(2,1)} %param.23) | copy-start | bytes 1572868
  7.2 51.6 %copy-start.3 = (bf16[128,8,128]{2,1,0:T(8,128)(2,1)S(1)}, bf16[128,8,128]{2,1,0:T(8,128)(2,1)}, u32[]{:S(2)}) copy-start(bf16[128,8,128]{2,1,0:T(8,128)(2,1)} %param.18) | copy-start | bytes 786436
  7.2 83.9 %all-gather.8.cloned.1.call-start = ((), (), s32[]{:S(2)}) async-start(), calls=%async_computation.1 | async-start | bytes 2129920 | tf_op jit(solution)/shard_map/all_gather | solution.py:37
  7.9 160.9 %all-gather.10.cloned.1.call-start = ((), (), s32[]{:S(2)}) async-start(), calls=%async_computation.2 | async-start | bytes 2129920 | tf_op jit(solution)/shard_map/all_gather | solution.py:38
  8.7 261.0 %all-gather.12.cloned.1.call-start = ((), (), s32[]{:S(2)}) async-start(), calls=%async_computation.4 | async-start | bytes 17039360 | tf_op jit(solution)/shard_map/all_gather | solution.py:11
  15.2 407.2 %reduce-scatter.2.cloned.1.call-start = ((), (), s32[]{:S(2)}) async-start(), calls=%async_computation.3 | async-start | bytes 8519680 | tf_op jit(solution)/shard_map/reduce_scatter | solution.py:124
  182.5 160.1 %copy-start.4 = (f32[128,16]{0,1:T(8,128)S(1)}, f32[128,16]{0,1:T(8,128)}, u32[]{:S(2)}) copy-start(f32[128,16]{0,1:T(8,128)} %param.25) | copy-start | bytes 24580
  182.5 341.0 %all-gather.14.cloned.1.call-start = ((), (), s32[]{:S(2)}) async-start(), calls=%async_computation.5 | async-start | bytes 17039360 | tf_op jit(solution)/shard_map/all_gather | solution.py:11
  269.6 77.2 %copy-start.5 = (f32[128,16]{0,1:T(8,128)S(1)}, f32[128,16]{0,1:T(8,128)}, u32[]{:S(2)}) copy-start(f32[128,16]{0,1:T(8,128)} %param.26) | copy-start | bytes 24580
Sparse Core Ops, SparseCore 0:
  10.8 80.2 all-gather.7
  93.9 74.9 all-gather.9
  172.2 97.4 all-gather.11
  273.7 148.6 reduce-scatter.1
  425.4 98.0 all-gather.13
where the time goes:
time: 626 us; the launch traced here: 619 us
  waiting for transfers between devices  363 us (58%)
  other arithmetic  144 us (23%)
  blocking collectives  57.4 us (9%)
  matrix products  23.2 us (4%)
  between operations  14.1 us (2%)
  local copies, waits for them, and re-layouts  11.3 us (2%)
    all_gather x2, waiting for transfers between devices, carried_in(): everything = jax.tree.map(lambda part: lax.all_gather(part, axis), x)  186 us
    select_n x128, other arithmetic, turn(): return jax.tree.map(lambda a, b: jnp.where(reached, a, b), new, before)  138 us
    all_gather x1, waiting for transfers between devices, attention_grads(): lax.all_gather(value_vectors, 'ctx', axis=0, tiled=True)  74.9 us
    reduce_scatter x1, waiting for transfers between devices, attention_grads(): key_rows = lax.psum_scatter(buffer, 'ctx', scatter_dimension=0, tiled=True)  67.8 us
    all_gather x1, blocking collectives, carried_in(): everything = jax.tree.map(lambda part: lax.all_gather(part, axis), x)  42.9 us
    all_gather x1, waiting for transfers between devices, attention_grads(): lax.all_gather(key_vectors, 'ctx', axis=0, tiled=True)  32.2 us
    psum x1, blocking collectives, mixer_grads(): lax.psum((in_map_part.reshape(local_rows, state_size), out_map_part.resha...  14.5 us
  transfers between devices with their start and end apart: 5, of which 5 were waited for; matrix products, arithmetic and copies ran while one was open for 17% of the time, Pallas kernels for 0%

commit v1 on v0

--- a/solution.py
+++ b/solution.py
@@ -6,20 +6,37 @@
 from jax.sharding import PartitionSpec as P
 
 
-def carried_in(x, axis, combine, identity, reverse):
+def carried_both(forward, backward, axis):
     length, here = (lax.axis_size(axis), lax.axis_index(axis))
-    everything = jax.tree.map(lambda part: lax.all_gather(part, axis), x)
-    start = jax.tree.map(
-        lambda part, zero: jnp.broadcast_to(jnp.asarray(zero, part.dtype), part.shape), x, identity
-    )
-
-    def turn(k, before):
-        at = length - 1 - k if reverse else k
-        reached = at > here if reverse else at < here
-        new = combine(before, jax.tree.map(lambda part: part[at], everything))
-        return jax.tree.map(lambda a, b: jnp.where(reached, a, b), new, before)
-
-    return lax.fori_loop(0, length, turn, start)
+    identity = lambda x: (jnp.ones_like(x[0]), jnp.zeros_like(x[1]))
+    fwd_total, fwd_excl = forward, identity(forward)
+    bwd_total, bwd_excl = backward, identity(backward)
+    shift = 1
+    while shift < length:
+        up = [(i, i + shift) for i in range(length - shift)]
+        down = [(i + shift, i) for i in range(length - shift)]
+        got_fwd = lax.ppermute(fwd_total, axis, up)
+        got_bwd = lax.ppermute(bwd_total, axis, down)
+        has_fwd = here >= shift
+        has_bwd = here + shift < length
+        pick = lambda ok, new, old: jax.tree.map(lambda a, b: jnp.where(ok, a, b), new, old)
+        fwd_excl = pick(has_fwd, blend_states(got_fwd, fwd_excl), fwd_excl)
+        bwd_excl = pick(has_bwd, blend_states(got_bwd, bwd_excl), bwd_excl)
+        if shift * 2 < length:
+            fwd_total = pick(has_fwd, blend_states(got_fwd, fwd_total), fwd_total)
+            bwd_total = pick(has_bwd, blend_states(got_bwd, bwd_total), bwd_total)
+        shift *= 2
+    return fwd_excl, bwd_excl
+
+
+def tp_sum(x, axis):
+    length = lax.axis_size(axis)
+    step = 1
+    while step < length:
+        pairs = [(i, i ^ step) for i in range(length)]
+        x = jax.tree.map(lambda a, b: a + b, x, lax.ppermute(x, axis, pairs))
+        step *= 2
+    return x
 
 
 def blend_states(earlier, later):
@@ -33,10 +50,10 @@
     local_groups = key_vectors.shape[1]
     repeats = local_heads // local_groups
     score_scale = 1.0 / math.sqrt(head_width)
-    whole_keys, whole_values = (
-        lax.all_gather(key_vectors, "ctx", axis=0, tiled=True),
-        lax.all_gather(value_vectors, "ctx", axis=0, tiled=True),
-    )
+    whole_kv = lax.all_gather(
+        jnp.concatenate([key_vectors, value_vectors], axis=1), "ctx", axis=0, tiled=True
+    )
+    whole_keys, whole_values = (whole_kv[:, :local_groups], whole_kv[:, local_groups:])
     all_tokens = whole_keys.shape[0]
     key_block = math.gcd(all_tokens, 1024)
     here = lax.axis_index("ctx")
@@ -153,15 +170,8 @@
     )
     bwd_decay = bwd_decay[::-1]
     bwd_state = bwd_state[::-1]
-    identity = (
-        jnp.ones((local_heads,), jnp.float32),
-        jnp.zeros((local_heads, head_width, state_size), jnp.float32),
-    )
-    unused_a, state_in = carried_in(
-        (fwd_decay[-1], fwd_state[-1]), "ctx", blend_states, identity, False
-    )
-    unused_b, pull_out = carried_in(
-        (bwd_decay[0], bwd_state[0]), "ctx", blend_states, identity, True
+    (unused_a, state_in), (unused_b, pull_out) = carried_both(
+        (fwd_decay[-1], fwd_state[-1]), (bwd_decay[0], bwd_state[0]), "ctx"
     )
     ones_row = jnp.ones((1, local_heads), jnp.float32)
     zero_row = jnp.zeros((1, local_heads, head_width, state_size), jnp.float32)
@@ -193,7 +203,7 @@
     out_map_part = out_map_part + jnp.einsum(
         "cth,cthp,chpn->ctn", from_start, grads_f, start_states, precision=highest
     )
-    grad_in_map, grad_out_map = lax.psum(
+    grad_in_map, grad_out_map = tp_sum(
         (in_map_part.reshape(local_rows, state_size), out_map_part.reshape(local_rows, state_size)),
         "tp",
     )

time: 626 us -> 371 us (0.59); the launches traced: 619 us -> 370 us
  waiting for transfers between devices: 363 us -> 211 us
  other arithmetic: 144 us -> 16.4 us
  starting transfers between devices: 0.38 us -> 95 us
  blocking collectives: 57.4 us -> 0 us
    all_gather x4 -> x1, waiting for transfers between devices: 294 us -> 82.3 us  [attention_grads(): lax.all_gather(jnp.concatenate([key_vectors, value_vectors], axis=1), 'ct...]
    select_n x128 -> x20, other arithmetic: 138 us -> 2.63 us  [carried_both(): jnp.where(ok, a, b)]
    ppermute x0 -> x26, waiting for transfers between devices: none -> 128 us  [the longest x11 114 us: carried_both(): got_bwd = lax.ppermute(bwd_total, axis, down)]
    ppermute x0 -> x26, starting transfers between devices: none -> 94.9 us  [the longest x11 76.2 us: carried_both(): got_fwd = lax.ppermute(fwd_total, axis, up)]
    reduce_scatter x1, waiting for transfers between devices: 67.8 us -> 0.01 us  [attention_grads(): key_rows = lax.psum_scatter(buffer, 'ctx', scatter_dimension=0, tiled=True)]
    all_gather x1 -> x0, blocking collectives: 42.9 us -> none  [carried_in(): everything = jax.tree.map(lambda part: lax.all_gather(part, axis), x)]
    psum x1 -> x0, blocking collectives: 14.5 us -> none  [mixer_grads(): lax.psum((in_map_part.reshape(local_rows, state_size), out_map_part.resha...]
  transfers between devices with their start and end apart: 5 -> 28, of which waited for: 5 -> 11; matrix products, arithmetic and copies ran while one was open for 17% -> 8% of each run, Pallas kernels for 0% -> 0%
where the time goes in v1:
time: 371 us; the launch traced here: 370 us
  waiting for transfers between devices  211 us (57%)
  starting transfers between devices  95 us (26%)
  matrix products  19.4 us (5%)
  other arithmetic  16.4 us (4%)
  between operations  14.7 us (4%)
  local copies, waits for them, and re-layouts  13.8 us (4%)
    ppermute x11, waiting for transfers between devices, carried_both(): got_bwd = lax.ppermute(bwd_total, axis, down)  114 us
    all_gather x1, waiting for transfers between devices, attention_grads(): lax.all_gather(jnp.concatenate([key_vectors, value_vectors], axis=1), 'ct...  82.3 us
    ppermute x11, starting transfers between devices, carried_both(): got_fwd = lax.ppermute(fwd_total, axis, up)  76.2 us
    ppermute x11, starting transfers between devices, carried_both(): got_bwd = lax.ppermute(bwd_total, axis, down)  14.4 us
    ppermute x11, waiting for transfers between devices, carried_both(): got_fwd = lax.ppermute(fwd_total, axis, up)  10.3 us
  transfers between devices with their start and end apart: 28, of which 11 were waited for; matrix products, arithmetic and copies ran while one was open for 8% of the time, Pallas kernels for 0%

profile of v1, /device:TPU:2, one launch (start us, length us, event | category | flops | bytes accessed | tf_op | source)
XLA Modules:
  0.0 370.0 jit_solution(943247194972280419)
XLA Ops:
  7.2 1.4 pad_maximum_fusion
  8.7 1.2 multiply_reduce_fusion.2
  10.0 1.1 copy_bitcast_fusion
  11.2 82.3 %all-gather.2.cloned.1.call-done = bf16[8192,2,128]{2,0,1:T(8,128)(2,1)} async-done(((bf16[128,2,128]{2,0,1:T(8,128)(2,1)}), bf16[8192,2,128]{2,0,1:T(8,128)(2,1)}) %all-gather.2.cloned.1.call-update) | async-done | bytes 4194320 | tf_op jit(solution)/shard_map/all_gather | solution.py:53
  93.5 3.9 %fusion.66 = (bf16[8192,1,128]{2,0,1:T(8,128)(2,1)}, bf16[8192,1,128]{2,0,1:T(8,128)(2,1)S(1)}) fusion(bf16[8192,2,128]{2,0,1:T(8,128)(2,1)} %all-gather.2.cloned.1.call-done), kind=kLoop, calls=%fused_computation.140 | loop fusion | bytes 8388608 | tf_op jit(solution)/shard_map/slice | solution.py:56
  97.4 1.9 while.26
  97.6 0.7 fusion.102
  98.3 0.9 exponential_reduce_fusion.2
  99.3 3.8 %broadcast_in_dim.45 = f32[8192,2,1,128]{3,0,2,1:T(8,128)} broadcast(f32[]{:T(128)} %constant.38.clone.1), dimensions={} | broadcast | bytes 8388612 | tf_op jit(solution)/shard_map/broadcast_in_dim | solution.py:126
  103.1 8.0 %while.27 = (s32[]{:T(128)}, f32[128,1,8,128]{0,3,2,1:T(8,128)S(1)}, f32[8192,2,1,128]{3,0,2,1:T(8,128)}, s32[]{:T(128)}, bf16[8192,1,128]{2,0,1:T(8,128)(2,1)S(...) while((s32[]{:T(128)}, ...), condition=%wide.region_6.7_spmd.clone, body=%wide.region_5.6_spmd.clone.sunk | while | flops 1354499200 | bytes 26367196 | solution.py:140
  103.1 0.7 fusion.113
  104.0 2.5 fusion.114
  107.0 1.0 fusion.116
  108.0 0.7 convolution_bitcast_fusion.4
  108.7 2.3 fusion.117
  112.0 2.2 collective-permute-start.13
  114.2 1.3 collective-permute-start
  116.0 2.5 fusion.59
  118.5 1.5 collective-permute-start.5
  120.7 2.3 multiply_reduce_fusion
  123.0 1.6 fusion.42
  124.7 1.3 collective-permute-start.6
  126.1 1.3 collective-permute-start.1
  127.4 6.5 %collective-permute-start.14 = (f32[32]{0:T(128)S(1)}, f32[32]{0:T(128)S(1)}, u32[]{:S(2)}, u32[]{:S(2)}) collective-permute-start(f32[32]{0:T(128)S(1)} %get-tuple-element.260), channel_id=1, source_target_pairs={{0,8},{4,12},{8,16},{12,20},{16,24},{20,28},{24,32},{28,36},{32,40... | collective-permute-start | bytes 392 | tf_op jit(solution)/shard_map/ppermute | solution.py:18
  133.9 3.0 collective-permute-done.6
  137.0 1.3 collective-permute-start.7
  138.4 1.3 collective-permute-start.2
  139.7 9.6 %collective-permute-done.7 = f32[32,64,16]{1,2,0:T(8,128)S(1)} collective-permute-done((f32[32,64,16]{1,2,0:T(8,128)S(1)}, f32[32,64,16]{1,2,0:T(8,128)S(1)}, u32[]{:S(2)}, u32[]{:S(2)}) %collective-permute-start.7) | collective-permute-done | bytes 131104 | tf_op jit(solution)/shard_map/ppermute | solution.py:19
  149.4 1.3 collective-permute-start.8
  150.7 1.3 collective-permute-start.3
  152.0 15.5 %collective-permute-done.8 = f32[32,64,16]{1,2,0:T(8,128)S(1)} collective-permute-done((f32[32,64,16]{1,2,0:T(8,128)S(1)}, f32[32,64,16]{1,2,0:T(8,128)S(1)}, u32[]{:S(2)}, u32[]{:S(2)}) %collective-permute-start.8) | collective-permute-done | bytes 131104 | tf_op jit(solution)/shard_map/ppermute | solution.py:19
  167.6 1.3 collective-permute-start.9
  169.0 1.3 collective-permute-start.4
  170.3 24.8 %collective-permute-done.9 = f32[32,64,16]{1,2,0:T(8,128)S(1)} collective-permute-done((f32[32,64,16]{1,2,0:T(8,128)S(1)}, f32[32,64,16]{1,2,0:T(8,128)S(1)}, u32[]{:S(2)}, u32[]{:S(2)}) %collective-permute-start.9) | collective-permute-done | bytes 131104 | tf_op jit(solution)/shard_map/ppermute | solution.py:19
  195.2 1.3 collective-permute-start.10
  196.5 61.1 %collective-permute-done.10 = f32[32,64,16]{1,2,0:T(8,128)S(1)} collective-permute-done((f32[32,64,16]{1,2,0:T(8,128)S(1)}, f32[32,64,16]{1,2,0:T(8,128)S(1)}, u32[]{:S(2)}, u32[]{:S(2)}) %collective-permute-start.10) | collective-permute-done | bytes 131104 | tf_op jit(solution)/shard_map/ppermute | solution.py:19
  258.5 0.7 multiply_reduce_fusion.8
  259.2 2.5 fusion.56
  261.8 1.3 collective-permute-start.18
  263.1 1.3 collective-permute-start.15
  264.5 10.0 %collective-permute-start.19 = (f32[32,64,16]{1,2,0:T(8,128)S(1)}, f32[32,64,16]{1,2,0:T(8,128)S(1)}, u32[]{:S(2)}, u32[]{:S(2)}) collective-permute-start(f32[32,64,16]{1,2,0:T(8,128)S(1)} %add_select_fusion.9), channel_id=1, source_target_pairs={{0,8},{4,12},{8,16},{12,20},{16,24},{20,28},{24,32},{28,36},{32,40... | collective-permute-start | bytes 393224 | tf_op jit(solution)/shard_map/ppermute | solution.py:18
  274.6 3.0 collective-permute-start.16
  277.6 4.9 %collective-permute-done.19 = f32[32,64,16]{1,2,0:T(8,128)S(1)} collective-permute-done((f32[32,64,16]{1,2,0:T(8,128)S(1)}, f32[32,64,16]{1,2,0:T(8,128)S(1)}, u32[]{:S(2)}, u32[]{:S(2)}) %collective-permute-start.19) | collective-permute-done | bytes 131104 | tf_op jit(solution)/shard_map/ppermute | solution.py:18
  282.6 4.8 %collective-permute-start.20 = (f32[32,64,16]{1,2,0:T(8,128)S(1)}, f32[32,64,16]{1,2,0:T(8,128)S(1)}, u32[]{:S(2)}, u32[]{:S(2)}) collective-permute-start(f32[32,64,16]{1,2,0:T(8,128)S(1)} %add_select_fusion.8), channel_id=1, source_target_pairs={{0,16},{4,20},{8,24},{12,28},{16,32},{20,36},{24,40},{28,44},{32,4... | collective-permute-start | bytes 393224 | tf_op jit(solution)/shard_map/ppermute | solution.py:18
  287.4 11.3 %collective-permute-start.17 = (f32[32]{0:T(128)S(1)}, f32[32]{0:T(128)S(1)}, u32[]{:S(2)}, u32[]{:S(2)}) collective-permute-start(f32[32]{0:T(128)S(1)} %broadcast_select_fusion.7), channel_id=1, source_target_pairs={{0,64},{4,68},{8,72},{12,76},{16,80},{20,84},{24,88},{28,92},{32,9... | collective-permute-start | bytes 392 | tf_op jit(solution)/shard_map/ppermute | solution.py:18
  298.9 4.4 %collective-permute-start.21 = (f32[32,64,16]{1,2,0:T(8,128)S(1)}, f32[32,64,16]{1,2,0:T(8,128)S(1)}, u32[]{:S(2)}, u32[]{:S(2)}) collective-permute-start(f32[32,64,16]{1,2,0:T(8,128)S(1)} %add_select_fusion.7), channel_id=1, source_target_pairs={{0,32},{4,36},{8,40},{12,44},{16,48},{20,52},{24,56},{28,60},{32,6... | collective-permute-start | bytes 393224 | tf_op jit(solution)/shard_map/ppermute | solution.py:18
  303.9 3.2 collective-permute-done.21
  307.2 15.9 %collective-permute-start.22 = (f32[32,64,16]{1,2,0:T(8,128)S(1)}, f32[32,64,16]{1,2,0:T(8,128)S(1)}, u32[]{:S(2)}, u32[]{:S(2)}) collective-permute-start(f32[32,64,16]{1,2,0:T(8,128)S(1)} %add_select_fusion.6), channel_id=1, source_target_pairs={{0,64},{4,68},{8,72},{12,76},{16,80},{20,84},{24,88},{28,92},{32,9... | collective-permute-start | bytes 393224 | tf_op jit(solution)/shard_map/ppermute | solution.py:18
  324.3 1.2 collective-permute-start.12
  325.6 2.1 collective-permute-done.22
  327.7 0.8 add_select_fusion.5
  328.5 15.6 %collective-permute-start.23 = (f32[32,64,16]{1,2,0:T(8,128)}, f32[32,64,16]{1,2,0:T(8,128)S(1)}, u32[]{:S(2)}, u32[]{:S(2)}) collective-permute-start(f32[32,64,16]{1,2,0:T(8,128)} %add_select_fusion.5), channel_id=1, source_target_pairs={{0,128},{4,132},{8,136},{12,140},{16,144},{20,148},{24,152},{28,15... | collective-permute-start | bytes 393224 | tf_op jit(solution)/shard_map/ppermute | solution.py:18
  344.2 1.8 fusion.48
  346.0 1.0 copy.86
  347.0 1.3 add.206
  348.3 1.3 multiply_reduce_fusion.7
  350.2 1.0 convolution_add_fusion
  351.8 0.8 fusion.54
  353.6 1.3 collective-permute-done.24
  354.9 2.0 collective-permute-start.25
  356.9 0.7 copy.87
  357.6 2.5 collective-permute-done.25
  360.7 0.9 copy.76
  361.6 0.9 convert.4
  (101 shorter events, 10.4 us)
Async XLA Ops:
  7.2 86.3 %all-gather.2.cloned.1.call-start = ((), (), s32[]{:S(2)}) async-start(), calls=%async_computation.1 | async-start | bytes 4259840 | tf_op jit(solution)/shard_map/all_gather | solution.py:53
  8.6 352.9 %reduce-scatter.2.cloned.1.call-start = ((), (), s32[]{:S(2)}) async-start(), calls=%async_computation.2 | async-start | bytes 8519680 | tf_op jit(solution)/shard_map/reduce_scatter | solution.py:141
  111.0 0.7 copy-start.5
  111.0 4.5 %copy-start = (bf16[128,2048]{1,0:T(8,128)(2,1)S(1)}, bf16[128,2048]{1,0:T(8,128)(2,1)}, u32[]{:S(2)}) copy-start(bf16[128,2048]{1,0:T(8,128)(2,1)} %param.20) | copy-start | bytes 1572868
  111.0 4.9 %copy-start.4 = (f32[128,16]{0,1:T(8,128)S(1)}, f32[128,16]{0,1:T(8,128)}, u32[]{:S(2)}) copy-start(f32[128,16]{0,1:T(8,128)} %param.22) | copy-start | bytes 24580
  111.1 9.0 %copy-start.1 = (bf16[128,2048]{1,0:T(8,128)(2,1)S(1)}, bf16[128,2048]{1,0:T(8,128)(2,1)}, u32[]{:S(2)}) copy-start(bf16[128,2048]{1,0:T(8,128)(2,1)} %param.19) | copy-start | bytes 1572868
  111.1 9.3 %copy-start.3 = (f32[128,16]{0,1:T(8,128)S(1)}, f32[128,16]{0,1:T(8,128)}, u32[]{:S(2)}) copy-start(f32[128,16]{0,1:T(8,128)} %param.21) | copy-start | bytes 24580
  112.0 14.0 %collective-permute-start.13 = (f32[32]{0:T(128)S(1)}, f32[32]{0:T(128)S(1)}, u32[]{:S(2)}, u32[]{:S(2)}) collective-permute-start(f32[32]{0:T(128)S(1)} %fusion.64), channel_id=1, source_target_pairs={{0,4},{4,8},{8,12},{12,16},{16,20},{20,24},{24,28},{28,32},{32,36}... | collective-permute-start | bytes 392 | tf_op jit(solution)/shard_map/ppermute | solution.py:18
  114.2 11.9 %collective-permute-start = (f32[32]{0:T(128)S(1)}, f32[32]{0:T(128)S(1)}, u32[]{:S(2)}, u32[]{:S(2)}) collective-permute-start(f32[32]{0:T(128)S(1)} %fusion.64), channel_id=1, source_target_pairs={{4,0},{8,4},{12,8},{16,12},{20,16},{24,20},{28,24},{32,28},{36,32}... | collective-permute-start | bytes 392 | tf_op jit(solution)/shard_map/ppermute | solution.py:19
  118.5 6.1 %collective-permute-start.5 = (f32[32,64,16]{1,2,0:T(8,128)S(1)}, f32[32,64,16]{1,2,0:T(8,128)S(1)}, u32[]{:S(2)}, u32[]{:S(2)}) collective-permute-start(f32[32,64,16]{1,2,0:T(8,128)S(1)} %fusion.59), channel_id=1, source_target_pairs={{4,0},{8,4},{12,8},{16,12},{20,16},{24,20},{28,24},{32,28},{36,32}... | collective-permute-start | bytes 393224 | tf_op jit(solution)/shard_map/ppermute | solution.py:19
  123.0 184.1 %copy-start.2 = (f32[128,128]{1,0:T(8,128)}, f32[128,128]{1,0:T(8,128)S(1)}, u32[]{:S(2)}) copy-start(f32[128,128]{1,0:T(8,128)S(1)} %get-tuple-element.205) | copy-start | bytes 196612
  124.7 12.2 %collective-permute-start.6 = (f32[32,64,16]{1,2,0:T(8,128)S(1)}, f32[32,64,16]{1,2,0:T(8,128)S(1)}, u32[]{:S(2)}, u32[]{:S(2)}) collective-permute-start(f32[32,64,16]{1,2,0:T(8,128)S(1)} %add_select_fusion.19), channel_id=1, source_target_pairs={{8,0},{12,4},{16,8},{20,12},{24,16},{28,20},{32,24},{36,28},{40,32... | collective-permute-start | bytes 393224 | tf_op jit(solution)/shard_map/ppermute | solution.py:19
  126.0 12.3 %copy-start.6 = (f32[32]{0:T(128)}, f32[32]{0:T(128)S(1)}, u32[]{:S(2)}) copy-start(f32[32]{0:T(128)S(1)} %collective-permute-done.13) | copy-start | bytes 388
  126.1 12.3 %collective-permute-start.1 = (f32[32]{0:T(128)S(1)}, f32[32]{0:T(128)S(1)}, u32[]{:S(2)}, u32[]{:S(2)}) collective-permute-start(f32[32]{0:T(128)S(1)} %get-tuple-element.261), channel_id=1, source_target_pairs={{8,0},{12,4},{16,8},{20,12},{24,16},{28,20},{32,24},{36,28},{40,32... | collective-permute-start | bytes 392 | tf_op jit(solution)/shard_map/ppermute | solution.py:19
  127.4 135.7 %collective-permute-start.14 = (f32[32]{0:T(128)S(1)}, f32[32]{0:T(128)S(1)}, u32[]{:S(2)}, u32[]{:S(2)}) collective-permute-start(f32[32]{0:T(128)S(1)} %get-tuple-element.260), channel_id=1, source_target_pairs={{0,8},{4,12},{8,16},{12,20},{16,24},{20,28},{24,32},{28,36},{32,40... | collective-permute-start | bytes 392 | tf_op jit(solution)/shard_map/ppermute | solution.py:18
  137.0 12.3 %collective-permute-start.7 = (f32[32,64,16]{1,2,0:T(8,128)S(1)}, f32[32,64,16]{1,2,0:T(8,128)S(1)}, u32[]{:S(2)}, u32[]{:S(2)}) collective-permute-start(f32[32,64,16]{1,2,0:T(8,128)S(1)} %add_select_fusion.18), channel_id=1, source_target_pairs={{16,0},{20,4},{24,8},{28,12},{32,16},{36,20},{40,24},{44,28},{48,3... | collective-permute-start | bytes 393224 | tf_op jit(solution)/shard_map/ppermute | solution.py:19
  138.4 12.3 %collective-permute-start.2 = (f32[32]{0:T(128)S(1)}, f32[32]{0:T(128)S(1)}, u32[]{:S(2)}, u32[]{:S(2)}) collective-permute-start(f32[32]{0:T(128)S(1)} %broadcast_select_fusion.12), channel_id=1, source_target_pairs={{16,0},{20,4},{24,8},{28,12},{32,16},{36,20},{40,24},{44,28},{48,3... | collective-permute-start | bytes 392 | tf_op jit(solution)/shard_map/ppermute | solution.py:19
  149.4 18.1 %collective-permute-start.8 = (f32[32,64,16]{1,2,0:T(8,128)S(1)}, f32[32,64,16]{1,2,0:T(8,128)S(1)}, u32[]{:S(2)}, u32[]{:S(2)}) collective-permute-start(f32[32,64,16]{1,2,0:T(8,128)S(1)} %add_select_fusion.17), channel_id=1, source_target_pairs={{32,0},{36,4},{40,8},{44,12},{48,16},{52,20},{56,24},{60,28},{64,3... | collective-permute-start | bytes 393224 | tf_op jit(solution)/shard_map/ppermute | solution.py:19
  150.7 18.2 %collective-permute-start.3 = (f32[32]{0:T(128)S(1)}, f32[32]{0:T(128)S(1)}, u32[]{:S(2)}, u32[]{:S(2)}) collective-permute-start(f32[32]{0:T(128)S(1)} %broadcast_select_fusion.14), channel_id=1, source_target_pairs={{32,0},{36,4},{40,8},{44,12},{48,16},{52,20},{56,24},{60,28},{64,3... | collective-permute-start | bytes 392 | tf_op jit(solution)/shard_map/ppermute | solution.py:19
  167.6 27.5 %collective-permute-start.9 = (f32[32,64,16]{1,2,0:T(8,128)S(1)}, f32[32,64,16]{1,2,0:T(8,128)S(1)}, u32[]{:S(2)}, u32[]{:S(2)}) collective-permute-start(f32[32,64,16]{1,2,0:T(8,128)S(1)} %add_select_fusion.16), channel_id=1, source_target_pairs={{64,0},{68,4},{72,8},{76,12},{80,16},{84,20},{88,24},{92,28},{96,3... | collective-permute-start | bytes 393224 | tf_op jit(solution)/shard_map/ppermute | solution.py:19
  169.0 27.6 %collective-permute-start.4 = (f32[32]{0:T(128)S(1)}, f32[32]{0:T(128)S(1)}, u32[]{:S(2)}, u32[]{:S(2)}) collective-permute-start(f32[32]{0:T(128)S(1)} %broadcast_select_fusion.16), channel_id=1, source_target_pairs={{64,0},{68,4},{72,8},{76,12},{80,16},{84,20},{88,24},{92,28},{96,3... | collective-permute-start | bytes 392 | tf_op jit(solution)/shard_map/ppermute | solution.py:19
  195.2 62.5 %collective-permute-start.10 = (f32[32,64,16]{1,2,0:T(8,128)S(1)}, f32[32,64,16]{1,2,0:T(8,128)S(1)}, u32[]{:S(2)}, u32[]{:S(2)}) collective-permute-start(f32[32,64,16]{1,2,0:T(8,128)S(1)} %add_select_fusion.15), channel_id=1, source_target_pairs={{128,0},{132,4},{136,8},{140,12},{144,16},{148,20},{152,24},{156,2... | collective-permute-start | bytes 393224 | tf_op jit(solution)/shard_map/ppermute | solution.py:19
  257.9 65.2 %copy-start.7 = (f32[32]{0:T(128)S(1)}, f32[32]{0:T(128)}, u32[]{:S(2)}) copy-start(f32[32]{0:T(128)} %copy-done.6) | copy-start | bytes 388
  261.8 2.6 collective-permute-start.18
  263.1 11.5 %collective-permute-start.15 = (f32[32]{0:T(128)S(1)}, f32[32]{0:T(128)S(1)}, u32[]{:S(2)}, u32[]{:S(2)}) collective-permute-start(f32[32]{0:T(128)S(1)} %broadcast_select_fusion.3), channel_id=1, source_target_pairs={{0,16},{4,20},{8,24},{12,28},{16,32},{20,36},{24,40},{28,44},{32,4... | collective-permute-start | bytes 392 | tf_op jit(solution)/shard_map/ppermute | solution.py:18
  264.5 18.0 %collective-permute-start.19 = (f32[32,64,16]{1,2,0:T(8,128)S(1)}, f32[32,64,16]{1,2,0:T(8,128)S(1)}, u32[]{:S(2)}, u32[]{:S(2)}) collective-permute-start(f32[32,64,16]{1,2,0:T(8,128)S(1)} %add_select_fusion.9), channel_id=1, source_target_pairs={{0,8},{4,12},{8,16},{12,20},{16,24},{20,28},{24,32},{28,36},{32,40... | collective-permute-start | bytes 393224 | tf_op jit(solution)/shard_map/ppermute | solution.py:18
  274.6 12.8 %collective-permute-start.16 = (f32[32]{0:T(128)S(1)}, f32[32]{0:T(128)S(1)}, u32[]{:S(2)}, u32[]{:S(2)}) collective-permute-start(f32[32]{0:T(128)S(1)} %broadcast_select_fusion.5), channel_id=1, source_target_pairs={{0,32},{4,36},{8,40},{12,44},{16,48},{20,52},{24,56},{28,60},{32,6... | collective-permute-start | bytes 392 | tf_op jit(solution)/shard_map/ppermute | solution.py:18
  282.6 16.1 %collective-permute-start.20 = (f32[32,64,16]{1,2,0:T(8,128)S(1)}, f32[32,64,16]{1,2,0:T(8,128)S(1)}, u32[]{:S(2)}, u32[]{:S(2)}) collective-permute-start(f32[32,64,16]{1,2,0:T(8,128)S(1)} %add_select_fusion.8), channel_id=1, source_target_pairs={{0,16},{4,20},{8,24},{12,28},{16,32},{20,36},{24,40},{28,44},{32,4... | collective-permute-start | bytes 393224 | tf_op jit(solution)/shard_map/ppermute | solution.py:18
  287.4 35.7 %collective-permute-start.17 = (f32[32]{0:T(128)S(1)}, f32[32]{0:T(128)S(1)}, u32[]{:S(2)}, u32[]{:S(2)}) collective-permute-start(f32[32]{0:T(128)S(1)} %broadcast_select_fusion.7), channel_id=1, source_target_pairs={{0,64},{4,68},{8,72},{12,76},{16,80},{20,84},{24,88},{28,92},{32,9... | collective-permute-start | bytes 392 | tf_op jit(solution)/shard_map/ppermute | solution.py:18
  298.9 8.2 %collective-permute-start.21 = (f32[32,64,16]{1,2,0:T(8,128)S(1)}, f32[32,64,16]{1,2,0:T(8,128)S(1)}, u32[]{:S(2)}, u32[]{:S(2)}) collective-permute-start(f32[32,64,16]{1,2,0:T(8,128)S(1)} %add_select_fusion.7), channel_id=1, source_target_pairs={{0,32},{4,36},{8,40},{12,44},{16,48},{20,52},{24,56},{28,60},{32,6... | collective-permute-start | bytes 393224 | tf_op jit(solution)/shard_map/ppermute | solution.py:18
  303.4 20.3 %collective-permute-start.11 = (f32[128,16]{0,1:T(8,128)S(1)}, f32[128,16]{0,1:T(8,128)S(1)}, u32[]{:S(2)}, u32[]{:S(2)}) collective-permute-start(f32[128,16]{0,1:T(8,128)S(1)} %convolution_add_fusion.1), channel_id=1, source_target_pairs={{0,1},{1,0},{2,3},{3,2},{4,5},{5,4},{6,7},{7,6},{8,9},{9,8},{10,11... | collective-permute-start | bytes 24584 | tf_op jit(solution)/shard_map/ppermute | solution.py:37
  307.2 20.5 %collective-permute-start.22 = (f32[32,64,16]{1,2,0:T(8,128)S(1)}, f32[32,64,16]{1,2,0:T(8,128)S(1)}, u32[]{:S(2)}, u32[]{:S(2)}) collective-permute-start(f32[32,64,16]{1,2,0:T(8,128)S(1)} %add_select_fusion.6), channel_id=1, source_target_pairs={{0,64},{4,68},{8,72},{12,76},{16,80},{20,84},{24,88},{28,92},{32,9... | collective-permute-start | bytes 393224 | tf_op jit(solution)/shard_map/ppermute | solution.py:18
  324.3 22.7 %collective-permute-start.12 = (f32[128,16]{0,1:T(8,128)}, f32[128,16]{0,1:T(8,128)}, u32[]{:S(2)}, u32[]{:S(2)}) collective-permute-start(f32[128,16]{0,1:T(8,128)} %add.205), channel_id=1, source_target_pairs={{0,2},{1,3},{2,0},{3,1},{4,6},{5,7},{6,4},{7,5},{8,10},{9,11},{10,... | collective-permute-start | bytes 24584 | tf_op jit(solution)/shard_map/ppermute | solution.py:37
  328.5 19.8 %collective-permute-start.23 = (f32[32,64,16]{1,2,0:T(8,128)}, f32[32,64,16]{1,2,0:T(8,128)S(1)}, u32[]{:S(2)}, u32[]{:S(2)}) collective-permute-start(f32[32,64,16]{1,2,0:T(8,128)} %add_select_fusion.5), channel_id=1, source_target_pairs={{0,128},{4,132},{8,136},{12,140},{16,144},{20,148},{24,152},{28,15... | collective-permute-start | bytes 393224 | tf_op jit(solution)/shard_map/ppermute | solution.py:18
  351.2 3.7 %collective-permute-start.24 = (f32[128,16]{0,1:T(8,128)S(1)}, f32[128,16]{0,1:T(8,128)S(1)}, u32[]{:S(2)}, u32[]{:S(2)}) collective-permute-start(f32[128,16]{0,1:T(8,128)S(1)} %convolution_add_fusion), channel_id=1, source_target_pairs={{0,1},{1,0},{2,3},{3,2},{4,5},{5,4},{6,7},{7,6},{8,9},{9,8},{10,11... | collective-permute-start | bytes 24584 | tf_op jit(solution)/shard_map/ppermute | solution.py:37
  354.9 5.2 %collective-permute-start.25 = (f32[128,16]{0,1:T(8,128)S(1)}, f32[128,16]{0,1:T(8,128)S(1)}, u32[]{:S(2)}, u32[]{:S(2)}) collective-permute-start(f32[128,16]{0,1:T(8,128)S(1)} %add.218), channel_id=1, source_target_pairs={{0,2},{1,3},{2,0},{3,1},{4,6},{5,7},{6,4},{7,5},{8,10},{9,11},{10,... | collective-permute-start | bytes 24584 | tf_op jit(solution)/shard_map/ppermute | solution.py:37
Sparse Core Ops, SparseCore 0:
  11.4 82.0 all-gather.1
  111.2 221.5 reduce-scatter.1

commit v2 on v1

--- a/solution.py
+++ b/solution.py
@@ -4,6 +4,9 @@
 import jax.numpy as jnp
 from jax import lax
 from jax.sharding import PartitionSpec as P
+
+
+CTX = "ctx"
 
 
 def carried_both(forward, backward, axis):
@@ -45,18 +48,19 @@
     return (decay_early * decay_later, decay_later[..., None, None] * state_early + state_later)
 
 
-def attention_grads(queries, key_vectors, value_vectors, attention_out, grad_attention):
+def attention_grads(queries, key_vectors, value_vectors, attention_out, grad_attention, carried):
     local_rows, local_heads, head_width = queries.shape
     local_groups = key_vectors.shape[1]
     repeats = local_heads // local_groups
     score_scale = 1.0 / math.sqrt(head_width)
     whole_kv = lax.all_gather(
-        jnp.concatenate([key_vectors, value_vectors], axis=1), "ctx", axis=0, tiled=True
-    )
+        jnp.concatenate([key_vectors, value_vectors], axis=1), CTX, axis=0, tiled=True
+    )
+    whole_kv, carried = lax.optimization_barrier((whole_kv, carried))
     whole_keys, whole_values = (whole_kv[:, :local_groups], whole_kv[:, local_groups:])
     all_tokens = whole_keys.shape[0]
     key_block = math.gcd(all_tokens, 1024)
-    here = lax.axis_index("ctx")
+    here = lax.axis_index(CTX)
 
     def scores_of(entry, first_row, length):
         query_grp, query_pos = (entry[0], entry[3])
@@ -138,12 +142,14 @@
 
     query_start = jnp.zeros(entry[0].shape, jnp.float32)
     query_acc, buffer = lax.fori_loop(0, entry[5], joint_step, (query_start, buffer))
-    key_rows = lax.psum_scatter(buffer, "ctx", scatter_dimension=0, tiled=True)
+    buffer, query_acc, carried = lax.optimization_barrier((buffer, query_acc, carried))
+    key_rows = lax.psum_scatter(buffer, CTX, scatter_dimension=0, tiled=True)
     grad_queries = query_acc.reshape(local_rows, local_heads, head_width).astype(jnp.bfloat16)
-    return (grad_queries, key_rows[:, 0].astype(jnp.bfloat16), key_rows[:, 1].astype(jnp.bfloat16))
-
-
-def mixer_grads(mix_input, grad_mix, input_map, output_map, decay_log):
+    grads = (grad_queries, key_rows[:, 0].astype(jnp.bfloat16), key_rows[:, 1].astype(jnp.bfloat16))
+    return grads, carried
+
+
+def mixer_carry(mix_input, grad_mix, input_map, output_map, decay_log):
     local_rows, channels = mix_input.shape
     local_heads = decay_log.shape[1]
     head_width = channels // local_heads
@@ -171,8 +177,29 @@
     bwd_decay = bwd_decay[::-1]
     bwd_state = bwd_state[::-1]
     (unused_a, state_in), (unused_b, pull_out) = carried_both(
-        (fwd_decay[-1], fwd_state[-1]), (bwd_decay[0], bwd_state[0]), "ctx"
-    )
+        (fwd_decay[-1], fwd_state[-1]), (bwd_decay[0], bwd_state[0]), CTX
+    )
+    return (state_in, pull_out, fwd_decay, fwd_state, bwd_decay, bwd_state)
+
+
+def mixer_grads(mix_input, grad_mix, input_map, output_map, decay_log, carried):
+    state_in, pull_out, fwd_decay, fwd_state, bwd_decay, bwd_state = carried
+    local_rows, channels = mix_input.shape
+    local_heads = decay_log.shape[1]
+    head_width = channels // local_heads
+    state_size = input_map.shape[1]
+    span_len = math.gcd(local_rows, 128)
+    span_count = local_rows // span_len
+    highest = lax.Precision.HIGHEST
+    inputs_f = mix_input.astype(jnp.float32).reshape(span_count, span_len, local_heads, head_width)
+    grads_f = grad_mix.astype(jnp.float32).reshape(span_count, span_len, local_heads, head_width)
+    in_maps = input_map.reshape(span_count, span_len, state_size)
+    out_maps = output_map.reshape(span_count, span_len, state_size)
+    cum_log = jnp.cumsum(decay_log.reshape(span_count, span_len, local_heads), axis=1)
+    total_log = cum_log[:, -1]
+    to_end = jnp.exp(total_log[:, None, :] - cum_log)
+    from_start = jnp.exp(cum_log)
+    span_decay = jnp.exp(total_log)
     ones_row = jnp.ones((1, local_heads), jnp.float32)
     zero_row = jnp.zeros((1, local_heads, head_width, state_size), jnp.float32)
     prev_decay = jnp.concatenate([ones_row, fwd_decay[:-1]], axis=0)
@@ -238,35 +265,36 @@
     output_map,
     decay_log,
 ):
-    grad_queries, grad_keys, grad_values = attention_grads(
-        queries, key_vectors, value_vectors, attention_out, grad_attention
+    carried = mixer_carry(mix_input, grad_mix, input_map, output_map, decay_log)
+    (grad_queries, grad_keys, grad_values), carried = attention_grads(
+        queries, key_vectors, value_vectors, attention_out, grad_attention, carried
     )
     grad_input, grad_in_map, grad_out_map, grad_decay = mixer_grads(
-        mix_input, grad_mix, input_map, output_map, decay_log
+        mix_input, grad_mix, input_map, output_map, decay_log, carried
     )
     return (grad_queries, grad_keys, grad_values, grad_input, grad_in_map, grad_out_map, grad_decay)
 
 
 def solution(mesh):
     in_specs = (
-        P("ctx", "tp", None),
-        P("ctx", "tp", None),
-        P("ctx", "tp", None),
-        P("ctx", "tp", None),
-        P("ctx", "tp", None),
-        P("ctx", "tp"),
-        P("ctx", "tp"),
-        P("ctx", None),
-        P("ctx", None),
-        P("ctx", "tp"),
+        P(CTX, "tp", None),
+        P(CTX, "tp", None),
+        P(CTX, "tp", None),
+        P(CTX, "tp", None),
+        P(CTX, "tp", None),
+        P(CTX, "tp"),
+        P(CTX, "tp"),
+        P(CTX, None),
+        P(CTX, None),
+        P(CTX, "tp"),
     )
     out_specs = (
-        P("ctx", "tp", None),
-        P("ctx", "tp", None),
-        P("ctx", "tp", None),
-        P("ctx", "tp"),
-        P("ctx", None),
-        P("ctx", None),
-        P("ctx", "tp"),
+        P(CTX, "tp", None),
+        P(CTX, "tp", None),
+        P(CTX, "tp", None),
+        P(CTX, "tp"),
+        P(CTX, None),
+        P(CTX, None),
+        P(CTX, "tp"),
     )
     return jax.shard_map(local, mesh=mesh, in_specs=in_specs, out_specs=out_specs, check_vma=False)

time: 371 us -> 388 us (1.046)
  waiting for transfers between devices: 211 us -> 225 us
  starting transfers between devices: 95 us -> 100 us
  other arithmetic: 16.4 us -> 11.5 us
    reduce_scatter x1, waiting for transfers between devices: 0.01 us -> 194 us  [attention_grads(): key_rows = lax.psum_scatter(buffer, CTX, scatter_dimension=0, tiled=True)]
    ppermute x11, waiting for transfers between devices: 114 us -> 19.3 us  [carried_both(): got_bwd = lax.ppermute(bwd_total, axis, down)]
    all_gather x1, waiting for transfers between devices: 82.3 us -> 0.01 us  [attention_grads(): lax.all_gather(jnp.concatenate([key_vectors, value_vectors], axis=1), CTX...]
    ppermute x11, starting transfers between devices: 76.2 us -> 80.3 us  [carried_both(): got_fwd = lax.ppermute(fwd_total, axis, up)]
  transfers between devices with their start and end apart: 28 -> 28, of which waited for: 11 -> 9; matrix products, arithmetic and copies ran while one was open for 8% -> 6% of each run, Pallas kernels for 0% -> 0%
where the time goes in v2:
time: 388 us; the launch traced here: 386 us
  waiting for transfers between devices  225 us (58%)
  starting transfers between devices  100 us (26%)
  matrix products  18.2 us (5%)
  local copies, waits for them, and re-layouts  16.3 us (4%)
  between operations  14.8 us (4%)
  other arithmetic  11.5 us (3%)
    reduce_scatter x1, waiting for transfers between devices, attention_grads(): key_rows = lax.psum_scatter(buffer, CTX, scatter_dimension=0, tiled=True)  194 us
    ppermute x11, starting transfers between devices, carried_both(): got_fwd = lax.ppermute(fwd_total, axis, up)  80.3 us
    ppermute x11, waiting for transfers between devices, carried_both(): got_bwd = lax.ppermute(bwd_total, axis, down)  19.3 us
    ppermute x11, starting transfers between devices, carried_both(): got_bwd = lax.ppermute(bwd_total, axis, down)  14.2 us
    ppermute x11, waiting for transfers between devices, carried_both(): got_fwd = lax.ppermute(fwd_total, axis, up)  11.8 us
  transfers between devices with their start and end apart: 28, of which 9 were waited for; matrix products, arithmetic and copies ran while one was open for 6% of the time, Pallas kernels for 0%

profile of v2, /device:TPU:2, one launch (start us, length us, event | category | flops | bytes accessed | tf_op | source)
XLA Modules:
  0.0 386.4 jit_solution(1306682639084772976)
XLA Ops:
  7.2 1.4 pad_maximum_fusion
  8.7 0.9 copy.73
  9.8 1.3 collective-permute-start.11
  11.1 3.0 collective-permute-start
  14.2 1.4 copy.76
  15.5 1.3 copy.74
  17.1 2.5 fusion.63
  19.7 3.1 collective-permute-start.5
  22.8 2.5 fusion.60
  25.4 1.3 collective-permute-start.16
  26.9 0.8 copy_bitcast_fusion
  27.8 4.6 %collective-permute-start.1 = (f32[32]{0:T(128)S(1)}, f32[32]{0:T(128)S(1)}, u32[]{:S(2)}, u32[]{:S(2)}) collective-permute-start(f32[32]{0:T(128)S(1)} %get-tuple-element.273), channel_id=1, source_target_pairs={{0,8},{4,12},{8,16},{12,20},{16,24},{20,28},{24,32},{28,36},{32,40... | collective-permute-start | bytes 392 | tf_op jit(solution)/shard_map/ppermute | solution.py:21
  32.5 1.3 collective-permute-start.12
  33.8 6.9 %collective-permute-start.2 = (f32[32]{0:T(128)S(1)}, f32[32]{0:T(128)S(1)}, u32[]{:S(2)}, u32[]{:S(2)}) collective-permute-start(f32[32]{0:T(128)S(1)} %broadcast_select_fusion.12), channel_id=1, source_target_pairs={{0,16},{4,20},{8,24},{12,28},{16,32},{20,36},{24,40},{28,44},{32,4... | collective-permute-start | bytes 392 | tf_op jit(solution)/shard_map/ppermute | solution.py:21
  40.7 1.3 collective-permute-start.13
  42.0 10.7 %collective-permute-start.3 = (f32[32]{0:T(128)S(1)}, f32[32]{0:T(128)S(1)}, u32[]{:S(2)}, u32[]{:S(2)}) collective-permute-start(f32[32]{0:T(128)S(1)} %broadcast_select_fusion.14), channel_id=1, source_target_pairs={{0,32},{4,36},{8,40},{12,44},{16,48},{20,52},{24,56},{28,60},{32,6... | collective-permute-start | bytes 392 | tf_op jit(solution)/shard_map/ppermute | solution.py:21
  52.8 1.3 collective-permute-start.14
  54.1 5.9 %collective-permute-start.4 = (f32[32]{0:T(128)S(1)}, f32[32]{0:T(128)S(1)}, u32[]{:S(2)}, u32[]{:S(2)}) collective-permute-start(f32[32]{0:T(128)S(1)} %broadcast_select_fusion.16), channel_id=1, source_target_pairs={{0,64},{4,68},{8,72},{12,76},{16,80},{20,84},{24,88},{28,92},{32,9... | collective-permute-start | bytes 392 | tf_op jit(solution)/shard_map/ppermute | solution.py:21
  60.0 1.3 collective-permute-start.15
  61.5 2.0 collective-permute-start.6
  63.5 9.3 %collective-permute-done.15 = f32[32]{0:T(128)S(1)} collective-permute-done((f32[32]{0:T(128)S(1)}, f32[32]{0:T(128)S(1)}, u32[]{:S(2)}, u32[]{:S(2)}) %collective-permute-start.15) | collective-permute-done | bytes 160 | tf_op jit(solution)/shard_map/ppermute | solution.py:22
  72.8 1.3 collective-permute-start.17
  74.2 8.1 %collective-permute-start.7 = (f32[32,64,16]{1,2,0:T(8,128)S(1)}, f32[32,64,16]{1,2,0:T(8,128)S(1)}, u32[]{:S(2)}, u32[]{:S(2)}) collective-permute-start(f32[32,64,16]{1,2,0:T(8,128)S(1)} %add_select_fusion.18), channel_id=1, source_target_pairs={{0,16},{4,20},{8,24},{12,28},{16,32},{20,36},{24,40},{28,44},{32,4... | collective-permute-start | bytes 393224 | tf_op jit(solution)/shard_map/ppermute | solution.py:21
  82.3 2.5 collective-permute-done.17
  84.9 1.3 collective-permute-start.18
  86.2 2.1 collective-permute-done.7
  88.4 7.3 %collective-permute-start.8 = (f32[32,64,16]{1,2,0:T(8,128)S(1)}, f32[32,64,16]{1,2,0:T(8,128)S(1)}, u32[]{:S(2)}, u32[]{:S(2)}) collective-permute-start(f32[32,64,16]{1,2,0:T(8,128)S(1)} %add_select_fusion.17), channel_id=1, source_target_pairs={{0,32},{4,36},{8,40},{12,44},{16,48},{20,52},{24,56},{28,60},{32,6... | collective-permute-start | bytes 393224 | tf_op jit(solution)/shard_map/ppermute | solution.py:21
  95.8 1.3 collective-permute-start.19
  97.1 4.8 %collective-permute-done.8 = f32[32,64,16]{1,2,0:T(8,128)S(1)} collective-permute-done((f32[32,64,16]{1,2,0:T(8,128)S(1)}, f32[32,64,16]{1,2,0:T(8,128)S(1)}, u32[]{:S(2)}, u32[]{:S(2)}) %collective-permute-start.8) | collective-permute-done | bytes 131104 | tf_op jit(solution)/shard_map/ppermute | solution.py:21
  102.0 10.6 %collective-permute-start.9 = (f32[32,64,16]{1,2,0:T(8,128)S(1)}, f32[32,64,16]{1,2,0:T(8,128)S(1)}, u32[]{:S(2)}, u32[]{:S(2)}) collective-permute-start(f32[32,64,16]{1,2,0:T(8,128)S(1)} %add_select_fusion.16), channel_id=1, source_target_pairs={{0,64},{4,68},{8,72},{12,76},{16,80},{20,84},{24,88},{28,92},{32,9... | collective-permute-start | bytes 393224 | tf_op jit(solution)/shard_map/ppermute | solution.py:21
  112.8 1.3 collective-permute-start.20
  114.1 2.5 collective-permute-done.9
  116.6 18.0 %collective-permute-start.10 = (f32[32,64,16]{1,2,0:T(8,128)S(1)}, f32[32,64,16]{1,2,0:T(8,128)S(1)}, u32[]{:S(2)}, u32[]{:S(2)}) collective-permute-start(f32[32,64,16]{1,2,0:T(8,128)S(1)} %add_select_fusion.15), channel_id=1, source_target_pairs={{0,128},{4,132},{8,136},{12,140},{16,144},{20,148},{24,152},{28,15... | collective-permute-start | bytes 393224 | tf_op jit(solution)/shard_map/ppermute | solution.py:21
  134.8 1.3 collective-permute-start.21
  136.1 2.4 collective-permute-done.10
  138.6 1.0 add_select_fusion.10
  139.5 7.5 %collective-permute-done.21 = f32[32,64,16]{1,2,0:T(8,128)S(1)} collective-permute-done((f32[32,64,16]{1,2,0:T(8,128)S(1)}, f32[32,64,16]{1,2,0:T(8,128)S(1)}, u32[]{:S(2)}, u32[]{:S(2)}) %collective-permute-start.21) | collective-permute-done | bytes 131104 | tf_op jit(solution)/shard_map/ppermute | solution.py:22
  147.0 0.9 add_select_fusion
  148.0 3.9 fusion.69
  151.8 1.9 while.26
  152.1 0.7 fusion.105
  152.8 0.9 exponential_reduce_fusion.2
  153.8 3.8 broadcast_in_dim.41
  157.5 8.0 %while.27 = (s32[]{:T(128)}, f32[128,1,8,128]{0,3,2,1:T(8,128)S(1)}, f32[8192,2,1,128]{3,0,2,1:T(8,128)}, s32[]{:T(128)}, bf16[8192,1,128]{2,0,1:T(8,128)(2,1)S(...) while((s32[]{:T(128)}, ...), condition=%wide.region_7.8_spmd.clone, body=%wide.region_6.7_spmd.clone.sunk | while | flops 1354499200 | bytes 27415800 | solution.py:144
  157.5 0.7 fusion.116
  158.5 2.5 fusion.117
  161.4 1.0 fusion.119
  162.4 0.7 convolution_bitcast_fusion.4
  163.2 2.3 fusion.120
  165.9 0.6 copy-done.1
  166.5 1.7 multiply_reduce_fusion
  170.3 1.5 collective-permute-start.24
  172.3 1.8 fusion.46
  174.2 1.8 fusion.50
  176.4 2.2 collective-permute-start.23
  178.5 1.4 collective-permute-start.25
  180.0 0.9 copy.80
  180.9 1.0 copy.86
  181.9 0.7 copy.87
  182.6 0.6 add.216
  183.7 0.6 add.219
  184.3 193.7 %reduce-scatter.2.cloned.1.call-done = f32[128,2,1,128]{3,0,2,1:T(8,128)} async-done(((f32[8192,2,1,128]{3,0,2,1:T(8,128)}), f32[128,2,1,128]{3,0,2,1:T(8,128)}) %reduce-scatter.2.cloned.1.call-update) | async-done | bytes 131088 | tf_op jit(solution)/shard_map/reduce_scatter | solution.py:146
  378.0 0.9 convert.4
  378.9 0.6 slice_bitcast_fusion
  (104 shorter events, 6.7 us)
Async XLA Ops:
  7.2 9.9 %copy-start.8 = (f32[128,16]{0,1:T(8,128)S(1)}, f32[128,16]{0,1:T(8,128)}, u32[]{:S(2)}) copy-start(f32[128,16]{0,1:T(8,128)} %param.21) | copy-start | bytes 24580
  7.2 15.6 %copy-start.9 = (f32[128,16]{0,1:T(8,128)S(1)}, f32[128,16]{0,1:T(8,128)}, u32[]{:S(2)}) copy-start(f32[128,16]{0,1:T(8,128)} %param.22) | copy-start | bytes 24580
  7.2 140.8 %all-gather.2.cloned.1.call-start = ((), (), s32[]{:S(2)}) async-start(), calls=%async_computation.1 | async-start | bytes 4259840 | tf_op jit(solution)/shard_map/all_gather | solution.py:56
  8.7 18.0 %copy-start.4 = (bf16[128,8,128]{2,1,0:T(8,128)(2,1)S(1)}, bf16[128,8,128]{2,1,0:T(8,128)(2,1)}, u32[]{:S(2)}) copy-start(bf16[128,8,128]{2,1,0:T(8,128)(2,1)} %param.18) | copy-start | bytes 786436
  8.7 18.0 %copy-start.5 = (bf16[128,8,128]{2,1,0:T(8,128)(2,1)S(1)}, bf16[128,8,128]{2,1,0:T(8,128)(2,1)}, u32[]{:S(2)}) copy-start(bf16[128,8,128]{2,1,0:T(8,128)(2,1)} %param.17) | copy-start | bytes 786436
  8.7 369.3 %reduce-scatter.2.cloned.1.call-start = ((), (), s32[]{:S(2)}) async-start(), calls=%async_computation.2 | async-start | bytes 8519680 | tf_op jit(solution)/shard_map/reduce_scatter | solution.py:146
  9.8 18.0 %collective-permute-start.11 = (f32[32]{0:T(128)S(1)}, f32[32]{0:T(128)S(1)}, u32[]{:S(2)}, u32[]{:S(2)}) collective-permute-start(f32[32]{0:T(128)S(1)} %fusion.68), channel_id=1, source_target_pairs={{4,0},{8,4},{12,8},{16,12},{20,16},{24,20},{28,24},{32,28},{36,32}... | collective-permute-start | bytes 392 | tf_op jit(solution)/shard_map/ppermute | solution.py:22
  11.1 16.7 %collective-permute-start = (f32[32]{0:T(128)S(1)}, f32[32]{0:T(128)S(1)}, u32[]{:S(2)}, u32[]{:S(2)}) collective-permute-start(f32[32]{0:T(128)S(1)} %fusion.68), channel_id=1, source_target_pairs={{0,4},{4,8},{8,12},{12,16},{16,20},{20,24},{24,28},{28,32},{32,36}... | collective-permute-start | bytes 392 | tf_op jit(solution)/shard_map/ppermute | solution.py:21
  14.2 12.8 %copy-start.6 = (bf16[128,8,128]{2,1,0:T(8,128)(2,1)S(1)}, bf16[128,8,128]{2,1,0:T(8,128)(2,1)}, u32[]{:S(2)}) copy-start(bf16[128,8,128]{2,1,0:T(8,128)(2,1)} %param.14) | copy-start | bytes 786436
  16.9 9.8 %copy-start = (bf16[128,2048]{0,1:T(8,128)(2,1)}, bf16[128,2048]{0,1:T(8,128)(2,1)S(1)}, u32[]{:S(2)}) copy-start(bf16[128,2048]{0,1:T(8,128)(2,1)S(1)} %copy.74) | copy-start | bytes 1572868
  19.7 41.7 %collective-permute-start.5 = (f32[32,64,16]{1,2,0:T(8,128)S(1)}, f32[32,64,16]{1,2,0:T(8,128)S(1)}, u32[]{:S(2)}, u32[]{:S(2)}) collective-permute-start(f32[32,64,16]{1,2,0:T(8,128)S(1)} %fusion.63), channel_id=1, source_target_pairs={{0,4},{4,8},{8,12},{12,16},{16,20},{20,24},{24,28},{28,32},{32,36}... | collective-permute-start | bytes 393224 | tf_op jit(solution)/shard_map/ppermute | solution.py:21
  25.4 36.0 %collective-permute-start.16 = (f32[32,64,16]{1,2,0:T(8,128)S(1)}, f32[32,64,16]{1,2,0:T(8,128)S(1)}, u32[]{:S(2)}, u32[]{:S(2)}) collective-permute-start(f32[32,64,16]{1,2,0:T(8,128)S(1)} %fusion.60), channel_id=1, source_target_pairs={{4,0},{8,4},{12,8},{16,12},{20,16},{24,20},{28,24},{32,28},{36,32}... | collective-permute-start | bytes 393224 | tf_op jit(solution)/shard_map/ppermute | solution.py:22
  27.8 5.9 %collective-permute-start.1 = (f32[32]{0:T(128)S(1)}, f32[32]{0:T(128)S(1)}, u32[]{:S(2)}, u32[]{:S(2)}) collective-permute-start(f32[32]{0:T(128)S(1)} %get-tuple-element.273), channel_id=1, source_target_pairs={{0,8},{4,12},{8,16},{12,20},{16,24},{20,28},{24,32},{28,36},{32,40... | collective-permute-start | bytes 392 | tf_op jit(solution)/shard_map/ppermute | solution.py:21
  32.5 8.2 %collective-permute-start.12 = (f32[32]{0:T(128)S(1)}, f32[32]{0:T(128)S(1)}, u32[]{:S(2)}, u32[]{:S(2)}) collective-permute-start(f32[32]{0:T(128)S(1)} %get-tuple-element.272), channel_id=1, source_target_pairs={{8,0},{12,4},{16,8},{20,12},{24,16},{28,20},{32,24},{36,28},{40,32... | collective-permute-start | bytes 392 | tf_op jit(solution)/shard_map/ppermute | solution.py:22
  33.8 8.2 %collective-permute-start.2 = (f32[32]{0:T(128)S(1)}, f32[32]{0:T(128)S(1)}, u32[]{:S(2)}, u32[]{:S(2)}) collective-permute-start(f32[32]{0:T(128)S(1)} %broadcast_select_fusion.12), channel_id=1, source_target_pairs={{0,16},{4,20},{8,24},{12,28},{16,32},{20,36},{24,40},{28,44},{32,4... | collective-permute-start | bytes 392 | tf_op jit(solution)/shard_map/ppermute | solution.py:21
  40.7 12.0 %collective-permute-start.13 = (f32[32]{0:T(128)S(1)}, f32[32]{0:T(128)S(1)}, u32[]{:S(2)}, u32[]{:S(2)}) collective-permute-start(f32[32]{0:T(128)S(1)} %broadcast_select_fusion.3), channel_id=1, source_target_pairs={{16,0},{20,4},{24,8},{28,12},{32,16},{36,20},{40,24},{44,28},{48,3... | collective-permute-start | bytes 392 | tf_op jit(solution)/shard_map/ppermute | solution.py:22
  42.0 12.0 %collective-permute-start.3 = (f32[32]{0:T(128)S(1)}, f32[32]{0:T(128)S(1)}, u32[]{:S(2)}, u32[]{:S(2)}) collective-permute-start(f32[32]{0:T(128)S(1)} %broadcast_select_fusion.14), channel_id=1, source_target_pairs={{0,32},{4,36},{8,40},{12,44},{16,48},{20,52},{24,56},{28,60},{32,6... | collective-permute-start | bytes 392 | tf_op jit(solution)/shard_map/ppermute | solution.py:21
  52.8 7.2 %collective-permute-start.14 = (f32[32]{0:T(128)S(1)}, f32[32]{0:T(128)S(1)}, u32[]{:S(2)}, u32[]{:S(2)}) collective-permute-start(f32[32]{0:T(128)S(1)} %broadcast_select_fusion.5), channel_id=1, source_target_pairs={{32,0},{36,4},{40,8},{44,12},{48,16},{52,20},{56,24},{60,28},{64,3... | collective-permute-start | bytes 392 | tf_op jit(solution)/shard_map/ppermute | solution.py:22
  54.1 7.2 %collective-permute-start.4 = (f32[32]{0:T(128)S(1)}, f32[32]{0:T(128)S(1)}, u32[]{:S(2)}, u32[]{:S(2)}) collective-permute-start(f32[32]{0:T(128)S(1)} %broadcast_select_fusion.16), channel_id=1, source_target_pairs={{0,64},{4,68},{8,72},{12,76},{16,80},{20,84},{24,88},{28,92},{32,9... | collective-permute-start | bytes 392 | tf_op jit(solution)/shard_map/ppermute | solution.py:21
  60.0 12.8 %collective-permute-start.15 = (f32[32]{0:T(128)S(1)}, f32[32]{0:T(128)S(1)}, u32[]{:S(2)}, u32[]{:S(2)}) collective-permute-start(f32[32]{0:T(128)S(1)} %broadcast_select_fusion.7), channel_id=1, source_target_pairs={{64,0},{68,4},{72,8},{76,12},{80,16},{84,20},{88,24},{92,28},{96,3... | collective-permute-start | bytes 392 | tf_op jit(solution)/shard_map/ppermute | solution.py:22
  61.5 12.6 %collective-permute-start.6 = (f32[32,64,16]{1,2,0:T(8,128)S(1)}, f32[32,64,16]{1,2,0:T(8,128)S(1)}, u32[]{:S(2)}, u32[]{:S(2)}) collective-permute-start(f32[32,64,16]{1,2,0:T(8,128)S(1)} %get-tuple-element.277), channel_id=1, source_target_pairs={{0,8},{4,12},{8,16},{12,20},{16,24},{20,28},{24,32},{28,36},{32,40... | collective-permute-start | bytes 393224 | tf_op jit(solution)/shard_map/ppermute | solution.py:21
  72.8 12.0 %collective-permute-start.17 = (f32[32,64,16]{1,2,0:T(8,128)S(1)}, f32[32,64,16]{1,2,0:T(8,128)S(1)}, u32[]{:S(2)}, u32[]{:S(2)}) collective-permute-start(f32[32,64,16]{1,2,0:T(8,128)S(1)} %get-tuple-element.276), channel_id=1, source_target_pairs={{8,0},{12,4},{16,8},{20,12},{24,16},{28,20},{32,24},{36,28},{40,32... | collective-permute-start | bytes 393224 | tf_op jit(solution)/shard_map/ppermute | solution.py:22
  74.2 14.1 %collective-permute-start.7 = (f32[32,64,16]{1,2,0:T(8,128)S(1)}, f32[32,64,16]{1,2,0:T(8,128)S(1)}, u32[]{:S(2)}, u32[]{:S(2)}) collective-permute-start(f32[32,64,16]{1,2,0:T(8,128)S(1)} %add_select_fusion.18), channel_id=1, source_target_pairs={{0,16},{4,20},{8,24},{12,28},{16,32},{20,36},{24,40},{28,44},{32,4... | collective-permute-start | bytes 393224 | tf_op jit(solution)/shard_map/ppermute | solution.py:21
  84.9 10.8 %collective-permute-start.18 = (f32[32,64,16]{1,2,0:T(8,128)S(1)}, f32[32,64,16]{1,2,0:T(8,128)S(1)}, u32[]{:S(2)}, u32[]{:S(2)}) collective-permute-start(f32[32,64,16]{1,2,0:T(8,128)S(1)} %add_select_fusion.8), channel_id=1, source_target_pairs={{16,0},{20,4},{24,8},{28,12},{32,16},{36,20},{40,24},{44,28},{48,3... | collective-permute-start | bytes 393224 | tf_op jit(solution)/shard_map/ppermute | solution.py:22
  88.4 13.5 %collective-permute-start.8 = (f32[32,64,16]{1,2,0:T(8,128)S(1)}, f32[32,64,16]{1,2,0:T(8,128)S(1)}, u32[]{:S(2)}, u32[]{:S(2)}) collective-permute-start(f32[32,64,16]{1,2,0:T(8,128)S(1)} %add_select_fusion.17), channel_id=1, source_target_pairs={{0,32},{4,36},{8,40},{12,44},{16,48},{20,52},{24,56},{28,60},{32,6... | collective-permute-start | bytes 393224 | tf_op jit(solution)/shard_map/ppermute | solution.py:21
  95.8 16.8 %collective-permute-start.19 = (f32[32,64,16]{1,2,0:T(8,128)S(1)}, f32[32,64,16]{1,2,0:T(8,128)S(1)}, u32[]{:S(2)}, u32[]{:S(2)}) collective-permute-start(f32[32,64,16]{1,2,0:T(8,128)S(1)} %add_select_fusion.7), channel_id=1, source_target_pairs={{32,0},{36,4},{40,8},{44,12},{48,16},{52,20},{56,24},{60,28},{64,3... | collective-permute-start | bytes 393224 | tf_op jit(solution)/shard_map/ppermute | solution.py:22
  102.0 14.5 %collective-permute-start.9 = (f32[32,64,16]{1,2,0:T(8,128)S(1)}, f32[32,64,16]{1,2,0:T(8,128)S(1)}, u32[]{:S(2)}, u32[]{:S(2)}) collective-permute-start(f32[32,64,16]{1,2,0:T(8,128)S(1)} %add_select_fusion.16), channel_id=1, source_target_pairs={{0,64},{4,68},{8,72},{12,76},{16,80},{20,84},{24,88},{28,92},{32,9... | collective-permute-start | bytes 393224 | tf_op jit(solution)/shard_map/ppermute | solution.py:21
  112.8 21.9 %collective-permute-start.20 = (f32[32,64,16]{1,2,0:T(8,128)S(1)}, f32[32,64,16]{1,2,0:T(8,128)S(1)}, u32[]{:S(2)}, u32[]{:S(2)}) collective-permute-start(f32[32,64,16]{1,2,0:T(8,128)S(1)} %add_select_fusion.6), channel_id=1, source_target_pairs={{64,0},{68,4},{72,8},{76,12},{80,16},{84,20},{88,24},{92,28},{96,3... | collective-permute-start | bytes 393224 | tf_op jit(solution)/shard_map/ppermute | solution.py:22
  116.6 21.9 %collective-permute-start.10 = (f32[32,64,16]{1,2,0:T(8,128)S(1)}, f32[32,64,16]{1,2,0:T(8,128)S(1)}, u32[]{:S(2)}, u32[]{:S(2)}) collective-permute-start(f32[32,64,16]{1,2,0:T(8,128)S(1)} %add_select_fusion.15), channel_id=1, source_target_pairs={{0,128},{4,132},{8,136},{12,140},{16,144},{20,148},{24,152},{28,15... | collective-permute-start | bytes 393224 | tf_op jit(solution)/shard_map/ppermute | solution.py:21
  134.8 12.2 %collective-permute-start.21 = (f32[32,64,16]{1,2,0:T(8,128)S(1)}, f32[32,64,16]{1,2,0:T(8,128)S(1)}, u32[]{:S(2)}, u32[]{:S(2)}) collective-permute-start(f32[32,64,16]{1,2,0:T(8,128)S(1)} %add_select_fusion.5), channel_id=1, source_target_pairs={{128,0},{132,4},{136,8},{140,12},{144,16},{148,20},{152,24},{156,2... | collective-permute-start | bytes 393224 | tf_op jit(solution)/shard_map/ppermute | solution.py:22
  157.5 0.9 copy-start.7
  165.5 1.0 copy-start.1
  165.5 2.7 copy-start.2
  165.5 4.0 %copy-start.3 = (f32[32,64,16]{1,2,0:T(8,128)S(1)}, f32[32,64,16]{1,2,0:T(8,128)}, u32[]{:S(2)}) copy-start(f32[32,64,16]{1,2,0:T(8,128)} %add_select_fusion.10) | copy-start | bytes 393220
  169.0 7.4 %collective-permute-start.22 = (f32[128,16]{0,1:T(8,128)S(1)}, f32[128,16]{0,1:T(8,128)S(1)}, u32[]{:S(2)}, u32[]{:S(2)}) collective-permute-start(f32[128,16]{0,1:T(8,128)S(1)} %convolution_add_fusion.1), channel_id=1, source_target_pairs={{0,1},{1,0},{2,3},{3,2},{4,5},{5,4},{6,7},{7,6},{8,9},{9,8},{10,11... | collective-permute-start | bytes 24584 | tf_op jit(solution)/shard_map/ppermute | solution.py:40
  170.3 8.3 %collective-permute-start.24 = (f32[128,16]{0,1:T(8,128)S(1)}, f32[128,16]{0,1:T(8,128)S(1)}, u32[]{:S(2)}, u32[]{:S(2)}) collective-permute-start(f32[128,16]{0,1:T(8,128)S(1)} %convolution_add_fusion), channel_id=1, source_target_pairs={{0,1},{1,0},{2,3},{3,2},{4,5},{5,4},{6,7},{7,6},{8,9},{9,8},{10,11... | collective-permute-start | bytes 24584 | tf_op jit(solution)/shard_map/ppermute | solution.py:40
  176.4 6.3 %collective-permute-start.23 = (f32[128,16]{0,1:T(8,128)S(1)}, f32[128,16]{0,1:T(8,128)S(1)}, u32[]{:S(2)}, u32[]{:S(2)}) collective-permute-start(f32[128,16]{0,1:T(8,128)S(1)} %add.215), channel_id=1, source_target_pairs={{0,2},{1,3},{2,0},{3,1},{4,6},{5,7},{6,4},{7,5},{8,10},{9,11},{10,... | collective-permute-start | bytes 24584 | tf_op jit(solution)/shard_map/ppermute | solution.py:40
  178.5 5.2 %collective-permute-start.25 = (f32[128,16]{0,1:T(8,128)S(1)}, f32[128,16]{0,1:T(8,128)S(1)}, u32[]{:S(2)}, u32[]{:S(2)}) collective-permute-start(f32[128,16]{0,1:T(8,128)S(1)} %add.218), channel_id=1, source_target_pairs={{0,2},{1,3},{2,0},{3,1},{4,6},{5,7},{6,4},{7,5},{8,10},{9,11},{10,... | collective-permute-start | bytes 24584 | tf_op jit(solution)/shard_map/ppermute | solution.py:40
Sparse Core Ops, SparseCore 0:
  10.8 83.6 all-gather.1
  165.6 212.3 reduce-scatter.1

commit v3 on v2

--- a/solution.py
+++ b/solution.py
@@ -1,4 +1,6 @@
 import math
+
+import numpy as np
 
 import jax
 import jax.numpy as jnp
@@ -6,7 +8,7 @@
 from jax.sharding import PartitionSpec as P
 
 
-CTX = "ctx"
+CTX = ("z", "yc")
 
 
 def carried_both(forward, backward, axis):
@@ -53,9 +55,9 @@
     local_groups = key_vectors.shape[1]
     repeats = local_heads // local_groups
     score_scale = 1.0 / math.sqrt(head_width)
-    whole_kv = lax.all_gather(
-        jnp.concatenate([key_vectors, value_vectors], axis=1), CTX, axis=0, tiled=True
-    )
+    whole_kv = jnp.concatenate([key_vectors, value_vectors], axis=1)
+    whole_kv = lax.all_gather(whole_kv, CTX[1], axis=0, tiled=True)
+    whole_kv = lax.all_gather(whole_kv, CTX[0], axis=0, tiled=True)
     whole_kv, carried = lax.optimization_barrier((whole_kv, carried))
     whole_keys, whole_values = (whole_kv[:, :local_groups], whole_kv[:, local_groups:])
     all_tokens = whole_keys.shape[0]
@@ -143,7 +145,10 @@
     query_start = jnp.zeros(entry[0].shape, jnp.float32)
     query_acc, buffer = lax.fori_loop(0, entry[5], joint_step, (query_start, buffer))
     buffer, query_acc, carried = lax.optimization_barrier((buffer, query_acc, carried))
-    key_rows = lax.psum_scatter(buffer, CTX, scatter_dimension=0, tiled=True)
+    ctx_size = all_tokens // local_rows
+    parts = buffer.reshape(ctx_size, local_rows, *buffer.shape[1:]).astype(jnp.bfloat16)
+    parts = lax.all_to_all(parts, CTX, 0, 0, tiled=False)
+    key_rows = jnp.sum(parts.astype(jnp.float32), axis=0)
     grad_queries = query_acc.reshape(local_rows, local_heads, head_width).astype(jnp.bfloat16)
     grads = (grad_queries, key_rows[:, 0].astype(jnp.bfloat16), key_rows[:, 1].astype(jnp.bfloat16))
     return grads, carried
@@ -297,4 +302,10 @@
         P(CTX, None),
         P(CTX, "tp"),
     )
-    return jax.shard_map(local, mesh=mesh, in_specs=in_specs, out_specs=out_specs, check_vma=False)
+    ctx_size = mesh.shape["ctx"]
+    inner = math.gcd(ctx_size, 8)
+    devices = np.asarray(mesh.devices).reshape(ctx_size // inner, inner, mesh.shape["tp"])
+    split_mesh = jax.sharding.Mesh(devices, ("z", "yc", "tp"))
+    return jax.shard_map(
+        local, mesh=split_mesh, in_specs=in_specs, out_specs=out_specs, check_vma=False
+    )

time: 388 us -> 362 us (0.933)
  waiting for transfers between devices: 225 us -> 109 us
  starting transfers between devices: 100 us -> 169 us
  blocking collectives: 0 us -> 14.7 us
  other arithmetic: 11.5 us -> 16.7 us
    reduce_scatter x1 -> x0, waiting for transfers between devices: 194 us -> none  [attention_grads(): key_rows = lax.psum_scatter(buffer, CTX, scatter_dimension=0, tiled=True)]
    all_to_all x0 -> x1, waiting for transfers between devices: none -> 77.8 us  [attention_grads(): parts = lax.all_to_all(parts, CTX, 0, 0, tiled=False)]
    all_to_all x0 -> x1, starting transfers between devices: none -> 70.2 us  [attention_grads(): parts = lax.all_to_all(parts, CTX, 0, 0, tiled=False)]
    all_gather x0 -> x1, blocking collectives: none -> 14.7 us  [attention_grads(): whole_kv = lax.all_gather(whole_kv, CTX[1], axis=0, tiled=True)]
    convert_element_type x0 -> x1, other arithmetic: none -> 3.92 us  [attention_grads(): buffer.reshape(ctx_size, local_rows, *buffer.shape[1:]).astype(jnp.bfloat16)]
  transfers between devices with their start and end apart: 28 -> 28, of which waited for: 9 -> 9; matrix products, arithmetic and copies ran while one was open for 6% -> 7% of each run, Pallas kernels for 0% -> 0%
where the time goes in v3:
time: 362 us; the launch traced here: 360 us
  starting transfers between devices  169 us (47%)
  waiting for transfers between devices  109 us (30%)
  matrix products  18.2 us (5%)
  local copies, waits for them, and re-layouts  18 us (5%)
  other arithmetic  16.7 us (5%)
  between operations  14.8 us (4%)
  blocking collectives  14.7 us (4%)
    ppermute x11, starting transfers between devices, carried_both(): got_fwd = lax.ppermute(fwd_total, axis, up)  78.4 us
    all_to_all x1, waiting for transfers between devices, attention_grads(): parts = lax.all_to_all(parts, CTX, 0, 0, tiled=False)  77.8 us
    all_to_all x1, starting transfers between devices, attention_grads(): parts = lax.all_to_all(parts, CTX, 0, 0, tiled=False)  70.2 us
    ppermute x11, waiting for transfers between devices, carried_both(): got_bwd = lax.ppermute(bwd_total, axis, down)  20.8 us
    all_gather x1, blocking collectives, attention_grads(): whole_kv = lax.all_gather(whole_kv, CTX[1], axis=0, tiled=True)  14.7 us
    ppermute x11, starting transfers between devices, carried_both(): got_bwd = lax.ppermute(bwd_total, axis, down)  14.2 us
    ppermute x11, waiting for transfers between devices, carried_both(): got_fwd = lax.ppermute(fwd_total, axis, up)  9.67 us
  transfers between devices with their start and end apart: 28, of which 9 were waited for; matrix products, arithmetic and copies ran while one was open for 7% of the time, Pallas kernels for 0%

profile of v3, /device:TPU:2, one launch (start us, length us, event | category | flops | bytes accessed | tf_op | source)
XLA Modules:
  0.0 360.1 jit_solution(3085189779972882152)
XLA Ops:
  7.2 0.8 pad_maximum_fusion
  8.0 14.7 %all_gather.6 = bf16[1024,2,128]{2,0,1:T(8,128)(2,1)} all-gather(bf16[128,2,128]{2,0,1:T(8,128)(2,1)S(1)} %pad_maximum_fusion), channel_id=1, replica_groups=mesh['z'=8,'yc'=8,'tp'=4] {'yc'}, dimensions={0}, use_global_device_ids=true | all-gather | bytes 589824 | tf_op jit(solution)/shard_map/all_gather | solution.py:59
  22.8 0.9 copy.94
  23.8 1.3 collective-permute-start.11
  25.1 3.0 collective-permute-start
  28.2 1.4 copy.97
  29.6 1.3 copy.95
  31.2 2.5 fusion.63
  33.7 3.5 collective-permute-start.5
  37.3 2.5 fusion.60
  39.8 1.3 collective-permute-start.16
  41.4 0.8 copy_bitcast_fusion
  42.3 4.2 %collective-permute-start.1 = (f32[32]{0:T(128)S(1)}, f32[32]{0:T(128)S(1)}, u32[]{:S(2)}, u32[]{:S(2)}) collective-permute-start(f32[32]{0:T(128)S(1)} %get-tuple-element.291), channel_id=1, source_target_pairs={{0,8},{4,12},{8,16},{12,20},{16,24},{20,28},{24,32},{28,36},{32,40... | collective-permute-start | bytes 392 | tf_op jit(solution)/shard_map/ppermute | solution.py:23
  46.4 1.3 collective-permute-start.12
  47.8 7.0 %collective-permute-start.2 = (f32[32]{0:T(128)S(1)}, f32[32]{0:T(128)S(1)}, u32[]{:S(2)}, u32[]{:S(2)}) collective-permute-start(f32[32]{0:T(128)S(1)} %broadcast_select_fusion.12), channel_id=1, source_target_pairs={{0,16},{4,20},{8,24},{12,28},{16,32},{20,36},{24,40},{28,44},{32,4... | collective-permute-start | bytes 392 | tf_op jit(solution)/shard_map/ppermute | solution.py:23
  54.8 1.3 collective-permute-start.13
  56.1 10.7 %collective-permute-start.3 = (f32[32]{0:T(128)S(1)}, f32[32]{0:T(128)S(1)}, u32[]{:S(2)}, u32[]{:S(2)}) collective-permute-start(f32[32]{0:T(128)S(1)} %broadcast_select_fusion.14), channel_id=1, source_target_pairs={{0,32},{4,36},{8,40},{12,44},{16,48},{20,52},{24,56},{28,60},{32,6... | collective-permute-start | bytes 392 | tf_op jit(solution)/shard_map/ppermute | solution.py:23
  66.8 1.3 collective-permute-start.14
  68.1 5.9 %collective-permute-start.4 = (f32[32]{0:T(128)S(1)}, f32[32]{0:T(128)S(1)}, u32[]{:S(2)}, u32[]{:S(2)}) collective-permute-start(f32[32]{0:T(128)S(1)} %broadcast_select_fusion.16), channel_id=1, source_target_pairs={{0,64},{4,68},{8,72},{12,76},{16,80},{20,84},{24,88},{28,92},{32,9... | collective-permute-start | bytes 392 | tf_op jit(solution)/shard_map/ppermute | solution.py:23
  74.1 1.3 collective-permute-start.15
  75.6 2.0 collective-permute-start.6
  77.6 9.2 %collective-permute-done.15 = f32[32]{0:T(128)S(1)} collective-permute-done((f32[32]{0:T(128)S(1)}, f32[32]{0:T(128)S(1)}, u32[]{:S(2)}, u32[]{:S(2)}) %collective-permute-start.15) | collective-permute-done | bytes 160 | tf_op jit(solution)/shard_map/ppermute | solution.py:24
  86.8 1.3 collective-permute-start.17
  88.2 5.0 %collective-permute-start.7 = (f32[32,64,16]{1,2,0:T(8,128)S(1)}, f32[32,64,16]{1,2,0:T(8,128)S(1)}, u32[]{:S(2)}, u32[]{:S(2)}) collective-permute-start(f32[32,64,16]{1,2,0:T(8,128)S(1)} %add_select_fusion.18), channel_id=1, source_target_pairs={{0,16},{4,20},{8,24},{12,28},{16,32},{20,36},{24,40},{28,44},{32,4... | collective-permute-start | bytes 393224 | tf_op jit(solution)/shard_map/ppermute | solution.py:23
  93.3 4.0 %collective-permute-done.17 = f32[32,64,16]{1,2,0:T(8,128)S(1)} collective-permute-done((f32[32,64,16]{1,2,0:T(8,128)S(1)}, f32[32,64,16]{1,2,0:T(8,128)S(1)}, u32[]{:S(2)}, u32[]{:S(2)}) %collective-permute-start.17) | collective-permute-done | bytes 131104 | tf_op jit(solution)/shard_map/ppermute | solution.py:24
  97.4 1.3 collective-permute-start.18
  98.7 0.8 collective-permute-done.7
  99.7 9.6 %collective-permute-start.8 = (f32[32,64,16]{1,2,0:T(8,128)S(1)}, f32[32,64,16]{1,2,0:T(8,128)S(1)}, u32[]{:S(2)}, u32[]{:S(2)}) collective-permute-start(f32[32,64,16]{1,2,0:T(8,128)S(1)} %add_select_fusion.17), channel_id=1, source_target_pairs={{0,32},{4,36},{8,40},{12,44},{16,48},{20,52},{24,56},{28,60},{32,6... | collective-permute-start | bytes 393224 | tf_op jit(solution)/shard_map/ppermute | solution.py:23
  109.4 1.3 collective-permute-start.19
  110.7 4.0 %collective-permute-done.8 = f32[32,64,16]{1,2,0:T(8,128)S(1)} collective-permute-done((f32[32,64,16]{1,2,0:T(8,128)S(1)}, f32[32,64,16]{1,2,0:T(8,128)S(1)}, u32[]{:S(2)}, u32[]{:S(2)}) %collective-permute-start.8) | collective-permute-done | bytes 131104 | tf_op jit(solution)/shard_map/ppermute | solution.py:23
  114.8 9.4 %collective-permute-start.9 = (f32[32,64,16]{1,2,0:T(8,128)S(1)}, f32[32,64,16]{1,2,0:T(8,128)S(1)}, u32[]{:S(2)}, u32[]{:S(2)}) collective-permute-start(f32[32,64,16]{1,2,0:T(8,128)S(1)} %add_select_fusion.16), channel_id=1, source_target_pairs={{0,64},{4,68},{8,72},{12,76},{16,80},{20,84},{24,88},{28,92},{32,9... | collective-permute-start | bytes 393224 | tf_op jit(solution)/shard_map/ppermute | solution.py:23
  124.4 1.3 collective-permute-start.20
  125.7 2.4 collective-permute-done.9
  128.2 18.0 %collective-permute-start.10 = (f32[32,64,16]{1,2,0:T(8,128)S(1)}, f32[32,64,16]{1,2,0:T(8,128)S(1)}, u32[]{:S(2)}, u32[]{:S(2)}) collective-permute-start(f32[32,64,16]{1,2,0:T(8,128)S(1)} %add_select_fusion.15), channel_id=1, source_target_pairs={{0,128},{4,132},{8,136},{12,140},{16,144},{20,148},{24,152},{28,15... | collective-permute-start | bytes 393224 | tf_op jit(solution)/shard_map/ppermute | solution.py:23
  146.4 1.3 collective-permute-start.21
  147.7 2.4 collective-permute-done.10
  150.1 1.0 add_select_fusion.10
  151.1 7.5 %collective-permute-done.21 = f32[32,64,16]{1,2,0:T(8,128)S(1)} collective-permute-done((f32[32,64,16]{1,2,0:T(8,128)S(1)}, f32[32,64,16]{1,2,0:T(8,128)S(1)}, u32[]{:S(2)}, u32[]{:S(2)}) %collective-permute-start.21) | collective-permute-done | bytes 131104 | tf_op jit(solution)/shard_map/ppermute | solution.py:24
  158.6 1.0 add_select_fusion
  159.5 3.9 %fusion.69 = (bf16[8192,1,128]{2,0,1:T(8,128)(2,1)}, bf16[8192,1,128]{2,0,1:T(8,128)(2,1)S(1)}) fusion(bf16[8192,2,128]{2,0,1:T(8,128)(2,1)} %all-gather.2.cloned.1.call-done), kind=kLoop, calls=%fused_computation.141 | loop fusion | bytes 8388608 | tf_op jit(solution)/shard_map/slice | solution.py:62
  163.4 1.9 while.26
  163.6 0.7 fusion.105
  164.4 0.9 exponential_reduce_fusion.2
  165.3 3.8 %broadcast_in_dim.41 = f32[8192,2,1,128]{3,0,2,1:T(8,128)} broadcast(f32[]{:T(128)} %constant.46.clone.1), dimensions={} | broadcast | bytes 8388612 | tf_op jit(solution)/shard_map/broadcast_in_dim | solution.py:132
  169.1 8.0 %while.27 = (s32[]{:T(128)}, f32[128,1,8,128]{0,3,2,1:T(8,128)S(1)}, f32[8192,2,1,128]{3,0,2,1:T(8,128)}, s32[]{:T(128)}, bf16[8192,1,128]{2,0,1:T(8,128)(2,1)S(...) while((s32[]{:T(128)}, ...), condition=%wide.region_7.8_spmd.clone, body=%wide.region_6.7_spmd.clone.sunk | while | flops 1354499200 | bytes 27415800 | solution.py:146
  169.1 0.7 fusion.116
  170.0 2.5 fusion.117
  173.0 1.0 fusion.119
  174.0 0.7 convolution_bitcast_fusion.4
  174.7 2.3 fusion.120
  177.1 3.9 %bitcast_convert_fusion = bf16[8192,2,1,128]{3,0,1,2:T(8,128)(2,1)S(1)} fusion(f32[8192,2,1,128]{3,0,2,1:T(8,128)} %get-tuple-element.120), kind=kLoop, calls=%fused_computation.49 | loop fusion | flops 2097152 | bytes 12582912 | tf_op jit(solution)/shard_map/convert_element_type | solution.py:149
  181.0 2.3 copy.103
  183.3 70.2 %all-to-all-start = ((bf16[64,128,2,1,128]{4,1,2,3,0:T(8,128)(2,1)}), bf16[64,128,2,1,128]{4,1,2,3,0:T(8,128)(2,1)}, u32[]{:S(2)}, u32[]{:S(2)}) async-start(bf16[64,128,2,1,128]{4,1,2,3,0:T(8,128)(2,1)} %copy.103), calls=%async_computation | async-start | bytes 8388608 | tf_op jit(solution)/shard_map/all_to_all | solution.py:150
  253.9 1.7 multiply_reduce_fusion
  257.6 1.7 collective-permute-start.24
  259.9 1.8 fusion.46
  261.8 1.8 fusion.50
  264.0 2.2 collective-permute-start.23
  266.2 1.4 collective-permute-start.25
  267.6 0.9 copy.101
  268.5 1.0 copy.109
  269.5 0.7 copy.110
  271.9 77.8 %all-to-all-done = bf16[64,128,2,1,128]{4,1,2,3,0:T(8,128)(2,1)} async-done(((bf16[64,128,2,1,128]{4,1,2,3,0:T(8,128)(2,1)}), bf16[64,128,2,1,128]{4,1,2,3,0:T(8,128)(2,1)}, u32[]{:S(2)}, u32[]{:S(2)}) %all-to-all-start) | async-done | bytes 4194336 | tf_op jit(solution)/shard_map/all_to_all | solution.py:150
  349.7 2.9 reduce.15
  (106 shorter events, 8.5 us)
Async XLA Ops:
  7.2 24.0 %copy-start.8 = (f32[128,16]{0,1:T(8,128)S(1)}, f32[128,16]{0,1:T(8,128)}, u32[]{:S(2)}) copy-start(f32[128,16]{0,1:T(8,128)} %param.21) | copy-start | bytes 24580
  7.2 30.1 %copy-start.9 = (f32[128,16]{0,1:T(8,128)S(1)}, f32[128,16]{0,1:T(8,128)}, u32[]{:S(2)}) copy-start(f32[128,16]{0,1:T(8,128)} %param.22) | copy-start | bytes 24580
  7.2 152.3 %all-gather.2.cloned.1.call-start = ((), (), s32[]{:S(2)}) async-start(), calls=%async_computation.1 | async-start | bytes 4718592 | tf_op jit(solution)/shard_map/all_gather | solution.py:60
  22.8 18.4 %copy-start.4 = (bf16[128,8,128]{2,1,0:T(8,128)(2,1)S(1)}, bf16[128,8,128]{2,1,0:T(8,128)(2,1)}, u32[]{:S(2)}) copy-start(bf16[128,8,128]{2,1,0:T(8,128)(2,1)} %param.18) | copy-start | bytes 786436
  22.8 18.4 %copy-start.5 = (bf16[128,8,128]{2,1,0:T(8,128)(2,1)S(1)}, bf16[128,8,128]{2,1,0:T(8,128)(2,1)}, u32[]{:S(2)}) copy-start(bf16[128,8,128]{2,1,0:T(8,128)(2,1)} %param.17) | copy-start | bytes 786436
  23.8 18.4 %collective-permute-start.11 = (f32[32]{0:T(128)S(1)}, f32[32]{0:T(128)S(1)}, u32[]{:S(2)}, u32[]{:S(2)}) collective-permute-start(f32[32]{0:T(128)S(1)} %fusion.68), channel_id=1, source_target_pairs={{4,0},{8,4},{12,8},{16,12},{20,16},{24,20},{28,24},{32,28},{36,32}... | collective-permute-start | bytes 392 | tf_op jit(solution)/shard_map/ppermute | solution.py:24
  25.1 17.1 %collective-permute-start = (f32[32]{0:T(128)S(1)}, f32[32]{0:T(128)S(1)}, u32[]{:S(2)}, u32[]{:S(2)}) collective-permute-start(f32[32]{0:T(128)S(1)} %fusion.68), channel_id=1, source_target_pairs={{0,4},{4,8},{8,12},{12,16},{16,20},{20,24},{24,28},{28,32},{32,36}... | collective-permute-start | bytes 392 | tf_op jit(solution)/shard_map/ppermute | solution.py:23
  28.2 13.2 %copy-start.6 = (bf16[128,8,128]{2,1,0:T(8,128)(2,1)S(1)}, bf16[128,8,128]{2,1,0:T(8,128)(2,1)}, u32[]{:S(2)}) copy-start(bf16[128,8,128]{2,1,0:T(8,128)(2,1)} %param.14) | copy-start | bytes 786436
  30.9 44.6 %copy-start = (bf16[128,2048]{0,1:T(8,128)(2,1)}, bf16[128,2048]{0,1:T(8,128)(2,1)S(1)}, u32[]{:S(2)}) copy-start(bf16[128,2048]{0,1:T(8,128)(2,1)S(1)} %copy.95) | copy-start | bytes 1572868
  33.7 41.7 %collective-permute-start.5 = (f32[32,64,16]{1,2,0:T(8,128)S(1)}, f32[32,64,16]{1,2,0:T(8,128)S(1)}, u32[]{:S(2)}, u32[]{:S(2)}) collective-permute-start(f32[32,64,16]{1,2,0:T(8,128)S(1)} %fusion.63), channel_id=1, source_target_pairs={{0,4},{4,8},{8,12},{12,16},{16,20},{20,24},{24,28},{28,32},{32,36}... | collective-permute-start | bytes 393224 | tf_op jit(solution)/shard_map/ppermute | solution.py:23
  39.8 35.6 %collective-permute-start.16 = (f32[32,64,16]{1,2,0:T(8,128)S(1)}, f32[32,64,16]{1,2,0:T(8,128)S(1)}, u32[]{:S(2)}, u32[]{:S(2)}) collective-permute-start(f32[32,64,16]{1,2,0:T(8,128)S(1)} %fusion.60), channel_id=1, source_target_pairs={{4,0},{8,4},{12,8},{16,12},{20,16},{24,20},{28,24},{32,28},{36,32}... | collective-permute-start | bytes 393224 | tf_op jit(solution)/shard_map/ppermute | solution.py:24
  42.3 5.5 %collective-permute-start.1 = (f32[32]{0:T(128)S(1)}, f32[32]{0:T(128)S(1)}, u32[]{:S(2)}, u32[]{:S(2)}) collective-permute-start(f32[32]{0:T(128)S(1)} %get-tuple-element.291), channel_id=1, source_target_pairs={{0,8},{4,12},{8,16},{12,20},{16,24},{20,28},{24,32},{28,36},{32,40... | collective-permute-start | bytes 392 | tf_op jit(solution)/shard_map/ppermute | solution.py:23
  46.4 8.3 %collective-permute-start.12 = (f32[32]{0:T(128)S(1)}, f32[32]{0:T(128)S(1)}, u32[]{:S(2)}, u32[]{:S(2)}) collective-permute-start(f32[32]{0:T(128)S(1)} %get-tuple-element.290), channel_id=1, source_target_pairs={{8,0},{12,4},{16,8},{20,12},{24,16},{28,20},{32,24},{36,28},{40,32... | collective-permute-start | bytes 392 | tf_op jit(solution)/shard_map/ppermute | solution.py:24
  47.8 8.3 %collective-permute-start.2 = (f32[32]{0:T(128)S(1)}, f32[32]{0:T(128)S(1)}, u32[]{:S(2)}, u32[]{:S(2)}) collective-permute-start(f32[32]{0:T(128)S(1)} %broadcast_select_fusion.12), channel_id=1, source_target_pairs={{0,16},{4,20},{8,24},{12,28},{16,32},{20,36},{24,40},{28,44},{32,4... | collective-permute-start | bytes 392 | tf_op jit(solution)/shard_map/ppermute | solution.py:23
  54.8 12.0 %collective-permute-start.13 = (f32[32]{0:T(128)S(1)}, f32[32]{0:T(128)S(1)}, u32[]{:S(2)}, u32[]{:S(2)}) collective-permute-start(f32[32]{0:T(128)S(1)} %broadcast_select_fusion.3), channel_id=1, source_target_pairs={{16,0},{20,4},{24,8},{28,12},{32,16},{36,20},{40,24},{44,28},{48,3... | collective-permute-start | bytes 392 | tf_op jit(solution)/shard_map/ppermute | solution.py:24
  56.1 12.0 %collective-permute-start.3 = (f32[32]{0:T(128)S(1)}, f32[32]{0:T(128)S(1)}, u32[]{:S(2)}, u32[]{:S(2)}) collective-permute-start(f32[32]{0:T(128)S(1)} %broadcast_select_fusion.14), channel_id=1, source_target_pairs={{0,32},{4,36},{8,40},{12,44},{16,48},{20,52},{24,56},{28,60},{32,6... | collective-permute-start | bytes 392 | tf_op jit(solution)/shard_map/ppermute | solution.py:23
  66.8 7.2 %collective-permute-start.14 = (f32[32]{0:T(128)S(1)}, f32[32]{0:T(128)S(1)}, u32[]{:S(2)}, u32[]{:S(2)}) collective-permute-start(f32[32]{0:T(128)S(1)} %broadcast_select_fusion.5), channel_id=1, source_target_pairs={{32,0},{36,4},{40,8},{44,12},{48,16},{52,20},{56,24},{60,28},{64,3... | collective-permute-start | bytes 392 | tf_op jit(solution)/shard_map/ppermute | solution.py:24
  68.1 7.2 %collective-permute-start.4 = (f32[32]{0:T(128)S(1)}, f32[32]{0:T(128)S(1)}, u32[]{:S(2)}, u32[]{:S(2)}) collective-permute-start(f32[32]{0:T(128)S(1)} %broadcast_select_fusion.16), channel_id=1, source_target_pairs={{0,64},{4,68},{8,72},{12,76},{16,80},{20,84},{24,88},{28,92},{32,9... | collective-permute-start | bytes 392 | tf_op jit(solution)/shard_map/ppermute | solution.py:23
  74.1 12.8 %collective-permute-start.15 = (f32[32]{0:T(128)S(1)}, f32[32]{0:T(128)S(1)}, u32[]{:S(2)}, u32[]{:S(2)}) collective-permute-start(f32[32]{0:T(128)S(1)} %broadcast_select_fusion.7), channel_id=1, source_target_pairs={{64,0},{68,4},{72,8},{76,12},{80,16},{84,20},{88,24},{92,28},{96,3... | collective-permute-start | bytes 392 | tf_op jit(solution)/shard_map/ppermute | solution.py:24
  75.6 12.6 %collective-permute-start.6 = (f32[32,64,16]{1,2,0:T(8,128)S(1)}, f32[32,64,16]{1,2,0:T(8,128)S(1)}, u32[]{:S(2)}, u32[]{:S(2)}) collective-permute-start(f32[32,64,16]{1,2,0:T(8,128)S(1)} %get-tuple-element.295), channel_id=1, source_target_pairs={{0,8},{4,12},{8,16},{12,20},{16,24},{20,28},{24,32},{28,36},{32,40... | collective-permute-start | bytes 393224 | tf_op jit(solution)/shard_map/ppermute | solution.py:23
  86.8 10.5 %collective-permute-start.17 = (f32[32,64,16]{1,2,0:T(8,128)S(1)}, f32[32,64,16]{1,2,0:T(8,128)S(1)}, u32[]{:S(2)}, u32[]{:S(2)}) collective-permute-start(f32[32,64,16]{1,2,0:T(8,128)S(1)} %get-tuple-element.294), channel_id=1, source_target_pairs={{8,0},{12,4},{16,8},{20,12},{24,16},{28,20},{32,24},{36,28},{40,32... | collective-permute-start | bytes 393224 | tf_op jit(solution)/shard_map/ppermute | solution.py:24
  88.2 11.3 %collective-permute-start.7 = (f32[32,64,16]{1,2,0:T(8,128)S(1)}, f32[32,64,16]{1,2,0:T(8,128)S(1)}, u32[]{:S(2)}, u32[]{:S(2)}) collective-permute-start(f32[32,64,16]{1,2,0:T(8,128)S(1)} %add_select_fusion.18), channel_id=1, source_target_pairs={{0,16},{4,20},{8,24},{12,28},{16,32},{20,36},{24,40},{28,44},{32,4... | collective-permute-start | bytes 393224 | tf_op jit(solution)/shard_map/ppermute | solution.py:23
  97.4 11.9 %collective-permute-start.18 = (f32[32,64,16]{1,2,0:T(8,128)S(1)}, f32[32,64,16]{1,2,0:T(8,128)S(1)}, u32[]{:S(2)}, u32[]{:S(2)}) collective-permute-start(f32[32,64,16]{1,2,0:T(8,128)S(1)} %add_select_fusion.8), channel_id=1, source_target_pairs={{16,0},{20,4},{24,8},{28,12},{32,16},{36,20},{40,24},{44,28},{48,3... | collective-permute-start | bytes 393224 | tf_op jit(solution)/shard_map/ppermute | solution.py:24
  99.7 15.0 %collective-permute-start.8 = (f32[32,64,16]{1,2,0:T(8,128)S(1)}, f32[32,64,16]{1,2,0:T(8,128)S(1)}, u32[]{:S(2)}, u32[]{:S(2)}) collective-permute-start(f32[32,64,16]{1,2,0:T(8,128)S(1)} %add_select_fusion.17), channel_id=1, source_target_pairs={{0,32},{4,36},{8,40},{12,44},{16,48},{20,52},{24,56},{28,60},{32,6... | collective-permute-start | bytes 393224 | tf_op jit(solution)/shard_map/ppermute | solution.py:23
  109.4 14.8 %collective-permute-start.19 = (f32[32,64,16]{1,2,0:T(8,128)S(1)}, f32[32,64,16]{1,2,0:T(8,128)S(1)}, u32[]{:S(2)}, u32[]{:S(2)}) collective-permute-start(f32[32,64,16]{1,2,0:T(8,128)S(1)} %add_select_fusion.7), channel_id=1, source_target_pairs={{32,0},{36,4},{40,8},{44,12},{48,16},{52,20},{56,24},{60,28},{64,3... | collective-permute-start | bytes 393224 | tf_op jit(solution)/shard_map/ppermute | solution.py:24
  114.8 13.3 %collective-permute-start.9 = (f32[32,64,16]{1,2,0:T(8,128)S(1)}, f32[32,64,16]{1,2,0:T(8,128)S(1)}, u32[]{:S(2)}, u32[]{:S(2)}) collective-permute-start(f32[32,64,16]{1,2,0:T(8,128)S(1)} %add_select_fusion.16), channel_id=1, source_target_pairs={{0,64},{4,68},{8,72},{12,76},{16,80},{20,84},{24,88},{28,92},{32,9... | collective-permute-start | bytes 393224 | tf_op jit(solution)/shard_map/ppermute | solution.py:23
  124.4 21.9 %collective-permute-start.20 = (f32[32,64,16]{1,2,0:T(8,128)S(1)}, f32[32,64,16]{1,2,0:T(8,128)S(1)}, u32[]{:S(2)}, u32[]{:S(2)}) collective-permute-start(f32[32,64,16]{1,2,0:T(8,128)S(1)} %add_select_fusion.6), channel_id=1, source_target_pairs={{64,0},{68,4},{72,8},{76,12},{80,16},{84,20},{88,24},{92,28},{96,3... | collective-permute-start | bytes 393224 | tf_op jit(solution)/shard_map/ppermute | solution.py:24
  128.2 21.9 %collective-permute-start.10 = (f32[32,64,16]{1,2,0:T(8,128)S(1)}, f32[32,64,16]{1,2,0:T(8,128)S(1)}, u32[]{:S(2)}, u32[]{:S(2)}) collective-permute-start(f32[32,64,16]{1,2,0:T(8,128)S(1)} %add_select_fusion.15), channel_id=1, source_target_pairs={{0,128},{4,132},{8,136},{12,140},{16,144},{20,148},{24,152},{28,15... | collective-permute-start | bytes 393224 | tf_op jit(solution)/shard_map/ppermute | solution.py:23
  146.4 12.2 %collective-permute-start.21 = (f32[32,64,16]{1,2,0:T(8,128)S(1)}, f32[32,64,16]{1,2,0:T(8,128)S(1)}, u32[]{:S(2)}, u32[]{:S(2)}) collective-permute-start(f32[32,64,16]{1,2,0:T(8,128)S(1)} %add_select_fusion.5), channel_id=1, source_target_pairs={{128,0},{132,4},{136,8},{140,12},{144,16},{148,20},{152,24},{156,2... | collective-permute-start | bytes 393224 | tf_op jit(solution)/shard_map/ppermute | solution.py:24
  169.1 0.9 copy-start.7
  183.3 70.6 %copy-start.1 = (bf16[128,2048]{0,1:T(8,128)(2,1)S(1)}, bf16[128,2048]{0,1:T(8,128)(2,1)}, u32[]{:S(2)}) copy-start(bf16[128,2048]{0,1:T(8,128)(2,1)} %copy-done) | copy-start | bytes 1572868
  183.3 166.5 %all-to-all-start = ((bf16[64,128,2,1,128]{4,1,2,3,0:T(8,128)(2,1)}), bf16[64,128,2,1,128]{4,1,2,3,0:T(8,128)(2,1)}, u32[]{:S(2)}, u32[]{:S(2)}) async-start(bf16[64,128,2,1,128]{4,1,2,3,0:T(8,128)(2,1)} %copy.103), calls=%async_computation | async-start | bytes 8388608 | tf_op jit(solution)/shard_map/all_to_all | solution.py:150
  253.5 2.2 copy-start.2
  253.5 3.4 copy-start.3
  256.4 7.6 %collective-permute-start.22 = (f32[128,16]{0,1:T(8,128)S(1)}, f32[128,16]{0,1:T(8,128)S(1)}, u32[]{:S(2)}, u32[]{:S(2)}) collective-permute-start(f32[128,16]{0,1:T(8,128)S(1)} %convolution_add_fusion.1), channel_id=1, source_target_pairs={{0,1},{1,0},{2,3},{3,2},{4,5},{5,4},{6,7},{7,6},{8,9},{9,8},{10,11... | collective-permute-start | bytes 24584 | tf_op jit(solution)/shard_map/ppermute | solution.py:42
  257.6 8.6 %collective-permute-start.24 = (f32[128,16]{0,1:T(8,128)S(1)}, f32[128,16]{0,1:T(8,128)S(1)}, u32[]{:S(2)}, u32[]{:S(2)}) collective-permute-start(f32[128,16]{0,1:T(8,128)S(1)} %convolution_add_fusion), channel_id=1, source_target_pairs={{0,1},{1,0},{2,3},{3,2},{4,5},{5,4},{6,7},{7,6},{8,9},{9,8},{10,11... | collective-permute-start | bytes 24584 | tf_op jit(solution)/shard_map/ppermute | solution.py:42
  264.0 6.3 %collective-permute-start.23 = (f32[128,16]{0,1:T(8,128)S(1)}, f32[128,16]{0,1:T(8,128)S(1)}, u32[]{:S(2)}, u32[]{:S(2)}) collective-permute-start(f32[128,16]{0,1:T(8,128)S(1)} %add.218), channel_id=1, source_target_pairs={{0,2},{1,3},{2,0},{3,1},{4,6},{5,7},{6,4},{7,5},{8,10},{9,11},{10,... | collective-permute-start | bytes 24584 | tf_op jit(solution)/shard_map/ppermute | solution.py:42
  266.2 5.2 %collective-permute-start.25 = (f32[128,16]{0,1:T(8,128)S(1)}, f32[128,16]{0,1:T(8,128)S(1)}, u32[]{:S(2)}, u32[]{:S(2)}) collective-permute-start(f32[128,16]{0,1:T(8,128)S(1)} %add.221), channel_id=1, source_target_pairs={{0,2},{1,3},{2,0},{3,1},{4,6},{5,7},{6,4},{7,5},{8,10},{9,11},{10,... | collective-permute-start | bytes 24584 | tf_op jit(solution)/shard_map/ppermute | solution.py:42
Sparse Core Ops, SparseCore 0:
  22.9 58.1 all-gather.1

commit v4 on v3

--- a/solution.py
+++ b/solution.py
@@ -13,9 +13,22 @@
 
 def carried_both(forward, backward, axis):
     length, here = (lax.axis_size(axis), lax.axis_index(axis))
+    heads, width, size = forward[1].shape
+
+    def pack(x):
+        decay, state = x
+        lanes = jnp.broadcast_to(decay[:, None], (heads, 128))
+        return jnp.concatenate([state.reshape(heads, width * size), lanes], axis=1)
+
+    def unpack(p):
+        return (p[:, width * size], p[:, : width * size].reshape(heads, width, size))
+
+    def join(earlier, later):
+        return pack(blend_states(unpack(earlier), unpack(later)))
+
     identity = lambda x: (jnp.ones_like(x[0]), jnp.zeros_like(x[1]))
-    fwd_total, fwd_excl = forward, identity(forward)
-    bwd_total, bwd_excl = backward, identity(backward)
+    fwd_total, fwd_excl = pack(forward), pack(identity(forward))
+    bwd_total, bwd_excl = pack(backward), pack(identity(backward))
     shift = 1
     while shift < length:
         up = [(i, i + shift) for i in range(length - shift)]
@@ -24,14 +37,13 @@
         got_bwd = lax.ppermute(bwd_total, axis, down)
         has_fwd = here >= shift
         has_bwd = here + shift < length
-        pick = lambda ok, new, old: jax.tree.map(lambda a, b: jnp.where(ok, a, b), new, old)
-        fwd_excl = pick(has_fwd, blend_states(got_fwd, fwd_excl), fwd_excl)
-        bwd_excl = pick(has_bwd, blend_states(got_bwd, bwd_excl), bwd_excl)
+        fwd_excl = jnp.where(has_fwd, join(got_fwd, fwd_excl), fwd_excl)
+        bwd_excl = jnp.where(has_bwd, join(got_bwd, bwd_excl), bwd_excl)
         if shift * 2 < length:
-            fwd_total = pick(has_fwd, blend_states(got_fwd, fwd_total), fwd_total)
-            bwd_total = pick(has_bwd, blend_states(got_bwd, bwd_total), bwd_total)
+            fwd_total = jnp.where(has_fwd, join(got_fwd, fwd_total), fwd_total)
+            bwd_total = jnp.where(has_bwd, join(got_bwd, bwd_total), bwd_total)
         shift *= 2
-    return fwd_excl, bwd_excl
+    return unpack(fwd_excl), unpack(bwd_excl)
 
 
 def tp_sum(x, axis):
@@ -181,14 +193,14 @@
     )
     bwd_decay = bwd_decay[::-1]
     bwd_state = bwd_state[::-1]
+    return (fwd_decay, fwd_state, bwd_decay, bwd_state)
+
+
+def mixer_grads(mix_input, grad_mix, input_map, output_map, decay_log, carried):
+    fwd_decay, fwd_state, bwd_decay, bwd_state = carried
     (unused_a, state_in), (unused_b, pull_out) = carried_both(
         (fwd_decay[-1], fwd_state[-1]), (bwd_decay[0], bwd_state[0]), CTX
     )
-    return (state_in, pull_out, fwd_decay, fwd_state, bwd_decay, bwd_state)
-
-
-def mixer_grads(mix_input, grad_mix, input_map, output_map, decay_log, carried):
-    state_in, pull_out, fwd_decay, fwd_state, bwd_decay, bwd_state = carried
     local_rows, channels = mix_input.shape
     local_heads = decay_log.shape[1]
     head_width = channels // local_heads

time: 362 us -> 372 us (1.028)
  waiting for transfers between devices: 109 us -> 69.1 us
  starting transfers between devices: 169 us -> 198 us
  local copies, waits for them, and re-layouts: 18 us -> 30.8 us
  other arithmetic: 16.7 us -> 21.2 us
    all_to_all x1, waiting for transfers between devices: 77.8 us -> 0.01 us  [attention_grads(): parts = lax.all_to_all(parts, CTX, 0, 0, tiled=False)]
    all_gather x1, waiting for transfers between devices: 0.01 us -> 41 us  [attention_grads(): whole_kv = lax.all_gather(whole_kv, CTX[0], axis=0, tiled=True)]
    ppermute x11 -> x6, starting transfers between devices: 78.4 us -> 108 us  [carried_both(): got_fwd = lax.ppermute(fwd_total, axis, up)]
    ppermute x11 -> x6, waiting for transfers between devices: 20.8 us -> 8.75 us  [carried_both(): got_bwd = lax.ppermute(bwd_total, axis, down)]
    ppermute x11 -> x6, waiting for transfers between devices: 9.67 us -> 17.9 us  [carried_both(): got_fwd = lax.ppermute(fwd_total, axis, up)]
    ppermute x11 -> x6, starting transfers between devices: 14.2 us -> 7.75 us  [carried_both(): got_bwd = lax.ppermute(bwd_total, axis, down)]
    all_to_all x1, starting transfers between devices: 70.2 us -> 76.2 us  [attention_grads(): parts = lax.all_to_all(parts, CTX, 0, 0, tiled=False)]
  transfers between devices with their start and end apart: 28 -> 18, of which waited for: 9 -> 8; matrix products, arithmetic and copies ran while one was open for 7% -> 13% of each run, Pallas kernels for 0% -> 0%
where the time goes in v4:
time: 372 us; the launch traced here: 369 us
  starting transfers between devices  198 us (53%)
  waiting for transfers between devices  69.1 us (19%)
  local copies, waits for them, and re-layouts  30.8 us (8%)
  other arithmetic  21.2 us (6%)
  matrix products  20.2 us (5%)
  between operations  14.9 us (4%)
  blocking collectives  14.7 us (4%)
    ppermute x6, starting transfers between devices, carried_both(): got_fwd = lax.ppermute(fwd_total, axis, up)  108 us
    all_to_all x1, starting transfers between devices, attention_grads(): parts = lax.all_to_all(parts, CTX, 0, 0, tiled=False)  76.2 us
    all_gather x1, waiting for transfers between devices, attention_grads(): whole_kv = lax.all_gather(whole_kv, CTX[0], axis=0, tiled=True)  41 us
    ppermute x6, waiting for transfers between devices, carried_both(): got_fwd = lax.ppermute(fwd_total, axis, up)  17.9 us
    all_gather x1, blocking collectives, attention_grads(): whole_kv = lax.all_gather(whole_kv, CTX[1], axis=0, tiled=True)  14.7 us
    ppermute x6, waiting for transfers between devices, carried_both(): got_bwd = lax.ppermute(bwd_total, axis, down)  8.75 us
    ppermute x6, starting transfers between devices, carried_both(): got_bwd = lax.ppermute(bwd_total, axis, down)  7.75 us
  transfers between devices with their start and end apart: 18, of which 8 were waited for; matrix products, arithmetic and copies ran while one was open for 13% of the time, Pallas kernels for 0%

profile of v4, /device:TPU:2, one launch (start us, length us, event | category | flops | bytes accessed | tf_op | source)
XLA Modules:
  0.0 369.2 jit_solution(6718820588294583177)
XLA Ops:
  7.2 0.8 pad_maximum_fusion.4
  8.0 14.7 %all_gather.6 = bf16[1024,2,128]{2,0,1:T(8,128)(2,1)} all-gather(bf16[128,2,128]{2,0,1:T(8,128)(2,1)S(1)} %pad_maximum_fusion.4), channel_id=1, replica_groups=mesh['z'=8,'yc'=8,'tp'=4] {'yc'}, dimensions={0}, use_global_device_ids=true | all-gather | bytes 589824 | tf_op jit(solution)/shard_map/all_gather | solution.py:71
  22.8 0.8 copy.133
  23.6 1.3 copy.136
  25.2 1.3 copy.134
  26.5 1.4 multiply_reduce_fusion.2
  28.1 0.6 slice_bitcast_fusion.2
  29.0 3.3 convolution_bitcast_fusion.4
  32.3 3.3 convolution_bitcast_fusion.3
  35.9 0.8 copy_bitcast_fusion
  36.7 2.3 multiply_reduce_fusion
  39.0 41.0 %all-gather.2.cloned.1.call-done = bf16[8192,2,128]{2,0,1:T(8,128)(2,1)} async-done(((bf16[1024,2,128]{2,0,1:T(8,128)(2,1)}), bf16[8192,2,128]{2,0,1:T(8,128)(2,1)}) %all-gather.2.cloned.1.call-update) | async-done | bytes 4194320 | tf_op jit(solution)/shard_map/all_gather | solution.py:72
  80.0 3.9 %fusion.77 = (bf16[8192,1,128]{2,0,1:T(8,128)(2,1)}, bf16[8192,1,128]{2,0,1:T(8,128)(2,1)S(1)}) fusion(bf16[8192,2,128]{2,0,1:T(8,128)(2,1)} %all-gather.2.cloned.1.call-done), kind=kLoop, calls=%fused_computation.194 | loop fusion | bytes 8388608 | tf_op jit(solution)/shard_map/slice | solution.py:74
  83.9 1.9 while.26
  84.1 0.7 fusion.113
  84.9 0.9 exponential_reduce_fusion.2
  85.8 3.8 %broadcast_in_dim.252 = f32[8192,2,1,128]{3,0,2,1:T(8,128)} broadcast(f32[]{:T(128)} %constant.41.clone.1), dimensions={} | broadcast | bytes 8388612 | tf_op jit(solution)/shard_map/broadcast_in_dim | solution.py:144
  89.6 8.0 %while.27 = (s32[]{:T(128)}, f32[128,1,8,128]{0,3,2,1:T(8,128)S(1)}, f32[8192,2,1,128]{3,0,2,1:T(8,128)}, s32[]{:T(128)}, bf16[8192,1,128]{2,0,1:T(8,128)(2,1)S(...) while((s32[]{:T(128)}, ...), condition=%wide.region_7.8_spmd.clone, body=%wide.region_6.7_spmd.clone.sunk | while | flops 1354499200 | bytes 27415800 | solution.py:158
  89.6 0.7 fusion.124
  90.6 2.5 fusion.125
  93.5 1.0 fusion.127
  94.5 0.7 convolution_bitcast_fusion.6
  95.2 2.3 fusion.128
  97.6 1.2 copy.146
  99.0 0.7 broadcast_in_dim.258
  99.8 1.3 collective-permute-start
  101.0 1.2 copy.156
  102.5 0.7 broadcast_in_dim.282
  103.2 3.0 collective-permute-start.8
  106.3 5.9 %bitcast_convert_fusion = bf16[8192,2,1,128]{3,0,1,2:T(8,128)(2,1)} fusion(f32[8192,2,1,128]{3,0,2,1:T(8,128)} %get-tuple-element.126), kind=kLoop, calls=%fused_computation.49 | loop fusion | flops 2097152 | bytes 12582912 | tf_op jit(solution)/shard_map/convert_element_type | solution.py:161
  112.2 0.9 copy.140
  113.1 4.7 %copy.142 = bf16[64,128,2,1,128]{4,1,2,3,0:T(8,128)(2,1)} copy(bf16[64,128,2,1,128]{4,1,0,2,3:T(8,128)(2,1)} %bitcast.275) | data formatting | bytes 8388608 | tf_op jit(solution)/shard_map/convert_element_type | solution.py:161
  117.8 76.2 %all-to-all-start = ((bf16[64,128,2,1,128]{4,1,2,3,0:T(8,128)(2,1)}), bf16[64,128,2,1,128]{4,1,2,3,0:T(8,128)(2,1)}, u32[]{:S(2)}, u32[]{:S(2)}) async-start(bf16[64,128,2,1,128]{4,1,2,3,0:T(8,128)(2,1)} %copy.142), calls=%async_computation | async-start | bytes 8388608 | tf_op jit(solution)/shard_map/all_to_all | solution.py:162
  195.4 1.3 collective-permute-start.1
  196.7 0.9 slice.327
  198.2 4.6 %collective-permute-start.9 = (f32[32,1152]{1,0:T(8,128)S(1)}, f32[32,1152]{1,0:T(8,128)S(1)}, u32[]{:S(2)}, u32[]{:S(2)}) collective-permute-start(f32[32,1152]{1,0:T(8,128)S(1)} %maximum_select_fusion.11), channel_id=1, source_target_pairs={{0,8},{4,12},{8,16},{12,20},{16,24},{20,28},{24,32},{28,36},{32,40... | collective-permute-start | bytes 442376 | tf_op jit(solution)/shard_map/ppermute | solution.py:36
  202.9 8.1 %collective-permute-done.9 = f32[32,1152]{1,0:T(8,128)S(1)} collective-permute-done((f32[32,1152]{1,0:T(8,128)S(1)}, f32[32,1152]{1,0:T(8,128)S(1)}, u32[]{:S(2)}, u32[]{:S(2)}) %collective-permute-start.9) | collective-permute-done | bytes 147488 | tf_op jit(solution)/shard_map/ppermute | solution.py:36
  211.3 5.3 %collective-permute-start.10 = (f32[32,1152]{1,0:T(8,128)S(1)}, f32[32,1152]{1,0:T(8,128)S(1)}, u32[]{:S(2)}, u32[]{:S(2)}) collective-permute-start(f32[32,1152]{1,0:T(8,128)S(1)} %maximum_select_fusion.13), channel_id=1, source_target_pairs={{0,16},{4,20},{8,24},{12,28},{16,32},{20,36},{24,40},{28,44},{32,4... | collective-permute-start | bytes 442376 | tf_op jit(solution)/shard_map/ppermute | solution.py:36
  217.3 1.0 slice_add_fusion.14
  218.4 1.3 collective-permute-start.2
  219.9 7.4 %collective-permute-done.10 = f32[32,1152]{1,0:T(8,128)S(1)} collective-permute-done((f32[32,1152]{1,0:T(8,128)S(1)}, f32[32,1152]{1,0:T(8,128)S(1)}, u32[]{:S(2)}, u32[]{:S(2)}) %collective-permute-start.10) | collective-permute-done | bytes 147488 | tf_op jit(solution)/shard_map/ppermute | solution.py:36
  227.6 76.9 %collective-permute-start.11 = (f32[32,1152]{1,0:T(8,128)S(1)}, f32[32,1152]{1,0:T(8,128)S(1)}, u32[]{:S(2)}, u32[]{:S(2)}) collective-permute-start(f32[32,1152]{1,0:T(8,128)S(1)} %maximum_select_fusion.15), channel_id=1, source_target_pairs={{0,32},{4,36},{8,40},{12,44},{16,48},{20,52},{24,56},{28,60},{32,6... | collective-permute-start | bytes 442376 | tf_op jit(solution)/shard_map/ppermute | solution.py:36
  304.9 1.3 collective-permute-start.3
  306.4 0.8 collective-permute-done.11
  307.5 5.3 %collective-permute-start.12 = (f32[32,1152]{1,0:T(8,128)S(1)}, f32[32,1152]{1,0:T(8,128)S(1)}, u32[]{:S(2)}, u32[]{:S(2)}) collective-permute-start(f32[32,1152]{1,0:T(8,128)S(1)} %maximum_select_fusion.17), channel_id=1, source_target_pairs={{0,64},{4,68},{8,72},{12,76},{16,80},{20,84},{24,88},{28,92},{32,9... | collective-permute-start | bytes 442376 | tf_op jit(solution)/shard_map/ppermute | solution.py:36
  313.2 1.3 collective-permute-start.4
  314.7 0.8 collective-permute-done.12
  315.9 13.1 %collective-permute-start.13 = (f32[32,1152]{1,0:T(8,128)S(1)}, f32[32,1152]{1,0:T(8,128)S(1)}, u32[]{:S(2)}, u32[]{:S(2)}) collective-permute-start(f32[32,1152]{1,0:T(8,128)S(1)} %maximum_select_fusion.19), channel_id=1, source_target_pairs={{0,128},{4,132},{8,136},{12,140},{16,144},{20,148},{24,152},{28,15... | collective-permute-start | bytes 442376 | tf_op jit(solution)/shard_map/ppermute | solution.py:36
  329.4 1.3 collective-permute-start.5
  330.9 0.8 collective-permute-done.13
  331.8 8.7 %collective-permute-done.5 = f32[32,1152]{1,0:T(8,128)S(1)} collective-permute-done((f32[32,1152]{1,0:T(8,128)S(1)}, f32[32,1152]{1,0:T(8,128)S(1)}, u32[]{:S(2)}, u32[]{:S(2)}) %collective-permute-start.5) | collective-permute-done | bytes 147488 | tf_op jit(solution)/shard_map/ppermute | solution.py:37
  342.4 0.8 collective-permute-start.6
  344.4 1.5 collective-permute-start.14
  346.2 1.8 fusion.46
  348.1 1.8 fusion.50
  349.9 0.7 fusion.70
  351.0 2.1 collective-permute-start.7
  353.1 1.5 collective-permute-start.15
  354.6 1.0 copy.165
  355.6 0.7 copy.166
  356.3 0.6 add.229
  356.9 1.4 collective-permute-done.15
  358.9 2.9 reduce.14
  361.7 0.6 slice_bitcast_fusion
  (193 shorter events, 12.4 us)
Async XLA Ops:
  7.2 21.8 %copy-start.8 = (f32[128,16]{0,1:T(8,128)S(1)}, f32[128,16]{0,1:T(8,128)}, u32[]{:S(2)}) copy-start(f32[128,16]{0,1:T(8,128)} %param.21) | copy-start | bytes 24580
  7.2 72.8 %all-gather.2.cloned.1.call-start = ((), (), s32[]{:S(2)}) async-start(), calls=%async_computation.1 | async-start | bytes 4718592 | tf_op jit(solution)/shard_map/all_gather | solution.py:72
  22.7 9.5 %copy-start.20 = (f32[128,16]{0,1:T(8,128)S(1)}, f32[128,16]{0,1:T(8,128)}, u32[]{:S(2)}) copy-start(f32[128,16]{0,1:T(8,128)} %param.22) | copy-start | bytes 24580
  24.9 10.9 %copy-start.2 = (bf16[128,8,128]{2,1,0:T(8,128)(2,1)S(1)}, bf16[128,8,128]{2,1,0:T(8,128)(2,1)}, u32[]{:S(2)}) copy-start(bf16[128,8,128]{2,1,0:T(8,128)(2,1)} %param.18) | copy-start | bytes 786436
  24.9 10.9 %copy-start.6 = (bf16[128,8,128]{2,1,0:T(8,128)(2,1)S(1)}, bf16[128,8,128]{2,1,0:T(8,128)(2,1)}, u32[]{:S(2)}) copy-start(bf16[128,8,128]{2,1,0:T(8,128)(2,1)} %param.14) | copy-start | bytes 786436
  25.1 10.4 %copy-start.3 = (f32[1,128,32]{2,1,0:T(8,128)}, f32[1,128,32]{2,1,0:T(8,128)S(1)}, u32[]{:S(2)}) copy-start(f32[1,128,32]{2,1,0:T(8,128)S(1)} %reduce_window_sum.20) | copy-start | bytes 49156
  25.2 10.4 %copy-start.13 = (f32[1,128,32]{1,2,0:T(8,128)}, f32[1,128,32]{1,2,0:T(8,128)S(1)}, u32[]{:S(2)}) copy-start(f32[1,128,32]{1,2,0:T(8,128)S(1)} %copy.135) | copy-start | bytes 49156
  26.5 12.5 %copy-start = (bf16[128,2048]{0,1:T(8,128)(2,1)}, bf16[128,2048]{0,1:T(8,128)(2,1)S(1)}, u32[]{:S(2)}) copy-start(bf16[128,2048]{0,1:T(8,128)(2,1)S(1)} %copy.134) | copy-start | bytes 1572868
  28.1 10.9 %copy-start.24 = (f32[32,128]{1,0:T(8,128)}, f32[32,128]{1,0:T(8,128)S(1)}, u32[]{:S(2)}) copy-start(f32[32,128]{1,0:T(8,128)S(1)} %copy.143) | copy-start | bytes 49156
  28.8 6.7 %copy-start.10 = (f32[128,32]{0,1:T(8,128)}, f32[128,32]{0,1:T(8,128)S(1)}, u32[]{:S(2)}) copy-start(f32[128,32]{0,1:T(8,128)S(1)} %get-tuple-element.349) | copy-start | bytes 49156
  29.0 10.0 %copy-start.28 = (pred[128,128]{1,0:T(8,128)(4,1)}, pred[128,128]{1,0:T(8,128)(4,1)S(1)}, u32[]{:S(2)}) copy-start(pred[128,128]{1,0:T(8,128)(4,1)S(1)} %iota_compare_fusion) | copy-start | bytes 49156
  35.8 44.2 %copy-start.22 = (f32[128,128]{1,0:T(8,128)}, f32[128,128]{1,0:T(8,128)S(1)}, u32[]{:S(2)}) copy-start(f32[128,128]{1,0:T(8,128)S(1)} %fusion.78) | copy-start | bytes 196612
  89.6 0.9 copy-start.7
  99.7 2.7 copy-start.17
  99.8 94.3 %collective-permute-start = (f32[32,1152]{1,0:T(8,128)S(1)}, f32[32,1152]{1,0:T(8,128)S(1)}, u32[]{:S(2)}, u32[]{:S(2)}) collective-permute-start(f32[32,1152]{1,0:T(8,128)S(1)} %pad_maximum_fusion), channel_id=1, source_target_pairs={{4,0},{8,4},{12,8},{16,12},{20,16},{24,20},{28,24},{32,28},{36,32}... | collective-permute-start | bytes 442376 | tf_op jit(solution)/shard_map/ppermute | solution.py:37
  103.2 9.0 %copy-start.15 = (f32[32,128]{1,0:T(8,128)}, f32[32,128]{1,0:T(8,128)S(1)}, u32[]{:S(2)}) copy-start(f32[32,128]{1,0:T(8,128)S(1)} %broadcast_in_dim.282) | copy-start | bytes 49156
  103.2 90.9 %collective-permute-start.8 = (f32[32,1152]{1,0:T(8,128)S(1)}, f32[32,1152]{1,0:T(8,128)S(1)}, u32[]{:S(2)}, u32[]{:S(2)}) collective-permute-start(f32[32,1152]{1,0:T(8,128)S(1)} %pad_maximum_fusion.1), channel_id=1, source_target_pairs={{0,4},{4,8},{8,12},{12,16},{16,20},{20,24},{24,28},{28,32},{32,36}... | collective-permute-start | bytes 442376 | tf_op jit(solution)/shard_map/ppermute | solution.py:36
  117.8 76.4 %copy-start.30 = (f32[1,32]{1,0:T(1,128)S(1)}, f32[1,32]{1,0:T(1,128)}, u32[]{:S(2)}) copy-start(f32[1,32]{1,0:T(1,128)} %get-tuple-element.130) | copy-start | bytes 388
  117.8 77.5 %copy-start.18 = (f32[32,128]{1,0:T(8,128)S(1)}, f32[32,128]{1,0:T(8,128)}, u32[]{:S(2)}) copy-start(f32[32,128]{1,0:T(8,128)} %copy-done.17) | copy-start | bytes 49156
  117.8 241.0 %all-to-all-start = ((bf16[64,128,2,1,128]{4,1,2,3,0:T(8,128)(2,1)}), bf16[64,128,2,1,128]{4,1,2,3,0:T(8,128)(2,1)}, u32[]{:S(2)}, u32[]{:S(2)}) async-start(bf16[64,128,2,1,128]{4,1,2,3,0:T(8,128)(2,1)} %copy.142), calls=%async_computation | async-start | bytes 8388608 | tf_op jit(solution)/shard_map/all_to_all | solution.py:162
  194.1 4.1 %copy-start.16 = (f32[32,128]{1,0:T(8,128)S(1)}, f32[32,128]{1,0:T(8,128)}, u32[]{:S(2)}) copy-start(f32[32,128]{1,0:T(8,128)} %copy-done.15) | copy-start | bytes 49156
  194.1 8.8 %copy-start.4 = (f32[32,1152]{1,0:T(8,128)S(1)}, f32[32,1152]{1,0:T(8,128)}, u32[]{:S(2)}) copy-start(f32[32,1152]{1,0:T(8,128)} %constant.85.clone.1) | copy-start | bytes 442372
  194.2 0.7 copy-start.19
  195.4 21.2 %collective-permute-start.1 = (f32[32,1152]{1,0:T(8,128)S(1)}, f32[32,1152]{1,0:T(8,128)S(1)}, u32[]{:S(2)}, u32[]{:S(2)}) collective-permute-start(f32[32,1152]{1,0:T(8,128)S(1)} %maximum_select_fusion.1), channel_id=1, source_target_pairs={{8,0},{12,4},{16,8},{20,12},{24,16},{28,20},{32,24},{36,28},{40,32... | collective-permute-start | bytes 442376 | tf_op jit(solution)/shard_map/ppermute | solution.py:37
  198.2 12.8 %collective-permute-start.9 = (f32[32,1152]{1,0:T(8,128)S(1)}, f32[32,1152]{1,0:T(8,128)S(1)}, u32[]{:S(2)}, u32[]{:S(2)}) collective-permute-start(f32[32,1152]{1,0:T(8,128)S(1)} %maximum_select_fusion.11), channel_id=1, source_target_pairs={{0,8},{4,12},{8,16},{12,20},{16,24},{20,28},{24,32},{28,36},{32,40... | collective-permute-start | bytes 442376 | tf_op jit(solution)/shard_map/ppermute | solution.py:36
  211.3 15.9 %collective-permute-start.10 = (f32[32,1152]{1,0:T(8,128)S(1)}, f32[32,1152]{1,0:T(8,128)S(1)}, u32[]{:S(2)}, u32[]{:S(2)}) collective-permute-start(f32[32,1152]{1,0:T(8,128)S(1)} %maximum_select_fusion.13), channel_id=1, source_target_pairs={{0,16},{4,20},{8,24},{12,28},{16,32},{20,36},{24,40},{28,44},{32,4... | collective-permute-start | bytes 442376 | tf_op jit(solution)/shard_map/ppermute | solution.py:36
  216.6 0.7 copy-start.12
  218.4 86.2 %collective-permute-start.2 = (f32[32,1152]{1,0:T(8,128)S(1)}, f32[32,1152]{1,0:T(8,128)S(1)}, u32[]{:S(2)}, u32[]{:S(2)}) collective-permute-start(f32[32,1152]{1,0:T(8,128)S(1)} %maximum_select_fusion.3), channel_id=1, source_target_pairs={{16,0},{20,4},{24,8},{28,12},{32,16},{36,20},{40,24},{44,28},{48,3... | collective-permute-start | bytes 442376 | tf_op jit(solution)/shard_map/ppermute | solution.py:37
  227.6 79.6 %collective-permute-start.11 = (f32[32,1152]{1,0:T(8,128)S(1)}, f32[32,1152]{1,0:T(8,128)S(1)}, u32[]{:S(2)}, u32[]{:S(2)}) collective-permute-start(f32[32,1152]{1,0:T(8,128)S(1)} %maximum_select_fusion.15), channel_id=1, source_target_pairs={{0,32},{4,36},{8,40},{12,44},{16,48},{20,52},{24,56},{28,60},{32,6... | collective-permute-start | bytes 442376 | tf_op jit(solution)/shard_map/ppermute | solution.py:36
  304.9 7.9 %collective-permute-start.3 = (f32[32,1152]{1,0:T(8,128)S(1)}, f32[32,1152]{1,0:T(8,128)S(1)}, u32[]{:S(2)}, u32[]{:S(2)}) collective-permute-start(f32[32,1152]{1,0:T(8,128)S(1)} %maximum_select_fusion.5), channel_id=1, source_target_pairs={{32,0},{36,4},{40,8},{44,12},{48,16},{52,20},{56,24},{60,28},{64,3... | collective-permute-start | bytes 442376 | tf_op jit(solution)/shard_map/ppermute | solution.py:37
  307.5 8.0 %collective-permute-start.12 = (f32[32,1152]{1,0:T(8,128)S(1)}, f32[32,1152]{1,0:T(8,128)S(1)}, u32[]{:S(2)}, u32[]{:S(2)}) collective-permute-start(f32[32,1152]{1,0:T(8,128)S(1)} %maximum_select_fusion.17), channel_id=1, source_target_pairs={{0,64},{4,68},{8,72},{12,76},{16,80},{20,84},{24,88},{28,92},{32,9... | collective-permute-start | bytes 442376 | tf_op jit(solution)/shard_map/ppermute | solution.py:36
  313.0 28.7 %copy-start.1 = (bf16[128,2048]{0,1:T(8,128)(2,1)S(1)}, bf16[128,2048]{0,1:T(8,128)(2,1)}, u32[]{:S(2)}) copy-start(bf16[128,2048]{0,1:T(8,128)(2,1)} %copy-done) | copy-start | bytes 1572868
  313.2 15.8 %collective-permute-start.4 = (f32[32,1152]{1,0:T(8,128)S(1)}, f32[32,1152]{1,0:T(8,128)S(1)}, u32[]{:S(2)}, u32[]{:S(2)}) collective-permute-start(f32[32,1152]{1,0:T(8,128)S(1)} %maximum_select_fusion.7), channel_id=1, source_target_pairs={{64,0},{68,4},{72,8},{76,12},{80,16},{84,20},{88,24},{92,28},{96,3... | collective-permute-start | bytes 442376 | tf_op jit(solution)/shard_map/ppermute | solution.py:37
  314.6 27.7 %copy-start.5 = (f32[128,128]{1,0:T(8,128)S(1)}, f32[128,128]{1,0:T(8,128)}, u32[]{:S(2)}) copy-start(f32[128,128]{1,0:T(8,128)} %get-tuple-element.245) | copy-start | bytes 196612
  314.6 27.7 %copy-start.21 = (f32[128,16]{0,1:T(8,128)S(1)}, f32[128,16]{0,1:T(8,128)}, u32[]{:S(2)}) copy-start(f32[128,16]{0,1:T(8,128)} %param.22) | copy-start | bytes 24580
  315.8 27.9 %copy-start.11 = (f32[128,32]{0,1:T(8,128)S(1)}, f32[128,32]{0,1:T(8,128)}, u32[]{:S(2)}) copy-start(f32[128,32]{0,1:T(8,128)} %copy-done.10) | copy-start | bytes 49156
  315.9 15.8 %collective-permute-start.13 = (f32[32,1152]{1,0:T(8,128)S(1)}, f32[32,1152]{1,0:T(8,128)S(1)}, u32[]{:S(2)}, u32[]{:S(2)}) collective-permute-start(f32[32,1152]{1,0:T(8,128)S(1)} %maximum_select_fusion.19), channel_id=1, source_target_pairs={{0,128},{4,132},{8,136},{12,140},{16,144},{20,148},{24,152},{28,15... | collective-permute-start | bytes 442376 | tf_op jit(solution)/shard_map/ppermute | solution.py:36
  329.3 15.0 %copy-start.9 = (f32[128,16]{0,1:T(8,128)S(1)}, f32[128,16]{0,1:T(8,128)}, u32[]{:S(2)}) copy-start(f32[128,16]{0,1:T(8,128)} %param.21) | copy-start | bytes 24580
  329.4 11.1 %collective-permute-start.5 = (f32[32,1152]{1,0:T(8,128)S(1)}, f32[32,1152]{1,0:T(8,128)S(1)}, u32[]{:S(2)}, u32[]{:S(2)}) collective-permute-start(f32[32,1152]{1,0:T(8,128)S(1)} %maximum_select_fusion.9), channel_id=1, source_target_pairs={{128,0},{132,4},{136,8},{140,12},{144,16},{148,20},{152,24},{156,2... | collective-permute-start | bytes 442376 | tf_op jit(solution)/shard_map/ppermute | solution.py:37
  340.7 7.3 %copy-start.14 = (f32[1,128,32]{1,2,0:T(8,128)S(1)}, f32[1,128,32]{1,2,0:T(8,128)}, u32[]{:S(2)}) copy-start(f32[1,128,32]{1,2,0:T(8,128)} %copy-done.13) | copy-start | bytes 49156
  340.7 7.3 %copy-start.26 = (f32[32,128]{1,0:T(8,128)S(1)}, f32[32,128]{1,0:T(8,128)}, u32[]{:S(2)}) copy-start(f32[32,128]{1,0:T(8,128)} %get-tuple-element.243) | copy-start | bytes 49156
  340.8 7.3 %copy-start.27 = (f32[32,128]{1,0:T(8,128)S(1)}, f32[32,128]{1,0:T(8,128)}, u32[]{:S(2)}) copy-start(f32[32,128]{1,0:T(8,128)} %get-tuple-element.244) | copy-start | bytes 49156
  340.8 7.3 %copy-start.23 = (f32[128,128]{1,0:T(8,128)S(1)}, f32[128,128]{1,0:T(8,128)}, u32[]{:S(2)}) copy-start(f32[128,128]{1,0:T(8,128)} %copy-done.22) | copy-start | bytes 196612
  340.8 7.3 %copy-start.25 = (f32[32,128]{1,0:T(8,128)S(1)}, f32[32,128]{1,0:T(8,128)}, u32[]{:S(2)}) copy-start(f32[32,128]{1,0:T(8,128)} %copy-done.24) | copy-start | bytes 49156
  340.8 7.3 %copy-start.29 = (pred[128,128]{1,0:T(8,128)(4,1)S(1)}, pred[128,128]{1,0:T(8,128)(4,1)}, u32[]{:S(2)}) copy-start(pred[128,128]{1,0:T(8,128)(4,1)} %copy-done.28) | copy-start | bytes 49156
  342.4 8.5 %collective-permute-start.6 = (f32[128,16]{0,1:T(8,128)S(1)}, f32[128,16]{0,1:T(8,128)S(1)}, u32[]{:S(2)}, u32[]{:S(2)}) collective-permute-start(f32[128,16]{0,1:T(8,128)S(1)} %convolution_add_fusion.1), channel_id=1, source_target_pairs={{0,1},{1,0},{2,3},{3,2},{4,5},{5,4},{6,7},{7,6},{8,9},{9,8},{10,11... | collective-permute-start | bytes 24584 | tf_op jit(solution)/shard_map/ppermute | solution.py:54
  344.4 8.7 %collective-permute-start.14 = (f32[128,16]{0,1:T(8,128)S(1)}, f32[128,16]{0,1:T(8,128)S(1)}, u32[]{:S(2)}, u32[]{:S(2)}) collective-permute-start(f32[128,16]{0,1:T(8,128)S(1)} %convolution_add_fusion), channel_id=1, source_target_pairs={{0,1},{1,0},{2,3},{3,2},{4,5},{5,4},{6,7},{7,6},{8,9},{9,8},{10,11... | collective-permute-start | bytes 24584 | tf_op jit(solution)/shard_map/ppermute | solution.py:54
  351.0 5.3 %collective-permute-start.7 = (f32[128,16]{0,1:T(8,128)S(1)}, f32[128,16]{0,1:T(8,128)S(1)}, u32[]{:S(2)}, u32[]{:S(2)}) collective-permute-start(f32[128,16]{0,1:T(8,128)S(1)} %add.228), channel_id=1, source_target_pairs={{0,2},{1,3},{2,0},{3,1},{4,6},{5,7},{6,4},{7,5},{8,10},{9,11},{10,... | collective-permute-start | bytes 24584 | tf_op jit(solution)/shard_map/ppermute | solution.py:54
  353.1 5.2 %collective-permute-start.15 = (f32[128,16]{0,1:T(8,128)S(1)}, f32[128,16]{0,1:T(8,128)S(1)}, u32[]{:S(2)}, u32[]{:S(2)}) collective-permute-start(f32[128,16]{0,1:T(8,128)S(1)} %add.241), channel_id=1, source_target_pairs={{0,2},{1,3},{2,0},{3,1},{4,6},{5,7},{6,4},{7,5},{8,10},{9,11},{10,... | collective-permute-start | bytes 24584 | tf_op jit(solution)/shard_map/ppermute | solution.py:54
Sparse Core Ops, SparseCore 0:
  22.9 57.0 all-gather.1

commit v5 on v4

--- a/solution.py
+++ b/solution.py
@@ -193,14 +193,14 @@
     )
     bwd_decay = bwd_decay[::-1]
     bwd_state = bwd_state[::-1]
-    return (fwd_decay, fwd_state, bwd_decay, bwd_state)
-
-
-def mixer_grads(mix_input, grad_mix, input_map, output_map, decay_log, carried):
-    fwd_decay, fwd_state, bwd_decay, bwd_state = carried
     (unused_a, state_in), (unused_b, pull_out) = carried_both(
         (fwd_decay[-1], fwd_state[-1]), (bwd_decay[0], bwd_state[0]), CTX
     )
+    return (state_in, pull_out, fwd_decay, fwd_state, bwd_decay, bwd_state)
+
+
+def mixer_grads(mix_input, grad_mix, input_map, output_map, decay_log, carried):
+    state_in, pull_out, fwd_decay, fwd_state, bwd_decay, bwd_state = carried
     local_rows, channels = mix_input.shape
     local_heads = decay_log.shape[1]
     head_width = channels // local_heads

time: 372 us -> 330 us (0.89)
  starting transfers between devices: 198 us -> 135 us
  waiting for transfers between devices: 69.1 us -> 91.3 us
    all_to_all x1, waiting for transfers between devices: 0.01 us -> 77.3 us  [attention_grads(): parts = lax.all_to_all(parts, CTX, 0, 0, tiled=False)]
    ppermute x6, starting transfers between devices: 108 us -> 50.7 us  [carried_both(): got_fwd = lax.ppermute(fwd_total, axis, up)]
    all_gather x1, waiting for transfers between devices: 41 us -> 0.01 us  [attention_grads(): whole_kv = lax.all_gather(whole_kv, CTX[0], axis=0, tiled=True)]
    ppermute x6, waiting for transfers between devices: 17.9 us -> 4.77 us  [carried_both(): got_fwd = lax.ppermute(fwd_total, axis, up)]
    all_to_all x1, starting transfers between devices: 76.2 us -> 70.2 us  [attention_grads(): parts = lax.all_to_all(parts, CTX, 0, 0, tiled=False)]
    unnamed x69 -> x53, local copies, waits for them, and re-layouts: 6.13 us -> 8.7 us
where the time goes in v5:
time: 330 us; the launch traced here: 328 us
  starting transfers between devices  135 us (41%)
  waiting for transfers between devices  91.3 us (28%)
  local copies, waits for them, and re-layouts  29.4 us (9%)
  matrix products  21.6 us (7%)
  other arithmetic  21.2 us (6%)
  between operations  14.8 us (4%)
  blocking collectives  14.7 us (4%)
    all_to_all x1, waiting for transfers between devices, attention_grads(): parts = lax.all_to_all(parts, CTX, 0, 0, tiled=False)  77.3 us
    all_to_all x1, starting transfers between devices, attention_grads(): parts = lax.all_to_all(parts, CTX, 0, 0, tiled=False)  70.2 us
    ppermute x6, starting transfers between devices, carried_both(): got_fwd = lax.ppermute(fwd_total, axis, up)  50.7 us
    all_gather x1, blocking collectives, attention_grads(): whole_kv = lax.all_gather(whole_kv, CTX[1], axis=0, tiled=True)  14.7 us
    ppermute x6, waiting for transfers between devices, carried_both(): got_bwd = lax.ppermute(bwd_total, axis, down)  8.75 us
    unnamed x53, local copies, waits for them, and re-layouts  8.7 us
    ppermute x6, starting transfers between devices, carried_both(): got_bwd = lax.ppermute(bwd_total, axis, down)  7.93 us
  transfers between devices with their start and end apart: 18, of which 8 were waited for; matrix products, arithmetic and copies ran while one was open for 13% of the time, Pallas kernels for 0%

profile of v5, /device:TPU:2, one launch (start us, length us, event | category | flops | bytes accessed | tf_op | source)
XLA Modules:
  0.0 328.1 jit_solution(707926729329335877)
XLA Ops:
  7.2 0.8 pad_maximum_fusion.4
  8.0 14.7 %all_gather.6 = bf16[1024,2,128]{2,0,1:T(8,128)(2,1)} all-gather(bf16[128,2,128]{2,0,1:T(8,128)(2,1)S(1)} %pad_maximum_fusion.4), channel_id=1, replica_groups=mesh['z'=8,'yc'=8,'tp'=4] {'yc'}, dimensions={0}, use_global_device_ids=true | all-gather | bytes 589824 | tf_op jit(solution)/shard_map/all_gather | solution.py:71
  22.8 0.8 copy.135
  24.4 1.3 copy.144
  25.7 1.3 copy.134
  27.3 4.2 %fusion.53 = f32[32,64,16]{0,2,1:T(8,128)S(1)} fusion(f32[128,32,64]{0,2,1:T(8,128)S(1)} %bitcast.279, f32[128,16]{0,1:T(8,128)S(1)} %copy-done.19), kind=kOutput, calls=%fused_computation.66 | convolution fusion | flops 50331648 | bytes 1187840 | tf_op jit(solution)/shard_map/cshp,csn->chpn/dot_general | solution.py:187
  31.7 4.2 %fusion.55 = f32[32,64,16]{0,2,1:T(8,128)S(1)} fusion(f32[128,32,64]{0,2,1:T(8,128)S(1)} %bitcast.278, f32[128,16]{0,1:T(8,128)S(1)} %copy-done.12), kind=kOutput, calls=%fused_computation.68 | convolution fusion | flops 50331648 | bytes 1187840 | tf_op jit(solution)/shard_map/cshp,csn->chpn/dot_general | solution.py:186
  36.2 1.3 collective-permute-start.6
  37.5 3.0 collective-permute-start
  40.6 1.2 multiply_reduce_fusion.3
  41.9 0.7 copy.154
  42.6 1.8 copy_bitcast_fusion
  45.0 0.7 copy.196
  46.6 1.0 copy.195
  47.6 1.2 multiply_add_fusion
  49.2 0.7 fusion.76
  50.0 1.0 maximum_select_fusion.11
  51.0 1.3 collective-permute-start.7
  52.3 4.6 %collective-permute-start.1 = (f32[32,1152]{1,0:T(8,128)S(1)}, f32[32,1152]{1,0:T(8,128)S(1)}, u32[]{:S(2)}, u32[]{:S(2)}) collective-permute-start(f32[32,1152]{1,0:T(8,128)S(1)} %get-tuple-element.339), channel_id=1, source_target_pairs={{0,8},{4,12},{8,16},{12,20},{16,24},{20,28},{24,32},{28,36},{32,40... | collective-permute-start | bytes 442376 | tf_op jit(solution)/shard_map/ppermute | solution.py:36
  56.9 0.7 broadcast_in_dim.273
  57.6 0.7 broadcast_in_dim.251
  58.3 1.0 maximum_select_fusion.10
  59.3 1.4 collective-permute-done.1
  61.1 6.3 %collective-permute-start.2 = (f32[32,1152]{1,0:T(8,128)S(1)}, f32[32,1152]{1,0:T(8,128)S(1)}, u32[]{:S(2)}, u32[]{:S(2)}) collective-permute-start(f32[32,1152]{1,0:T(8,128)S(1)} %maximum_select_fusion.3), channel_id=1, source_target_pairs={{0,16},{4,20},{8,24},{12,28},{16,32},{20,36},{24,40},{28,44},{32,4... | collective-permute-start | bytes 442376 | tf_op jit(solution)/shard_map/ppermute | solution.py:36
  67.8 1.3 collective-permute-start.8
  69.3 1.7 collective-permute-done.2
  71.3 15.9 %collective-permute-start.3 = (f32[32,1152]{1,0:T(8,128)S(1)}, f32[32,1152]{1,0:T(8,128)S(1)}, u32[]{:S(2)}, u32[]{:S(2)}) collective-permute-start(f32[32,1152]{1,0:T(8,128)S(1)} %maximum_select_fusion.5), channel_id=1, source_target_pairs={{0,32},{4,36},{8,40},{12,44},{16,48},{20,52},{24,56},{28,60},{32,6... | collective-permute-start | bytes 442376 | tf_op jit(solution)/shard_map/ppermute | solution.py:36
  87.5 1.3 collective-permute-start.9
  89.0 0.8 collective-permute-done.3
  90.2 5.7 %collective-permute-start.4 = (f32[32,1152]{1,0:T(8,128)S(1)}, f32[32,1152]{1,0:T(8,128)S(1)}, u32[]{:S(2)}, u32[]{:S(2)}) collective-permute-start(f32[32,1152]{1,0:T(8,128)S(1)} %maximum_select_fusion.7), channel_id=1, source_target_pairs={{0,64},{4,68},{8,72},{12,76},{16,80},{20,84},{24,88},{28,92},{32,9... | collective-permute-start | bytes 442376 | tf_op jit(solution)/shard_map/ppermute | solution.py:36
  96.2 1.3 collective-permute-start.10
  97.7 0.8 collective-permute-done.4
  98.9 15.3 %collective-permute-start.5 = (f32[32,1152]{1,0:T(8,128)S(1)}, f32[32,1152]{1,0:T(8,128)S(1)}, u32[]{:S(2)}, u32[]{:S(2)}) collective-permute-start(f32[32,1152]{1,0:T(8,128)S(1)} %maximum_select_fusion.9), channel_id=1, source_target_pairs={{0,128},{4,132},{8,136},{12,140},{16,144},{20,148},{24,152},{28,15... | collective-permute-start | bytes 442376 | tf_op jit(solution)/shard_map/ppermute | solution.py:36
  114.1 0.7 collective-permute-done.10
  115.2 1.5 collective-permute-start.11
  117.2 1.0 copy.143
  118.2 8.0 %collective-permute-done.11 = f32[32,1152]{1,0:T(8,128)S(1)} collective-permute-done((f32[32,1152]{1,0:T(8,128)S(1)}, f32[32,1152]{1,0:T(8,128)S(1)}, u32[]{:S(2)}, u32[]{:S(2)}) %collective-permute-start.11) | collective-permute-done | bytes 147488 | tf_op jit(solution)/shard_map/ppermute | solution.py:37
  126.5 1.0 copy.151
  127.5 3.9 %fusion.79 = (bf16[8192,1,128]{2,0,1:T(8,128)(2,1)}, bf16[8192,1,128]{2,0,1:T(8,128)(2,1)S(1)}) fusion(bf16[8192,2,128]{2,0,1:T(8,128)(2,1)} %all-gather.2.cloned.1.call-done), kind=kLoop, calls=%fused_computation.196 | loop fusion | bytes 8388608 | tf_op jit(solution)/shard_map/slice | solution.py:74
  131.4 1.9 while.26
  131.7 0.7 fusion.113
  132.4 0.9 exponential_reduce_fusion.2
  133.4 3.8 %broadcast_in_dim.139 = f32[8192,2,1,128]{3,0,2,1:T(8,128)} broadcast(f32[]{:T(128)} %constant.19.clone.1), dimensions={} | broadcast | bytes 8388612 | tf_op jit(solution)/shard_map/broadcast_in_dim | solution.py:144
  137.1 8.0 %while.27 = (s32[]{:T(128)}, f32[128,1,8,128]{0,3,2,1:T(8,128)S(1)}, f32[8192,2,1,128]{3,0,2,1:T(8,128)}, s32[]{:T(128)}, bf16[8192,1,128]{2,0,1:T(8,128)(2,1)S(...) while((s32[]{:T(128)}, ...), condition=%wide.region_7.8_spmd.clone, body=%wide.region_6.7_spmd.clone.sunk | while | flops 1354499200 | bytes 27415800 | solution.py:158
  137.1 0.7 fusion.124
  138.1 2.5 fusion.125
  141.0 1.0 fusion.127
  142.1 0.7 convolution_bitcast_fusion.4
  142.8 2.3 fusion.128
  145.1 3.9 %bitcast_convert_fusion = bf16[8192,2,1,128]{3,0,1,2:T(8,128)(2,1)S(1)} fusion(f32[8192,2,1,128]{3,0,2,1:T(8,128)} %get-tuple-element.120), kind=kLoop, calls=%fused_computation.49 | loop fusion | flops 2097152 | bytes 12582912 | tf_op jit(solution)/shard_map/convert_element_type | solution.py:161
  149.0 2.3 copy.157
  151.3 70.2 %all-to-all-start = ((bf16[64,128,2,1,128]{4,1,2,3,0:T(8,128)(2,1)}), bf16[64,128,2,1,128]{4,1,2,3,0:T(8,128)(2,1)}, u32[]{:S(2)}, u32[]{:S(2)}) async-start(bf16[64,128,2,1,128]{4,1,2,3,0:T(8,128)(2,1)} %copy.157), calls=%async_computation | async-start | bytes 8388608 | tf_op jit(solution)/shard_map/all_to_all | solution.py:162
  222.0 1.7 multiply_reduce_fusion
  224.8 0.8 collective-permute-start.12
  226.5 1.5 collective-permute-start.14
  228.3 1.8 fusion.46
  230.3 1.8 fusion.50
  232.5 2.2 collective-permute-start.13
  234.7 1.4 collective-permute-start.15
  236.2 0.9 copy.155
  237.1 1.0 copy.166
  238.1 0.7 copy.167
  240.5 77.3 %all-to-all-done = bf16[64,128,2,1,128]{4,1,2,3,0:T(8,128)(2,1)} async-done(((bf16[64,128,2,1,128]{4,1,2,3,0:T(8,128)(2,1)}), bf16[64,128,2,1,128]{4,1,2,3,0:T(8,128)(2,1)}, u32[]{:S(2)}, u32[]{:S(2)}) %all-to-all-start) | async-done | bytes 4194336 | tf_op jit(solution)/shard_map/all_to_all | solution.py:162
  317.8 2.9 reduce.15
  (173 shorter events, 13.9 us)
Async XLA Ops:
  7.2 20.1 %copy-start.19 = (f32[128,16]{0,1:T(8,128)S(1)}, f32[128,16]{0,1:T(8,128)}, u32[]{:S(2)}) copy-start(f32[128,16]{0,1:T(8,128)} %param.22) | copy-start | bytes 24580
  7.2 120.4 %all-gather.2.cloned.1.call-start = ((), (), s32[]{:S(2)}) async-start(), calls=%async_computation.1 | async-start | bytes 4718592 | tf_op jit(solution)/shard_map/all_gather | solution.py:72
  22.7 9.0 %copy-start.12 = (f32[128,16]{0,1:T(8,128)S(1)}, f32[128,16]{0,1:T(8,128)}, u32[]{:S(2)}) copy-start(f32[128,16]{0,1:T(8,128)} %param.21) | copy-start | bytes 24580
  23.7 0.6 copy-start.8
  23.8 12.4 %copy-start.22 = (f32[32]{0:T(128)}, f32[32]{0:T(128)S(1)}, u32[]{:S(2)}) copy-start(f32[32]{0:T(128)S(1)} %fusion.78) | copy-start | bytes 388
  24.4 11.6 %copy-start.16 = (f32[1,128,32]{1,2,0:T(8,128)}, f32[1,128,32]{1,2,0:T(8,128)S(1)}, u32[]{:S(2)}) copy-start(f32[1,128,32]{1,2,0:T(8,128)S(1)} %copy.136) | copy-start | bytes 49156
  27.0 13.6 %copy-start = (bf16[128,2048]{0,1:T(8,128)(2,1)}, bf16[128,2048]{0,1:T(8,128)(2,1)S(1)}, u32[]{:S(2)}) copy-start(bf16[128,2048]{0,1:T(8,128)(2,1)S(1)} %copy.134) | copy-start | bytes 1572868
  27.1 14.8 %copy-start.14 = (f32[128,32]{0,1:T(8,128)}, f32[128,32]{0,1:T(8,128)S(1)}, u32[]{:S(2)}) copy-start(f32[128,32]{0,1:T(8,128)S(1)} %get-tuple-element.342) | copy-start | bytes 49156
  31.7 10.2 %copy-start.6 = (f32[32,1024]{1,0:T(8,128)}, f32[32,1024]{1,0:T(8,128)S(1)}, u32[]{:S(2)}) copy-start(f32[32,1024]{1,0:T(8,128)S(1)} %copy.146) | copy-start | bytes 393220
  36.1 5.8 %copy-start.7 = (f32[32,1024]{1,0:T(8,128)}, f32[32,1024]{1,0:T(8,128)S(1)}, u32[]{:S(2)}) copy-start(f32[32,1024]{1,0:T(8,128)S(1)} %copy.138) | copy-start | bytes 393220
  36.2 8.8 %copy-start.18 = (f32[32,128]{1,0:T(8,128)}, f32[32,128]{1,0:T(8,128)S(1)}, u32[]{:S(2)}) copy-start(f32[32,128]{1,0:T(8,128)S(1)} %broadcast_in_dim.140) | copy-start | bytes 49156
  36.2 8.2 %collective-permute-start.6 = (f32[32,1152]{1,0:T(8,128)S(1)}, f32[32,1152]{1,0:T(8,128)S(1)}, u32[]{:S(2)}, u32[]{:S(2)}) collective-permute-start(f32[32,1152]{1,0:T(8,128)S(1)} %get-tuple-element.340), channel_id=1, source_target_pairs={{4,0},{8,4},{12,8},{16,12},{20,16},{24,20},{28,24},{32,28},{36,32}... | collective-permute-start | bytes 442376 | tf_op jit(solution)/shard_map/ppermute | solution.py:37
  37.5 7.5 %collective-permute-start = (f32[32,1152]{1,0:T(8,128)S(1)}, f32[32,1152]{1,0:T(8,128)S(1)}, u32[]{:S(2)}, u32[]{:S(2)}) collective-permute-start(f32[32,1152]{1,0:T(8,128)S(1)} %get-tuple-element.341), channel_id=1, source_target_pairs={{0,4},{4,8},{8,12},{12,16},{16,20},{20,24},{24,28},{28,32},{32,36}... | collective-permute-start | bytes 442376 | tf_op jit(solution)/shard_map/ppermute | solution.py:36
  45.9 0.7 copy-start.4
  48.8 20.4 %copy-start.5 = (f32[32,1024]{1,0:T(8,128)S(1)}, f32[32,1024]{1,0:T(8,128)}, u32[]{:S(2)}) copy-start(f32[32,1024]{1,0:T(8,128)} %copy-done.4) | copy-start | bytes 393220
  48.8 20.4 %copy-start.10 = (f32[32,1152]{1,0:T(8,128)S(1)}, f32[32,1152]{1,0:T(8,128)}, u32[]{:S(2)}) copy-start(f32[32,1152]{1,0:T(8,128)} %constant.83.clone.1) | copy-start | bytes 442372
  51.0 16.4 %collective-permute-start.7 = (f32[32,1152]{1,0:T(8,128)S(1)}, f32[32,1152]{1,0:T(8,128)S(1)}, u32[]{:S(2)}, u32[]{:S(2)}) collective-permute-start(f32[32,1152]{1,0:T(8,128)S(1)} %get-tuple-element.338), channel_id=1, source_target_pairs={{8,0},{12,4},{16,8},{20,12},{24,16},{28,20},{32,24},{36,28},{40,32... | collective-permute-start | bytes 442376 | tf_op jit(solution)/shard_map/ppermute | solution.py:37
  52.3 8.4 %collective-permute-start.1 = (f32[32,1152]{1,0:T(8,128)S(1)}, f32[32,1152]{1,0:T(8,128)S(1)}, u32[]{:S(2)}, u32[]{:S(2)}) collective-permute-start(f32[32,1152]{1,0:T(8,128)S(1)} %get-tuple-element.339), channel_id=1, source_target_pairs={{0,8},{4,12},{8,16},{12,20},{16,24},{20,28},{24,32},{28,36},{32,40... | collective-permute-start | bytes 442376 | tf_op jit(solution)/shard_map/ppermute | solution.py:36
  61.1 9.9 %collective-permute-start.2 = (f32[32,1152]{1,0:T(8,128)S(1)}, f32[32,1152]{1,0:T(8,128)S(1)}, u32[]{:S(2)}, u32[]{:S(2)}) collective-permute-start(f32[32,1152]{1,0:T(8,128)S(1)} %maximum_select_fusion.3), channel_id=1, source_target_pairs={{0,16},{4,20},{8,24},{12,28},{16,32},{20,36},{24,40},{28,44},{32,4... | collective-permute-start | bytes 442376 | tf_op jit(solution)/shard_map/ppermute | solution.py:36
  67.8 19.4 %collective-permute-start.8 = (f32[32,1152]{1,0:T(8,128)S(1)}, f32[32,1152]{1,0:T(8,128)S(1)}, u32[]{:S(2)}, u32[]{:S(2)}) collective-permute-start(f32[32,1152]{1,0:T(8,128)S(1)} %maximum_select_fusion.13), channel_id=1, source_target_pairs={{16,0},{20,4},{24,8},{28,12},{32,16},{36,20},{40,24},{44,28},{48,3... | collective-permute-start | bytes 442376 | tf_op jit(solution)/shard_map/ppermute | solution.py:37
  71.3 18.5 %collective-permute-start.3 = (f32[32,1152]{1,0:T(8,128)S(1)}, f32[32,1152]{1,0:T(8,128)S(1)}, u32[]{:S(2)}, u32[]{:S(2)}) collective-permute-start(f32[32,1152]{1,0:T(8,128)S(1)} %maximum_select_fusion.5), channel_id=1, source_target_pairs={{0,32},{4,36},{8,40},{12,44},{16,48},{20,52},{24,56},{28,60},{32,6... | collective-permute-start | bytes 442376 | tf_op jit(solution)/shard_map/ppermute | solution.py:36
  87.5 8.4 %collective-permute-start.9 = (f32[32,1152]{1,0:T(8,128)S(1)}, f32[32,1152]{1,0:T(8,128)S(1)}, u32[]{:S(2)}, u32[]{:S(2)}) collective-permute-start(f32[32,1152]{1,0:T(8,128)S(1)} %maximum_select_fusion.15), channel_id=1, source_target_pairs={{32,0},{36,4},{40,8},{44,12},{48,16},{52,20},{56,24},{60,28},{64,3... | collective-permute-start | bytes 442376 | tf_op jit(solution)/shard_map/ppermute | solution.py:37
  90.2 8.4 %collective-permute-start.4 = (f32[32,1152]{1,0:T(8,128)S(1)}, f32[32,1152]{1,0:T(8,128)S(1)}, u32[]{:S(2)}, u32[]{:S(2)}) collective-permute-start(f32[32,1152]{1,0:T(8,128)S(1)} %maximum_select_fusion.7), channel_id=1, source_target_pairs={{0,64},{4,68},{8,72},{12,76},{16,80},{20,84},{24,88},{28,92},{32,9... | collective-permute-start | bytes 442376 | tf_op jit(solution)/shard_map/ppermute | solution.py:36
  96.2 18.6 %collective-permute-start.10 = (f32[32,1152]{1,0:T(8,128)S(1)}, f32[32,1152]{1,0:T(8,128)S(1)}, u32[]{:S(2)}, u32[]{:S(2)}) collective-permute-start(f32[32,1152]{1,0:T(8,128)S(1)} %maximum_select_fusion.17), channel_id=1, source_target_pairs={{64,0},{68,4},{72,8},{76,12},{80,16},{84,20},{88,24},{92,28},{96,3... | collective-permute-start | bytes 442376 | tf_op jit(solution)/shard_map/ppermute | solution.py:37
  98.9 18.0 %collective-permute-start.5 = (f32[32,1152]{1,0:T(8,128)S(1)}, f32[32,1152]{1,0:T(8,128)S(1)}, u32[]{:S(2)}, u32[]{:S(2)}) collective-permute-start(f32[32,1152]{1,0:T(8,128)S(1)} %maximum_select_fusion.9), channel_id=1, source_target_pairs={{0,128},{4,132},{8,136},{12,140},{16,144},{20,148},{24,152},{28,15... | collective-permute-start | bytes 442376 | tf_op jit(solution)/shard_map/ppermute | solution.py:36
  115.2 11.0 %collective-permute-start.11 = (f32[32,1152]{1,0:T(8,128)S(1)}, f32[32,1152]{1,0:T(8,128)S(1)}, u32[]{:S(2)}, u32[]{:S(2)}) collective-permute-start(f32[32,1152]{1,0:T(8,128)S(1)} %maximum_select_fusion.19), channel_id=1, source_target_pairs={{128,0},{132,4},{136,8},{140,12},{144,16},{148,20},{152,24},{156,2... | collective-permute-start | bytes 442376 | tf_op jit(solution)/shard_map/ppermute | solution.py:37
  133.4 3.8 %copy-start.21 = (f32[128,8]{0,1:T(8,128)S(1)}, f32[128,8]{0,1:T(8,128)}, u32[]{:S(2)}) copy-start(f32[128,8]{0,1:T(8,128)} %copy.154) | copy-start | bytes 12292
  137.1 1.0 copy-start.11
  151.3 70.3 %copy-start.9 = (f32[1,128,32]{2,1,0:T(8,128)S(1)}, f32[1,128,32]{2,1,0:T(8,128)}, u32[]{:S(2)}) copy-start(f32[1,128,32]{2,1,0:T(8,128)} %copy-done.8) | copy-start | bytes 49156
  151.3 70.4 %copy-start.13 = (f32[128,16]{0,1:T(8,128)S(1)}, f32[128,16]{0,1:T(8,128)}, u32[]{:S(2)}) copy-start(f32[128,16]{0,1:T(8,128)} %param.21) | copy-start | bytes 24580
  151.3 70.4 %copy-start.20 = (f32[128,16]{0,1:T(8,128)S(1)}, f32[128,16]{0,1:T(8,128)}, u32[]{:S(2)}) copy-start(f32[128,16]{0,1:T(8,128)} %param.22) | copy-start | bytes 24580
  151.3 70.7 %copy-start.1 = (bf16[128,2048]{0,1:T(8,128)(2,1)S(1)}, bf16[128,2048]{0,1:T(8,128)(2,1)}, u32[]{:S(2)}) copy-start(bf16[128,2048]{0,1:T(8,128)(2,1)} %copy-done) | copy-start | bytes 1572868
  151.3 166.5 %all-to-all-start = ((bf16[64,128,2,1,128]{4,1,2,3,0:T(8,128)(2,1)}), bf16[64,128,2,1,128]{4,1,2,3,0:T(8,128)(2,1)}, u32[]{:S(2)}, u32[]{:S(2)}) async-start(bf16[64,128,2,1,128]{4,1,2,3,0:T(8,128)(2,1)} %copy.157), calls=%async_computation | async-start | bytes 8388608 | tf_op jit(solution)/shard_map/all_to_all | solution.py:162
  221.5 2.2 copy-start.3
  221.5 4.0 %copy-start.2 = (f32[32,1024]{0,1:T(8,128)S(1)}, f32[32,1024]{0,1:T(8,128)}, u32[]{:S(2)}) copy-start(f32[32,1024]{0,1:T(8,128)} %copy.143) | copy-start | bytes 393220
  221.6 4.3 %copy-start.15 = (f32[128,32]{0,1:T(8,128)S(1)}, f32[128,32]{0,1:T(8,128)}, u32[]{:S(2)}) copy-start(f32[128,32]{0,1:T(8,128)} %copy-done.14) | copy-start | bytes 49156
  223.8 6.6 %copy-start.17 = (f32[1,128,32]{1,2,0:T(8,128)S(1)}, f32[1,128,32]{1,2,0:T(8,128)}, u32[]{:S(2)}) copy-start(f32[1,128,32]{1,2,0:T(8,128)} %copy-done.16) | copy-start | bytes 49156
  224.8 7.7 %collective-permute-start.12 = (f32[128,16]{0,1:T(8,128)S(1)}, f32[128,16]{0,1:T(8,128)S(1)}, u32[]{:S(2)}, u32[]{:S(2)}) collective-permute-start(f32[128,16]{0,1:T(8,128)S(1)} %convolution_add_fusion.1), channel_id=1, source_target_pairs={{0,1},{1,0},{2,3},{3,2},{4,5},{5,4},{6,7},{7,6},{8,9},{9,8},{10,11... | collective-permute-start | bytes 24584 | tf_op jit(solution)/shard_map/ppermute | solution.py:54
  226.5 8.2 %collective-permute-start.14 = (f32[128,16]{0,1:T(8,128)S(1)}, f32[128,16]{0,1:T(8,128)S(1)}, u32[]{:S(2)}, u32[]{:S(2)}) collective-permute-start(f32[128,16]{0,1:T(8,128)S(1)} %convolution_add_fusion), channel_id=1, source_target_pairs={{0,1},{1,0},{2,3},{3,2},{4,5},{5,4},{6,7},{7,6},{8,9},{9,8},{10,11... | collective-permute-start | bytes 24584 | tf_op jit(solution)/shard_map/ppermute | solution.py:54
  232.5 6.3 %collective-permute-start.13 = (f32[128,16]{0,1:T(8,128)S(1)}, f32[128,16]{0,1:T(8,128)S(1)}, u32[]{:S(2)}, u32[]{:S(2)}) collective-permute-start(f32[128,16]{0,1:T(8,128)S(1)} %add.238), channel_id=1, source_target_pairs={{0,2},{1,3},{2,0},{3,1},{4,6},{5,7},{6,4},{7,5},{8,10},{9,11},{10,... | collective-permute-start | bytes 24584 | tf_op jit(solution)/shard_map/ppermute | solution.py:54
  234.7 5.2 %collective-permute-start.15 = (f32[128,16]{0,1:T(8,128)S(1)}, f32[128,16]{0,1:T(8,128)S(1)}, u32[]{:S(2)}, u32[]{:S(2)}) collective-permute-start(f32[128,16]{0,1:T(8,128)S(1)} %add.241), channel_id=1, source_target_pairs={{0,2},{1,3},{2,0},{3,1},{4,6},{5,7},{6,4},{7,5},{8,10},{9,11},{10,... | collective-permute-start | bytes 24584 | tf_op jit(solution)/shard_map/ppermute | solution.py:54
Sparse Core Ops, SparseCore 0:
  22.9 60.0 all-gather.1

commit v6 on v5

--- a/solution.py
+++ b/solution.py
@@ -73,7 +73,7 @@
     whole_kv, carried = lax.optimization_barrier((whole_kv, carried))
     whole_keys, whole_values = (whole_kv[:, :local_groups], whole_kv[:, local_groups:])
     all_tokens = whole_keys.shape[0]
-    key_block = math.gcd(all_tokens, 1024)
+    key_block = math.gcd(all_tokens, 512)
     here = lax.axis_index(CTX)
 
     def scores_of(entry, first_row, length):

time: 330 us -> 354 us (1.073)
  starting transfers between devices: 135 us -> 165 us
    all_to_all x1, starting transfers between devices: 70.2 us -> 96.9 us  [attention_grads(): parts = lax.all_to_all(parts, CTX, 0, 0, tiled=False)]
    unnamed x53 -> x61, local copies, waits for them, and re-layouts: 8.7 us -> 6.83 us
  transfers between devices with their start and end apart: 18 -> 18, of which waited for: 8 -> 8; matrix products, arithmetic and copies ran while one was open for 13% -> 11% of each run, Pallas kernels for 0% -> 0%
where the time goes in v6:
time: 354 us; the launch traced here: 352 us
  starting transfers between devices  165 us (47%)
  waiting for transfers between devices  92.8 us (26%)
  local copies, waits for them, and re-layouts  26.6 us (8%)
  matrix products  19.8 us (6%)
  other arithmetic  18.3 us (5%)
  between operations  14.9 us (4%)
  blocking collectives  14.7 us (4%)
    all_to_all x1, starting transfers between devices, attention_grads(): parts = lax.all_to_all(parts, CTX, 0, 0, tiled=False)  96.9 us
    all_to_all x1, waiting for transfers between devices, attention_grads(): parts = lax.all_to_all(parts, CTX, 0, 0, tiled=False)  77.3 us
    ppermute x6, starting transfers between devices, carried_both(): got_fwd = lax.ppermute(fwd_total, axis, up)  54.2 us
    all_gather x1, blocking collectives, attention_grads(): whole_kv = lax.all_gather(whole_kv, CTX[1], axis=0, tiled=True)  14.7 us
    ppermute x6, waiting for transfers between devices, carried_both(): got_bwd = lax.ppermute(bwd_total, axis, down)  8.76 us
    ppermute x6, starting transfers between devices, carried_both(): got_bwd = lax.ppermute(bwd_total, axis, down)  7.93 us
  transfers between devices with their start and end apart: 18, of which 8 were waited for; matrix products, arithmetic and copies ran while one was open for 11% of the time, Pallas kernels for 0%

profile of v6, /device:TPU:2, one launch (start us, length us, event | category | flops | bytes accessed | tf_op | source)
XLA Modules:
  0.0 352.3 jit_solution(14480170557618189216)
XLA Ops:
  7.2 0.8 pad_maximum_fusion.4
  8.1 14.7 %all_gather.6 = bf16[1024,2,128]{2,0,1:T(8,128)(2,1)} all-gather(bf16[128,2,128]{2,0,1:T(8,128)(2,1)S(1)} %pad_maximum_fusion.4), channel_id=1, replica_groups=mesh['z'=8,'yc'=8,'tp'=4] {'yc'}, dimensions={0}, use_global_device_ids=true | all-gather | bytes 589824 | tf_op jit(solution)/shard_map/all_gather | solution.py:71
  22.8 0.8 copy.135
  23.8 0.6 fusion.69
  24.5 1.3 copy.144
  26.6 4.2 %fusion.44 = f32[32,64,16]{0,2,1:T(8,128)S(1)} fusion(f32[128,32,64]{0,2,1:T(8,128)S(1)} %bitcast.270, f32[128,16]{0,1:T(8,128)S(1)} %copy-done.22), kind=kOutput, calls=%fused_computation.61 | convolution fusion | flops 50331648 | bytes 1187840 | tf_op jit(solution)/shard_map/cshp,csn->chpn/dot_general | solution.py:187
  31.1 5.0 %fusion.46 = f32[32,64,16]{0,2,1:T(8,128)S(1)} fusion(f32[128,32,64]{0,2,1:T(8,128)S(1)} %bitcast.269, f32[128,16]{0,1:T(8,128)} %param.21), kind=kOutput, calls=%fused_computation.63 | convolution fusion | flops 50331648 | bytes 1187840 | tf_op jit(solution)/shard_map/cshp,csn->chpn/dot_general | solution.py:186
  36.3 0.7 broadcast_in_dim.140
  37.0 1.3 collective-permute-start.6
  38.3 3.0 collective-permute-start
  41.6 0.7 copy.154
  42.4 0.6 copy.198
  43.1 0.6 copy.196
  44.0 0.9 slice.294
  44.9 1.0 copy.195
  45.9 1.2 multiply_add_fusion
  47.5 0.7 fusion.67
  48.3 1.0 maximum_select_fusion.11
  49.3 1.3 collective-permute-start.7
  50.6 6.8 %collective-permute-start.1 = (f32[32,1152]{1,0:T(8,128)S(1)}, f32[32,1152]{1,0:T(8,128)S(1)}, u32[]{:S(2)}, u32[]{:S(2)}) collective-permute-start(f32[32,1152]{1,0:T(8,128)S(1)} %get-tuple-element.339), channel_id=1, source_target_pairs={{0,8},{4,12},{8,16},{12,20},{16,24},{20,28},{24,32},{28,36},{32,40... | collective-permute-start | bytes 442376 | tf_op jit(solution)/shard_map/ppermute | solution.py:36
  57.6 2.5 collective-permute-done.1
  60.4 6.4 %collective-permute-start.2 = (f32[32,1152]{1,0:T(8,128)S(1)}, f32[32,1152]{1,0:T(8,128)S(1)}, u32[]{:S(2)}, u32[]{:S(2)}) collective-permute-start(f32[32,1152]{1,0:T(8,128)S(1)} %maximum_select_fusion.3), channel_id=1, source_target_pairs={{0,16},{4,20},{8,24},{12,28},{16,32},{20,36},{24,40},{28,44},{32,4... | collective-permute-start | bytes 442376 | tf_op jit(solution)/shard_map/ppermute | solution.py:36
  67.2 1.3 collective-permute-start.8
  68.7 2.2 collective-permute-done.2
  71.2 16.6 %collective-permute-start.3 = (f32[32,1152]{1,0:T(8,128)S(1)}, f32[32,1152]{1,0:T(8,128)S(1)}, u32[]{:S(2)}, u32[]{:S(2)}) collective-permute-start(f32[32,1152]{1,0:T(8,128)S(1)} %maximum_select_fusion.5), channel_id=1, source_target_pairs={{0,32},{4,36},{8,40},{12,44},{16,48},{20,52},{24,56},{28,60},{32,6... | collective-permute-start | bytes 442376 | tf_op jit(solution)/shard_map/ppermute | solution.py:36
  88.2 1.3 collective-permute-start.9
  89.7 0.8 collective-permute-done.3
  90.8 6.0 %collective-permute-start.4 = (f32[32,1152]{1,0:T(8,128)S(1)}, f32[32,1152]{1,0:T(8,128)S(1)}, u32[]{:S(2)}, u32[]{:S(2)}) collective-permute-start(f32[32,1152]{1,0:T(8,128)S(1)} %maximum_select_fusion.7), channel_id=1, source_target_pairs={{0,64},{4,68},{8,72},{12,76},{16,80},{20,84},{24,88},{28,92},{32,9... | collective-permute-start | bytes 442376 | tf_op jit(solution)/shard_map/ppermute | solution.py:36
  97.2 1.3 collective-permute-start.10
  98.7 0.8 collective-permute-done.4
  99.9 15.3 %collective-permute-start.5 = (f32[32,1152]{1,0:T(8,128)S(1)}, f32[32,1152]{1,0:T(8,128)S(1)}, u32[]{:S(2)}, u32[]{:S(2)}) collective-permute-start(f32[32,1152]{1,0:T(8,128)S(1)} %maximum_select_fusion.9), channel_id=1, source_target_pairs={{0,128},{4,132},{8,136},{12,140},{16,144},{20,148},{24,152},{28,15... | collective-permute-start | bytes 442376 | tf_op jit(solution)/shard_map/ppermute | solution.py:36
  115.1 0.7 collective-permute-done.10
  116.1 1.5 collective-permute-start.11
  118.1 1.0 copy.143
  119.1 8.1 %collective-permute-done.11 = f32[32,1152]{1,0:T(8,128)S(1)} collective-permute-done((f32[32,1152]{1,0:T(8,128)S(1)}, f32[32,1152]{1,0:T(8,128)S(1)}, u32[]{:S(2)}, u32[]{:S(2)}) %collective-permute-start.11) | collective-permute-done | bytes 147488 | tf_op jit(solution)/shard_map/ppermute | solution.py:37
  127.5 1.0 copy.151
  128.5 3.9 %fusion.70 = (bf16[8192,1,128]{2,0,1:T(8,128)(2,1)}, bf16[8192,1,128]{2,0,1:T(8,128)(2,1)S(1)}) fusion(bf16[8192,2,128]{2,0,1:T(8,128)(2,1)} %all-gather.2.cloned.1.call-done), kind=kLoop, calls=%fused_computation.191 | loop fusion | bytes 8388608 | tf_op jit(solution)/shard_map/slice | solution.py:74
  132.4 1.1 while.26
  133.6 3.8 %broadcast_in_dim.139 = f32[8192,2,1,128]{3,0,2,1:T(8,128)} broadcast(f32[]{:T(128)} %constant.19.clone.1), dimensions={} | broadcast | bytes 8388612 | tf_op jit(solution)/shard_map/broadcast_in_dim | solution.py:144
  137.3 5.2 %while.27 = (s32[]{:T(128)}, f32[128,1,8,128]{0,3,2,1:T(8,128)S(1)}, f32[8192,2,1,128]{3,0,2,1:T(8,128)}, s32[]{:T(128)}, bf16[8192,1,128]{2,0,1:T(8,128)(2,1)S(...) while((s32[]{:T(128)}, ...), condition=%wide.region_7.8_spmd.clone, body=%wide.region_6.7_spmd.clone.sunk | while | flops 675742336 | bytes 14169307 | solution.py:158
  137.5 0.6 fusion.114
  138.1 1.4 fusion.115
  140.7 1.9 fusion.117
  142.6 3.9 %bitcast_convert_fusion = bf16[8192,2,1,128]{3,0,1,2:T(8,128)(2,1)S(1)} fusion(f32[8192,2,1,128]{3,0,2,1:T(8,128)} %get-tuple-element.120), kind=kLoop, calls=%fused_computation.44 | loop fusion | flops 2097152 | bytes 12582912 | tf_op jit(solution)/shard_map/convert_element_type | solution.py:161
  146.5 2.3 copy.157
  148.8 96.9 %all-to-all-start = ((bf16[64,128,2,1,128]{4,1,2,3,0:T(8,128)(2,1)}), bf16[64,128,2,1,128]{4,1,2,3,0:T(8,128)(2,1)}, u32[]{:S(2)}, u32[]{:S(2)}) async-start(bf16[64,128,2,1,128]{4,1,2,3,0:T(8,128)(2,1)} %copy.157), calls=%async_computation | async-start | bytes 8388608 | tf_op jit(solution)/shard_map/all_to_all | solution.py:162
  246.2 1.7 multiply_reduce_fusion
  248.3 0.5 multiply_reduce_fusion.7
  249.0 0.5 collective-permute-start.12
  249.8 0.5 multiply_reduce_fusion.6
  250.5 1.8 collective-permute-start.14
  252.5 1.8 fusion.37
  254.5 1.8 fusion.41
  256.7 2.2 collective-permute-start.13
  259.0 1.4 collective-permute-start.15
  260.4 0.9 copy.155
  261.3 1.0 copy.166
  262.3 0.7 copy.167
  263.0 0.6 add.239
  263.6 0.5 collective-permute-done.15
  264.1 0.6 add.242
  264.7 77.3 %all-to-all-done = bf16[64,128,2,1,128]{4,1,2,3,0:T(8,128)(2,1)} async-done(((bf16[64,128,2,1,128]{4,1,2,3,0:T(8,128)(2,1)}), bf16[64,128,2,1,128]{4,1,2,3,0:T(8,128)(2,1)}, u32[]{:S(2)}, u32[]{:S(2)}) %all-to-all-start) | async-done | bytes 4194336 | tf_op jit(solution)/shard_map/all_to_all | solution.py:162
  342.0 2.9 reduce.15
  344.8 0.6 slice_bitcast_fusion
  (179 shorter events, 11.2 us)
Async XLA Ops:
  7.2 18.6 %copy-start.11 = (bf16[128,2048]{1,0:T(8,128)(2,1)S(1)}, bf16[128,2048]{1,0:T(8,128)(2,1)}, u32[]{:S(2)}) copy-start(bf16[128,2048]{1,0:T(8,128)(2,1)} %param.19) | copy-start | bytes 1572868
  7.2 121.3 %all-gather.2.cloned.1.call-start = ((), (), s32[]{:S(2)}) async-start(), calls=%async_computation.1 | async-start | bytes 4718592 | tf_op jit(solution)/shard_map/all_gather | solution.py:72
  23.8 0.7 copy-start.8
  24.4 1.8 copy-start.18
  25.8 0.8 copy-start
  25.8 0.8 copy-start.22
  26.1 4.8 %copy-start.2 = (bf16[128,2048]{0,1:T(8,128)(2,1)}, bf16[128,2048]{0,1:T(8,128)(2,1)S(1)}, u32[]{:S(2)}) copy-start(bf16[128,2048]{0,1:T(8,128)(2,1)S(1)} %copy.134) | copy-start | bytes 1572868
  26.2 4.7 %copy-start.16 = (f32[128,32]{0,1:T(8,128)}, f32[128,32]{0,1:T(8,128)S(1)}, u32[]{:S(2)}) copy-start(f32[128,32]{0,1:T(8,128)S(1)} %get-tuple-element.342) | copy-start | bytes 49156
  30.9 10.5 %copy-start.7 = (bf16[128,8,128]{2,1,0:T(8,128)(2,1)S(1)}, bf16[128,8,128]{2,1,0:T(8,128)(2,1)}, u32[]{:S(2)}) copy-start(bf16[128,8,128]{2,1,0:T(8,128)(2,1)} %param.18) | copy-start | bytes 786436
  30.9 10.5 %copy-start.12 = (bf16[128,8,128]{2,1,0:T(8,128)(2,1)S(1)}, bf16[128,8,128]{2,1,0:T(8,128)(2,1)}, u32[]{:S(2)}) copy-start(bf16[128,8,128]{2,1,0:T(8,128)(2,1)} %param.17) | copy-start | bytes 786436
  30.9 11.4 %copy-start.13 = (bf16[128,8,128]{2,1,0:T(8,128)(2,1)S(1)}, bf16[128,8,128]{2,1,0:T(8,128)(2,1)}, u32[]{:S(2)}) copy-start(bf16[128,8,128]{2,1,0:T(8,128)(2,1)} %param.14) | copy-start | bytes 786436
  36.3 5.4 %copy-start.6 = (f32[32,1024]{1,0:T(8,128)}, f32[32,1024]{1,0:T(8,128)S(1)}, u32[]{:S(2)}) copy-start(f32[32,1024]{1,0:T(8,128)S(1)} %copy.138) | copy-start | bytes 393220
  37.0 4.4 %copy-start.20 = (f32[32,128]{1,0:T(8,128)}, f32[32,128]{1,0:T(8,128)S(1)}, u32[]{:S(2)}) copy-start(f32[32,128]{1,0:T(8,128)S(1)} %broadcast_in_dim.140) | copy-start | bytes 49156
  37.0 5.4 %collective-permute-start.6 = (f32[32,1152]{1,0:T(8,128)S(1)}, f32[32,1152]{1,0:T(8,128)S(1)}, u32[]{:S(2)}, u32[]{:S(2)}) collective-permute-start(f32[32,1152]{1,0:T(8,128)S(1)} %get-tuple-element.340), channel_id=1, source_target_pairs={{4,0},{8,4},{12,8},{16,12},{20,16},{24,20},{28,24},{32,28},{36,32}... | collective-permute-start | bytes 442376 | tf_op jit(solution)/shard_map/ppermute | solution.py:37
  38.3 4.8 %collective-permute-start = (f32[32,1152]{1,0:T(8,128)S(1)}, f32[32,1152]{1,0:T(8,128)S(1)}, u32[]{:S(2)}, u32[]{:S(2)}) collective-permute-start(f32[32,1152]{1,0:T(8,128)S(1)} %get-tuple-element.341), channel_id=1, source_target_pairs={{0,4},{4,8},{8,12},{12,16},{16,20},{20,24},{24,28},{28,32},{32,36}... | collective-permute-start | bytes 442376 | tf_op jit(solution)/shard_map/ppermute | solution.py:36
  43.1 0.7 copy-start.21
  47.1 10.3 %copy-start.24 = (f32[32,1]{0,1:T(1,128)S(1)}, f32[32,1]{0,1:T(1,128)}, u32[]{:S(2)}) copy-start(f32[32,1]{0,1:T(1,128)} %copy.198) | copy-start | bytes 388
  47.1 10.4 %copy-start.25 = (f32[32,1]{0,1:T(1,128)S(1)}, f32[32,1]{0,1:T(1,128)}, u32[]{:S(2)}) copy-start(f32[32,1]{0,1:T(1,128)} %copy.196) | copy-start | bytes 388
  47.1 10.4 %copy-start.10 = (f32[32,1152]{1,0:T(8,128)S(1)}, f32[32,1152]{1,0:T(8,128)}, u32[]{:S(2)}) copy-start(f32[32,1152]{1,0:T(8,128)} %constant.83.clone.1) | copy-start | bytes 442372
  49.3 17.6 %collective-permute-start.7 = (f32[32,1152]{1,0:T(8,128)S(1)}, f32[32,1152]{1,0:T(8,128)S(1)}, u32[]{:S(2)}, u32[]{:S(2)}) collective-permute-start(f32[32,1152]{1,0:T(8,128)S(1)} %get-tuple-element.338), channel_id=1, source_target_pairs={{8,0},{12,4},{16,8},{20,12},{24,16},{28,20},{32,24},{36,28},{40,32... | collective-permute-start | bytes 442376 | tf_op jit(solution)/shard_map/ppermute | solution.py:37
  50.6 9.5 %collective-permute-start.1 = (f32[32,1152]{1,0:T(8,128)S(1)}, f32[32,1152]{1,0:T(8,128)S(1)}, u32[]{:S(2)}, u32[]{:S(2)}) collective-permute-start(f32[32,1152]{1,0:T(8,128)S(1)} %get-tuple-element.339), channel_id=1, source_target_pairs={{0,8},{4,12},{8,16},{12,20},{16,24},{20,28},{24,32},{28,36},{32,40... | collective-permute-start | bytes 442376 | tf_op jit(solution)/shard_map/ppermute | solution.py:36
  60.4 10.5 %collective-permute-start.2 = (f32[32,1152]{1,0:T(8,128)S(1)}, f32[32,1152]{1,0:T(8,128)S(1)}, u32[]{:S(2)}, u32[]{:S(2)}) collective-permute-start(f32[32,1152]{1,0:T(8,128)S(1)} %maximum_select_fusion.3), channel_id=1, source_target_pairs={{0,16},{4,20},{8,24},{12,28},{16,32},{20,36},{24,40},{28,44},{32,4... | collective-permute-start | bytes 442376 | tf_op jit(solution)/shard_map/ppermute | solution.py:36
  67.2 20.6 %collective-permute-start.8 = (f32[32,1152]{1,0:T(8,128)S(1)}, f32[32,1152]{1,0:T(8,128)S(1)}, u32[]{:S(2)}, u32[]{:S(2)}) collective-permute-start(f32[32,1152]{1,0:T(8,128)S(1)} %maximum_select_fusion.13), channel_id=1, source_target_pairs={{16,0},{20,4},{24,8},{28,12},{32,16},{36,20},{40,24},{44,28},{48,3... | collective-permute-start | bytes 442376 | tf_op jit(solution)/shard_map/ppermute | solution.py:37
  71.2 19.2 %collective-permute-start.3 = (f32[32,1152]{1,0:T(8,128)S(1)}, f32[32,1152]{1,0:T(8,128)S(1)}, u32[]{:S(2)}, u32[]{:S(2)}) collective-permute-start(f32[32,1152]{1,0:T(8,128)S(1)} %maximum_select_fusion.5), channel_id=1, source_target_pairs={{0,32},{4,36},{8,40},{12,44},{16,48},{20,52},{24,56},{28,60},{32,6... | collective-permute-start | bytes 442376 | tf_op jit(solution)/shard_map/ppermute | solution.py:36
  88.2 8.7 %collective-permute-start.9 = (f32[32,1152]{1,0:T(8,128)S(1)}, f32[32,1152]{1,0:T(8,128)S(1)}, u32[]{:S(2)}, u32[]{:S(2)}) collective-permute-start(f32[32,1152]{1,0:T(8,128)S(1)} %maximum_select_fusion.15), channel_id=1, source_target_pairs={{32,0},{36,4},{40,8},{44,12},{48,16},{52,20},{56,24},{60,28},{64,3... | collective-permute-start | bytes 442376 | tf_op jit(solution)/shard_map/ppermute | solution.py:37
  90.8 8.7 %collective-permute-start.4 = (f32[32,1152]{1,0:T(8,128)S(1)}, f32[32,1152]{1,0:T(8,128)S(1)}, u32[]{:S(2)}, u32[]{:S(2)}) collective-permute-start(f32[32,1152]{1,0:T(8,128)S(1)} %maximum_select_fusion.7), channel_id=1, source_target_pairs={{0,64},{4,68},{8,72},{12,76},{16,80},{20,84},{24,88},{28,92},{32,9... | collective-permute-start | bytes 442376 | tf_op jit(solution)/shard_map/ppermute | solution.py:36
  97.2 18.6 %collective-permute-start.10 = (f32[32,1152]{1,0:T(8,128)S(1)}, f32[32,1152]{1,0:T(8,128)S(1)}, u32[]{:S(2)}, u32[]{:S(2)}) collective-permute-start(f32[32,1152]{1,0:T(8,128)S(1)} %maximum_select_fusion.17), channel_id=1, source_target_pairs={{64,0},{68,4},{72,8},{76,12},{80,16},{84,20},{88,24},{92,28},{96,3... | collective-permute-start | bytes 442376 | tf_op jit(solution)/shard_map/ppermute | solution.py:37
  99.9 18.0 %collective-permute-start.5 = (f32[32,1152]{1,0:T(8,128)S(1)}, f32[32,1152]{1,0:T(8,128)S(1)}, u32[]{:S(2)}, u32[]{:S(2)}) collective-permute-start(f32[32,1152]{1,0:T(8,128)S(1)} %maximum_select_fusion.9), channel_id=1, source_target_pairs={{0,128},{4,132},{8,136},{12,140},{16,144},{20,148},{24,152},{28,15... | collective-permute-start | bytes 442376 | tf_op jit(solution)/shard_map/ppermute | solution.py:36
  116.1 11.0 %collective-permute-start.11 = (f32[32,1152]{1,0:T(8,128)S(1)}, f32[32,1152]{1,0:T(8,128)S(1)}, u32[]{:S(2)}, u32[]{:S(2)}) collective-permute-start(f32[32,1152]{1,0:T(8,128)S(1)} %maximum_select_fusion.19), channel_id=1, source_target_pairs={{128,0},{132,4},{136,8},{140,12},{144,16},{148,20},{152,24},{156,2... | collective-permute-start | bytes 442376 | tf_op jit(solution)/shard_map/ppermute | solution.py:37
  133.6 3.8 %copy-start.15 = (f32[128,8]{0,1:T(8,128)S(1)}, f32[128,8]{0,1:T(8,128)}, u32[]{:S(2)}) copy-start(f32[128,8]{0,1:T(8,128)} %copy.154) | copy-start | bytes 12292
  148.8 97.0 %copy-start.9 = (f32[1,128,32]{2,1,0:T(8,128)S(1)}, f32[1,128,32]{2,1,0:T(8,128)}, u32[]{:S(2)}) copy-start(f32[1,128,32]{2,1,0:T(8,128)} %copy-done.8) | copy-start | bytes 49156
  148.8 97.1 %copy-start.14 = (f32[128,16]{0,1:T(8,128)S(1)}, f32[128,16]{0,1:T(8,128)}, u32[]{:S(2)}) copy-start(f32[128,16]{0,1:T(8,128)} %param.21) | copy-start | bytes 24580
  148.8 97.1 %copy-start.23 = (f32[128,16]{0,1:T(8,128)S(1)}, f32[128,16]{0,1:T(8,128)}, u32[]{:S(2)}) copy-start(f32[128,16]{0,1:T(8,128)} %param.22) | copy-start | bytes 24580
  148.8 97.4 %copy-start.1 = (bf16[128,2048]{0,1:T(8,128)(2,1)S(1)}, bf16[128,2048]{0,1:T(8,128)(2,1)}, u32[]{:S(2)}) copy-start(bf16[128,2048]{0,1:T(8,128)(2,1)} %copy-done) | copy-start | bytes 1572868
  148.8 97.4 %copy-start.3 = (bf16[128,2048]{0,1:T(8,128)(2,1)S(1)}, bf16[128,2048]{0,1:T(8,128)(2,1)}, u32[]{:S(2)}) copy-start(bf16[128,2048]{0,1:T(8,128)(2,1)} %copy-done.2) | copy-start | bytes 1572868
  148.8 193.2 %all-to-all-start = ((bf16[64,128,2,1,128]{4,1,2,3,0:T(8,128)(2,1)}), bf16[64,128,2,1,128]{4,1,2,3,0:T(8,128)(2,1)}, u32[]{:S(2)}, u32[]{:S(2)}) async-start(bf16[64,128,2,1,128]{4,1,2,3,0:T(8,128)(2,1)} %copy.157), calls=%async_computation | async-start | bytes 8388608 | tf_op jit(solution)/shard_map/all_to_all | solution.py:162
  246.2 1.8 copy-start.5
  248.0 1.6 copy-start.4
  248.0 1.9 copy-start.17
  249.0 7.8 %collective-permute-start.12 = (f32[128,16]{0,1:T(8,128)S(1)}, f32[128,16]{0,1:T(8,128)S(1)}, u32[]{:S(2)}, u32[]{:S(2)}) collective-permute-start(f32[128,16]{0,1:T(8,128)S(1)} %convolution_add_fusion.1), channel_id=1, source_target_pairs={{0,1},{1,0},{2,3},{3,2},{4,5},{5,4},{6,7},{7,6},{8,9},{9,8},{10,11... | collective-permute-start | bytes 24584 | tf_op jit(solution)/shard_map/ppermute | solution.py:54
  249.8 4.7 %copy-start.19 = (f32[1,128,32]{1,2,0:T(8,128)S(1)}, f32[1,128,32]{1,2,0:T(8,128)}, u32[]{:S(2)}) copy-start(f32[1,128,32]{1,2,0:T(8,128)} %copy-done.18) | copy-start | bytes 49156
  250.5 8.4 %collective-permute-start.14 = (f32[128,16]{0,1:T(8,128)S(1)}, f32[128,16]{0,1:T(8,128)S(1)}, u32[]{:S(2)}, u32[]{:S(2)}) collective-permute-start(f32[128,16]{0,1:T(8,128)S(1)} %convolution_add_fusion), channel_id=1, source_target_pairs={{0,1},{1,0},{2,3},{3,2},{4,5},{5,4},{6,7},{7,6},{8,9},{9,8},{10,11... | collective-permute-start | bytes 24584 | tf_op jit(solution)/shard_map/ppermute | solution.py:54
  256.7 6.3 %collective-permute-start.13 = (f32[128,16]{0,1:T(8,128)S(1)}, f32[128,16]{0,1:T(8,128)S(1)}, u32[]{:S(2)}, u32[]{:S(2)}) collective-permute-start(f32[128,16]{0,1:T(8,128)S(1)} %add.238), channel_id=1, source_target_pairs={{0,2},{1,3},{2,0},{3,1},{4,6},{5,7},{6,4},{7,5},{8,10},{9,11},{10,... | collective-permute-start | bytes 24584 | tf_op jit(solution)/shard_map/ppermute | solution.py:54
  259.0 5.2 %collective-permute-start.15 = (f32[128,16]{0,1:T(8,128)S(1)}, f32[128,16]{0,1:T(8,128)S(1)}, u32[]{:S(2)}, u32[]{:S(2)}) collective-permute-start(f32[128,16]{0,1:T(8,128)S(1)} %add.241), channel_id=1, source_target_pairs={{0,2},{1,3},{2,0},{3,1},{4,6},{5,7},{6,4},{7,5},{8,10},{9,11},{10,... | collective-permute-start | bytes 24584 | tf_op jit(solution)/shard_map/ppermute | solution.py:54
Sparse Core Ops, SparseCore 0:
  22.9 60.0 all-gather.1

commit v7 on v6

--- a/solution.py
+++ b/solution.py
@@ -73,7 +73,7 @@
     whole_kv, carried = lax.optimization_barrier((whole_kv, carried))
     whole_keys, whole_values = (whole_kv[:, :local_groups], whole_kv[:, local_groups:])
     all_tokens = whole_keys.shape[0]
-    key_block = math.gcd(all_tokens, 512)
+    key_block = math.gcd(all_tokens, 2048)
     here = lax.axis_index(CTX)
 
     def scores_of(entry, first_row, length):

time: 354 us -> 319 us (0.901)
  starting transfers between devices: 165 us -> 118 us
  matrix products: 19.8 us -> 26 us
  other arithmetic: 18.3 us -> 23.2 us
    all_to_all x1, starting transfers between devices: 96.9 us -> 53.4 us  [attention_grads(): parts = lax.all_to_all(parts, CTX, 0, 0, tiled=False)]
    unnamed x61 -> x53, local copies, waits for them, and re-layouts: 6.83 us -> 8.7 us
  transfers between devices with their start and end apart: 18 -> 18, of which waited for: 8 -> 8; matrix products, arithmetic and copies ran while one was open for 11% -> 14% of each run, Pallas kernels for 0% -> 0%
where the time goes in v7:
time: 319 us; the launch traced here: 318 us
  starting transfers between devices  118 us (37%)
  waiting for transfers between devices  91.6 us (29%)
  local copies, waits for them, and re-layouts  29.4 us (9%)
  matrix products  26 us (8%)
  other arithmetic  23.2 us (7%)
  between operations  14.8 us (5%)
  blocking collectives  14.7 us (5%)
    all_to_all x1, waiting for transfers between devices, attention_grads(): parts = lax.all_to_all(parts, CTX, 0, 0, tiled=False)  77.5 us
    all_to_all x1, starting transfers between devices, attention_grads(): parts = lax.all_to_all(parts, CTX, 0, 0, tiled=False)  53.4 us
    ppermute x6, starting transfers between devices, carried_both(): got_fwd = lax.ppermute(fwd_total, axis, up)  50.7 us
    all_gather x1, blocking collectives, attention_grads(): whole_kv = lax.all_gather(whole_kv, CTX[1], axis=0, tiled=True)  14.7 us
    ppermute x6, waiting for transfers between devices, carried_both(): got_bwd = lax.ppermute(bwd_total, axis, down)  8.75 us
    unnamed x53, local copies, waits for them, and re-layouts  8.7 us
    ppermute x6, starting transfers between devices, carried_both(): got_bwd = lax.ppermute(bwd_total, axis, down)  7.93 us
  transfers between devices with their start and end apart: 18, of which 8 were waited for; matrix products, arithmetic and copies ran while one was open for 14% of the time, Pallas kernels for 0%

profile of v7, /device:TPU:2, one launch (start us, length us, event | category | flops | bytes accessed | tf_op | source)
XLA Modules:
  0.0 317.7 jit_solution(8195225485530778293)
XLA Ops:
  7.2 0.8 pad_maximum_fusion.4
  8.0 14.7 %all_gather.6 = bf16[1024,2,128]{2,0,1:T(8,128)(2,1)} all-gather(bf16[128,2,128]{2,0,1:T(8,128)(2,1)S(1)} %pad_maximum_fusion.4), channel_id=1, replica_groups=mesh['z'=8,'yc'=8,'tp'=4] {'yc'}, dimensions={0}, use_global_device_ids=true | all-gather | bytes 589824 | tf_op jit(solution)/shard_map/all_gather | solution.py:71
  22.8 0.8 copy.135
  24.4 1.3 copy.144
  25.7 1.3 copy.134
  27.3 4.2 %fusion.53 = f32[32,64,16]{0,2,1:T(8,128)S(1)} fusion(f32[128,32,64]{0,2,1:T(8,128)S(1)} %bitcast.279, f32[128,16]{0,1:T(8,128)S(1)} %copy-done.19), kind=kOutput, calls=%fused_computation.66 | convolution fusion | flops 50331648 | bytes 1187840 | tf_op jit(solution)/shard_map/cshp,csn->chpn/dot_general | solution.py:187
  31.7 4.2 %fusion.55 = f32[32,64,16]{0,2,1:T(8,128)S(1)} fusion(f32[128,32,64]{0,2,1:T(8,128)S(1)} %bitcast.278, f32[128,16]{0,1:T(8,128)S(1)} %copy-done.12), kind=kOutput, calls=%fused_computation.68 | convolution fusion | flops 50331648 | bytes 1187840 | tf_op jit(solution)/shard_map/cshp,csn->chpn/dot_general | solution.py:186
  36.2 1.3 collective-permute-start.6
  37.5 3.0 collective-permute-start
  40.6 1.2 multiply_reduce_fusion.3
  41.9 0.7 copy.154
  42.6 1.8 copy_bitcast_fusion
  45.0 0.7 copy.196
  46.6 1.0 copy.195
  47.6 1.2 multiply_add_fusion
  49.2 0.7 fusion.76
  50.0 1.0 maximum_select_fusion.11
  51.0 1.3 collective-permute-start.7
  52.3 4.6 %collective-permute-start.1 = (f32[32,1152]{1,0:T(8,128)S(1)}, f32[32,1152]{1,0:T(8,128)S(1)}, u32[]{:S(2)}, u32[]{:S(2)}) collective-permute-start(f32[32,1152]{1,0:T(8,128)S(1)} %get-tuple-element.339), channel_id=1, source_target_pairs={{0,8},{4,12},{8,16},{12,20},{16,24},{20,28},{24,32},{28,36},{32,40... | collective-permute-start | bytes 442376 | tf_op jit(solution)/shard_map/ppermute | solution.py:36
  56.9 0.7 broadcast_in_dim.273
  57.6 0.7 broadcast_in_dim.251
  58.3 1.0 maximum_select_fusion.10
  59.3 1.4 collective-permute-done.1
  61.1 6.3 %collective-permute-start.2 = (f32[32,1152]{1,0:T(8,128)S(1)}, f32[32,1152]{1,0:T(8,128)S(1)}, u32[]{:S(2)}, u32[]{:S(2)}) collective-permute-start(f32[32,1152]{1,0:T(8,128)S(1)} %maximum_select_fusion.3), channel_id=1, source_target_pairs={{0,16},{4,20},{8,24},{12,28},{16,32},{20,36},{24,40},{28,44},{32,4... | collective-permute-start | bytes 442376 | tf_op jit(solution)/shard_map/ppermute | solution.py:36
  67.8 1.3 collective-permute-start.8
  69.3 1.7 collective-permute-done.2
  71.3 15.9 %collective-permute-start.3 = (f32[32,1152]{1,0:T(8,128)S(1)}, f32[32,1152]{1,0:T(8,128)S(1)}, u32[]{:S(2)}, u32[]{:S(2)}) collective-permute-start(f32[32,1152]{1,0:T(8,128)S(1)} %maximum_select_fusion.5), channel_id=1, source_target_pairs={{0,32},{4,36},{8,40},{12,44},{16,48},{20,52},{24,56},{28,60},{32,6... | collective-permute-start | bytes 442376 | tf_op jit(solution)/shard_map/ppermute | solution.py:36
  87.5 1.3 collective-permute-start.9
  89.0 0.8 collective-permute-done.3
  90.2 5.7 %collective-permute-start.4 = (f32[32,1152]{1,0:T(8,128)S(1)}, f32[32,1152]{1,0:T(8,128)S(1)}, u32[]{:S(2)}, u32[]{:S(2)}) collective-permute-start(f32[32,1152]{1,0:T(8,128)S(1)} %maximum_select_fusion.7), channel_id=1, source_target_pairs={{0,64},{4,68},{8,72},{12,76},{16,80},{20,84},{24,88},{28,92},{32,9... | collective-permute-start | bytes 442376 | tf_op jit(solution)/shard_map/ppermute | solution.py:36
  96.2 1.3 collective-permute-start.10
  97.7 0.8 collective-permute-done.4
  98.9 15.3 %collective-permute-start.5 = (f32[32,1152]{1,0:T(8,128)S(1)}, f32[32,1152]{1,0:T(8,128)S(1)}, u32[]{:S(2)}, u32[]{:S(2)}) collective-permute-start(f32[32,1152]{1,0:T(8,128)S(1)} %maximum_select_fusion.9), channel_id=1, source_target_pairs={{0,128},{4,132},{8,136},{12,140},{16,144},{20,148},{24,152},{28,15... | collective-permute-start | bytes 442376 | tf_op jit(solution)/shard_map/ppermute | solution.py:36
  114.1 0.7 collective-permute-done.10
  115.2 1.5 collective-permute-start.11
  117.2 1.0 copy.143
  118.2 8.0 %collective-permute-done.11 = f32[32,1152]{1,0:T(8,128)S(1)} collective-permute-done((f32[32,1152]{1,0:T(8,128)S(1)}, f32[32,1152]{1,0:T(8,128)S(1)}, u32[]{:S(2)}, u32[]{:S(2)}) %collective-permute-start.11) | collective-permute-done | bytes 147488 | tf_op jit(solution)/shard_map/ppermute | solution.py:37
  126.5 1.0 copy.151
  127.5 3.9 %fusion.79 = (bf16[8192,1,128]{2,0,1:T(8,128)(2,1)}, bf16[8192,1,128]{2,0,1:T(8,128)(2,1)S(1)}) fusion(bf16[8192,2,128]{2,0,1:T(8,128)(2,1)} %all-gather.2.cloned.1.call-done), kind=kLoop, calls=%fused_computation.196 | loop fusion | bytes 8388608 | tf_op jit(solution)/shard_map/slice | solution.py:74
  131.4 3.4 %while.26 = (s32[]{:T(128)}, f32[1,128,8]{1,2,0:T(8,128)S(1)}, f32[1,128,8]{1,2,0:T(8,128)S(1)}, s32[]{:T(128)}, bf16[8192,1,128]{2,0,1:T(8,128)(2,1)S(1)}, /*in...) while((s32[]{:T(128)}, f32[1,128,8]{1,2,0:T(8,128)S(1)}, ...), condition=%wide.region_4.5_spmd.clone, body=%wide.region_1.4_spmd.clone.sunk | while | flops 551817344 | bytes 18420912 | solution.py:114
  131.8 1.2 fusion.113
  133.1 1.7 exponential_reduce_fusion.2
  134.9 3.8 %broadcast_in_dim.139 = f32[8192,2,1,128]{3,0,2,1:T(8,128)} broadcast(f32[]{:T(128)} %constant.19.clone.1), dimensions={} | broadcast | bytes 8388612 | tf_op jit(solution)/shard_map/broadcast_in_dim | solution.py:144
  138.6 12.8 %while.27 = (s32[]{:T(128)}, f32[128,1,8,128]{0,3,2,1:T(8,128)S(1)}, f32[8192,2,1,128]{3,0,2,1:T(8,128)}, s32[]{:T(128)}, bf16[8192,1,128]{2,0,1:T(8,128)(2,1)S(...) while((s32[]{:T(128)}, ...), condition=%wide.region_7.8_spmd.clone, body=%wide.region_6.7_spmd.clone.sunk | while | flops 2708867072 | bytes 51672308 | solution.py:158
  138.6 1.2 fusion.124
  140.3 4.0 %fusion.125 = bf16[128,8,2048]{0,2,1:T(8,128)(2,1)S(1)} fusion(f32[2048,128,8]{1,0,2:T(8,128)S(1)} %fusion.124, f32[128,8]{0,1:T(8,128)S(1)} %get-tuple-element.542, f32[128,8]{0,1:T(8,128)S(1)} %bitcast.288, pred[128,2048]{0,1:T(8,128)(4,1)S(1)} %broadcast_compare_fusion.5, bf16[8192,1,128]{2,0,1:T(8,128)(2,1)} %get-tuple-element.540, ...), kind=kOutput, calls=%fused_computation.17.clone.1 | convolution fusion | flops 551550976 | bytes 13639684 | tf_op jit(solution)/shard_map/while/body/tgrd,kgd->gtrk/dot_general | solution.py:123
  144.3 0.8 fusion.126
  145.1 1.9 fusion.127
  147.0 1.3 convolution_bitcast_fusion.4
  148.3 3.2 fusion.128
  151.5 3.9 %bitcast_convert_fusion = bf16[8192,2,1,128]{3,0,1,2:T(8,128)(2,1)S(1)} fusion(f32[8192,2,1,128]{3,0,2,1:T(8,128)} %get-tuple-element.120), kind=kLoop, calls=%fused_computation.49 | loop fusion | flops 2097152 | bytes 12582912 | tf_op jit(solution)/shard_map/convert_element_type | solution.py:161
  155.4 2.3 copy.157
  157.7 53.4 %all-to-all-start = ((bf16[64,128,2,1,128]{4,1,2,3,0:T(8,128)(2,1)}), bf16[64,128,2,1,128]{4,1,2,3,0:T(8,128)(2,1)}, u32[]{:S(2)}, u32[]{:S(2)}) async-start(bf16[64,128,2,1,128]{4,1,2,3,0:T(8,128)(2,1)} %copy.157), calls=%async_computation | async-start | bytes 8388608 | tf_op jit(solution)/shard_map/all_to_all | solution.py:162
  211.6 1.7 multiply_reduce_fusion
  215.9 1.5 collective-permute-start.14
  217.7 1.8 fusion.46
  219.7 1.8 fusion.50
  221.9 2.2 collective-permute-start.13
  224.1 1.4 collective-permute-start.15
  225.5 0.9 copy.155
  226.4 1.0 copy.166
  227.4 0.7 copy.167
  229.8 77.5 %all-to-all-done = bf16[64,128,2,1,128]{4,1,2,3,0:T(8,128)(2,1)} async-done(((bf16[64,128,2,1,128]{4,1,2,3,0:T(8,128)(2,1)}), bf16[64,128,2,1,128]{4,1,2,3,0:T(8,128)(2,1)}, u32[]{:S(2)}, u32[]{:S(2)}) %all-to-all-start) | async-done | bytes 4194336 | tf_op jit(solution)/shard_map/all_to_all | solution.py:162
  307.3 2.9 reduce.15
  (173 shorter events, 14.2 us)
Async XLA Ops:
  7.2 20.1 %copy-start.19 = (f32[128,16]{0,1:T(8,128)S(1)}, f32[128,16]{0,1:T(8,128)}, u32[]{:S(2)}) copy-start(f32[128,16]{0,1:T(8,128)} %param.22) | copy-start | bytes 24580
  7.2 120.4 %all-gather.2.cloned.1.call-start = ((), (), s32[]{:S(2)}) async-start(), calls=%async_computation.1 | async-start | bytes 4718592 | tf_op jit(solution)/shard_map/all_gather | solution.py:72
  22.7 9.0 %copy-start.12 = (f32[128,16]{0,1:T(8,128)S(1)}, f32[128,16]{0,1:T(8,128)}, u32[]{:S(2)}) copy-start(f32[128,16]{0,1:T(8,128)} %param.21) | copy-start | bytes 24580
  23.7 0.6 copy-start.8
  23.8 12.4 %copy-start.22 = (f32[32]{0:T(128)}, f32[32]{0:T(128)S(1)}, u32[]{:S(2)}) copy-start(f32[32]{0:T(128)S(1)} %fusion.78) | copy-start | bytes 388
  24.4 11.6 %copy-start.16 = (f32[1,128,32]{1,2,0:T(8,128)}, f32[1,128,32]{1,2,0:T(8,128)S(1)}, u32[]{:S(2)}) copy-start(f32[1,128,32]{1,2,0:T(8,128)S(1)} %copy.136) | copy-start | bytes 49156
  27.0 13.6 %copy-start = (bf16[128,2048]{0,1:T(8,128)(2,1)}, bf16[128,2048]{0,1:T(8,128)(2,1)S(1)}, u32[]{:S(2)}) copy-start(bf16[128,2048]{0,1:T(8,128)(2,1)S(1)} %copy.134) | copy-start | bytes 1572868
  27.1 14.8 %copy-start.14 = (f32[128,32]{0,1:T(8,128)}, f32[128,32]{0,1:T(8,128)S(1)}, u32[]{:S(2)}) copy-start(f32[128,32]{0,1:T(8,128)S(1)} %get-tuple-element.342) | copy-start | bytes 49156
  31.7 10.2 %copy-start.6 = (f32[32,1024]{1,0:T(8,128)}, f32[32,1024]{1,0:T(8,128)S(1)}, u32[]{:S(2)}) copy-start(f32[32,1024]{1,0:T(8,128)S(1)} %copy.146) | copy-start | bytes 393220
  36.1 5.8 %copy-start.7 = (f32[32,1024]{1,0:T(8,128)}, f32[32,1024]{1,0:T(8,128)S(1)}, u32[]{:S(2)}) copy-start(f32[32,1024]{1,0:T(8,128)S(1)} %copy.138) | copy-start | bytes 393220
  36.2 8.8 %copy-start.18 = (f32[32,128]{1,0:T(8,128)}, f32[32,128]{1,0:T(8,128)S(1)}, u32[]{:S(2)}) copy-start(f32[32,128]{1,0:T(8,128)S(1)} %broadcast_in_dim.140) | copy-start | bytes 49156
  36.2 8.2 %collective-permute-start.6 = (f32[32,1152]{1,0:T(8,128)S(1)}, f32[32,1152]{1,0:T(8,128)S(1)}, u32[]{:S(2)}, u32[]{:S(2)}) collective-permute-start(f32[32,1152]{1,0:T(8,128)S(1)} %get-tuple-element.340), channel_id=1, source_target_pairs={{4,0},{8,4},{12,8},{16,12},{20,16},{24,20},{28,24},{32,28},{36,32}... | collective-permute-start | bytes 442376 | tf_op jit(solution)/shard_map/ppermute | solution.py:37
  37.5 7.5 %collective-permute-start = (f32[32,1152]{1,0:T(8,128)S(1)}, f32[32,1152]{1,0:T(8,128)S(1)}, u32[]{:S(2)}, u32[]{:S(2)}) collective-permute-start(f32[32,1152]{1,0:T(8,128)S(1)} %get-tuple-element.341), channel_id=1, source_target_pairs={{0,4},{4,8},{8,12},{12,16},{16,20},{20,24},{24,28},{28,32},{32,36}... | collective-permute-start | bytes 442376 | tf_op jit(solution)/shard_map/ppermute | solution.py:36
  45.9 0.7 copy-start.4
  48.8 20.4 %copy-start.5 = (f32[32,1024]{1,0:T(8,128)S(1)}, f32[32,1024]{1,0:T(8,128)}, u32[]{:S(2)}) copy-start(f32[32,1024]{1,0:T(8,128)} %copy-done.4) | copy-start | bytes 393220
  48.8 20.4 %copy-start.10 = (f32[32,1152]{1,0:T(8,128)S(1)}, f32[32,1152]{1,0:T(8,128)}, u32[]{:S(2)}) copy-start(f32[32,1152]{1,0:T(8,128)} %constant.83.clone.1) | copy-start | bytes 442372
  51.0 16.4 %collective-permute-start.7 = (f32[32,1152]{1,0:T(8,128)S(1)}, f32[32,1152]{1,0:T(8,128)S(1)}, u32[]{:S(2)}, u32[]{:S(2)}) collective-permute-start(f32[32,1152]{1,0:T(8,128)S(1)} %get-tuple-element.338), channel_id=1, source_target_pairs={{8,0},{12,4},{16,8},{20,12},{24,16},{28,20},{32,24},{36,28},{40,32... | collective-permute-start | bytes 442376 | tf_op jit(solution)/shard_map/ppermute | solution.py:37
  52.3 8.4 %collective-permute-start.1 = (f32[32,1152]{1,0:T(8,128)S(1)}, f32[32,1152]{1,0:T(8,128)S(1)}, u32[]{:S(2)}, u32[]{:S(2)}) collective-permute-start(f32[32,1152]{1,0:T(8,128)S(1)} %get-tuple-element.339), channel_id=1, source_target_pairs={{0,8},{4,12},{8,16},{12,20},{16,24},{20,28},{24,32},{28,36},{32,40... | collective-permute-start | bytes 442376 | tf_op jit(solution)/shard_map/ppermute | solution.py:36
  61.1 9.9 %collective-permute-start.2 = (f32[32,1152]{1,0:T(8,128)S(1)}, f32[32,1152]{1,0:T(8,128)S(1)}, u32[]{:S(2)}, u32[]{:S(2)}) collective-permute-start(f32[32,1152]{1,0:T(8,128)S(1)} %maximum_select_fusion.3), channel_id=1, source_target_pairs={{0,16},{4,20},{8,24},{12,28},{16,32},{20,36},{24,40},{28,44},{32,4... | collective-permute-start | bytes 442376 | tf_op jit(solution)/shard_map/ppermute | solution.py:36
  67.8 19.4 %collective-permute-start.8 = (f32[32,1152]{1,0:T(8,128)S(1)}, f32[32,1152]{1,0:T(8,128)S(1)}, u32[]{:S(2)}, u32[]{:S(2)}) collective-permute-start(f32[32,1152]{1,0:T(8,128)S(1)} %maximum_select_fusion.13), channel_id=1, source_target_pairs={{16,0},{20,4},{24,8},{28,12},{32,16},{36,20},{40,24},{44,28},{48,3... | collective-permute-start | bytes 442376 | tf_op jit(solution)/shard_map/ppermute | solution.py:37
  71.3 18.5 %collective-permute-start.3 = (f32[32,1152]{1,0:T(8,128)S(1)}, f32[32,1152]{1,0:T(8,128)S(1)}, u32[]{:S(2)}, u32[]{:S(2)}) collective-permute-start(f32[32,1152]{1,0:T(8,128)S(1)} %maximum_select_fusion.5), channel_id=1, source_target_pairs={{0,32},{4,36},{8,40},{12,44},{16,48},{20,52},{24,56},{28,60},{32,6... | collective-permute-start | bytes 442376 | tf_op jit(solution)/shard_map/ppermute | solution.py:36
  87.5 8.4 %collective-permute-start.9 = (f32[32,1152]{1,0:T(8,128)S(1)}, f32[32,1152]{1,0:T(8,128)S(1)}, u32[]{:S(2)}, u32[]{:S(2)}) collective-permute-start(f32[32,1152]{1,0:T(8,128)S(1)} %maximum_select_fusion.15), channel_id=1, source_target_pairs={{32,0},{36,4},{40,8},{44,12},{48,16},{52,20},{56,24},{60,28},{64,3... | collective-permute-start | bytes 442376 | tf_op jit(solution)/shard_map/ppermute | solution.py:37
  90.2 8.4 %collective-permute-start.4 = (f32[32,1152]{1,0:T(8,128)S(1)}, f32[32,1152]{1,0:T(8,128)S(1)}, u32[]{:S(2)}, u32[]{:S(2)}) collective-permute-start(f32[32,1152]{1,0:T(8,128)S(1)} %maximum_select_fusion.7), channel_id=1, source_target_pairs={{0,64},{4,68},{8,72},{12,76},{16,80},{20,84},{24,88},{28,92},{32,9... | collective-permute-start | bytes 442376 | tf_op jit(solution)/shard_map/ppermute | solution.py:36
  96.2 18.6 %collective-permute-start.10 = (f32[32,1152]{1,0:T(8,128)S(1)}, f32[32,1152]{1,0:T(8,128)S(1)}, u32[]{:S(2)}, u32[]{:S(2)}) collective-permute-start(f32[32,1152]{1,0:T(8,128)S(1)} %maximum_select_fusion.17), channel_id=1, source_target_pairs={{64,0},{68,4},{72,8},{76,12},{80,16},{84,20},{88,24},{92,28},{96,3... | collective-permute-start | bytes 442376 | tf_op jit(solution)/shard_map/ppermute | solution.py:37
  98.9 18.0 %collective-permute-start.5 = (f32[32,1152]{1,0:T(8,128)S(1)}, f32[32,1152]{1,0:T(8,128)S(1)}, u32[]{:S(2)}, u32[]{:S(2)}) collective-permute-start(f32[32,1152]{1,0:T(8,128)S(1)} %maximum_select_fusion.9), channel_id=1, source_target_pairs={{0,128},{4,132},{8,136},{12,140},{16,144},{20,148},{24,152},{28,15... | collective-permute-start | bytes 442376 | tf_op jit(solution)/shard_map/ppermute | solution.py:36
  115.2 11.0 %collective-permute-start.11 = (f32[32,1152]{1,0:T(8,128)S(1)}, f32[32,1152]{1,0:T(8,128)S(1)}, u32[]{:S(2)}, u32[]{:S(2)}) collective-permute-start(f32[32,1152]{1,0:T(8,128)S(1)} %maximum_select_fusion.19), channel_id=1, source_target_pairs={{128,0},{132,4},{136,8},{140,12},{144,16},{148,20},{152,24},{156,2... | collective-permute-start | bytes 442376 | tf_op jit(solution)/shard_map/ppermute | solution.py:37
  134.9 3.8 %copy-start.21 = (f32[128,8]{0,1:T(8,128)S(1)}, f32[128,8]{0,1:T(8,128)}, u32[]{:S(2)}) copy-start(f32[128,8]{0,1:T(8,128)} %copy.154) | copy-start | bytes 12292
  138.6 1.6 copy-start.11
  157.7 53.4 %copy-start.9 = (f32[1,128,32]{2,1,0:T(8,128)S(1)}, f32[1,128,32]{2,1,0:T(8,128)}, u32[]{:S(2)}) copy-start(f32[1,128,32]{2,1,0:T(8,128)} %copy-done.8) | copy-start | bytes 49156
  157.7 53.6 %copy-start.13 = (f32[128,16]{0,1:T(8,128)S(1)}, f32[128,16]{0,1:T(8,128)}, u32[]{:S(2)}) copy-start(f32[128,16]{0,1:T(8,128)} %param.21) | copy-start | bytes 24580
  157.7 53.6 %copy-start.20 = (f32[128,16]{0,1:T(8,128)S(1)}, f32[128,16]{0,1:T(8,128)}, u32[]{:S(2)}) copy-start(f32[128,16]{0,1:T(8,128)} %param.22) | copy-start | bytes 24580
  157.7 53.9 %copy-start.1 = (bf16[128,2048]{0,1:T(8,128)(2,1)S(1)}, bf16[128,2048]{0,1:T(8,128)(2,1)}, u32[]{:S(2)}) copy-start(bf16[128,2048]{0,1:T(8,128)(2,1)} %copy-done) | copy-start | bytes 1572868
  157.7 149.6 %all-to-all-start = ((bf16[64,128,2,1,128]{4,1,2,3,0:T(8,128)(2,1)}), bf16[64,128,2,1,128]{4,1,2,3,0:T(8,128)(2,1)}, u32[]{:S(2)}, u32[]{:S(2)}) async-start(bf16[64,128,2,1,128]{4,1,2,3,0:T(8,128)(2,1)} %copy.157), calls=%async_computation | async-start | bytes 8388608 | tf_op jit(solution)/shard_map/all_to_all | solution.py:162
  211.1 2.2 copy-start.3
  211.1 3.8 %copy-start.2 = (f32[32,1024]{0,1:T(8,128)S(1)}, f32[32,1024]{0,1:T(8,128)}, u32[]{:S(2)}) copy-start(f32[32,1024]{0,1:T(8,128)} %copy.143) | copy-start | bytes 393220
  211.1 4.1 %copy-start.15 = (f32[128,32]{0,1:T(8,128)S(1)}, f32[128,32]{0,1:T(8,128)}, u32[]{:S(2)}) copy-start(f32[128,32]{0,1:T(8,128)} %copy-done.14) | copy-start | bytes 49156
  213.3 6.3 %copy-start.17 = (f32[1,128,32]{1,2,0:T(8,128)S(1)}, f32[1,128,32]{1,2,0:T(8,128)}, u32[]{:S(2)}) copy-start(f32[1,128,32]{1,2,0:T(8,128)} %copy-done.16) | copy-start | bytes 49156
  214.3 7.5 %collective-permute-start.12 = (f32[128,16]{0,1:T(8,128)S(1)}, f32[128,16]{0,1:T(8,128)S(1)}, u32[]{:S(2)}, u32[]{:S(2)}) collective-permute-start(f32[128,16]{0,1:T(8,128)S(1)} %convolution_add_fusion.1), channel_id=1, source_target_pairs={{0,1},{1,0},{2,3},{3,2},{4,5},{5,4},{6,7},{7,6},{8,9},{9,8},{10,11... | collective-permute-start | bytes 24584 | tf_op jit(solution)/shard_map/ppermute | solution.py:54
  215.9 8.2 %collective-permute-start.14 = (f32[128,16]{0,1:T(8,128)S(1)}, f32[128,16]{0,1:T(8,128)S(1)}, u32[]{:S(2)}, u32[]{:S(2)}) collective-permute-start(f32[128,16]{0,1:T(8,128)S(1)} %convolution_add_fusion), channel_id=1, source_target_pairs={{0,1},{1,0},{2,3},{3,2},{4,5},{5,4},{6,7},{7,6},{8,9},{9,8},{10,11... | collective-permute-start | bytes 24584 | tf_op jit(solution)/shard_map/ppermute | solution.py:54
  221.9 6.3 %collective-permute-start.13 = (f32[128,16]{0,1:T(8,128)S(1)}, f32[128,16]{0,1:T(8,128)S(1)}, u32[]{:S(2)}, u32[]{:S(2)}) collective-permute-start(f32[128,16]{0,1:T(8,128)S(1)} %add.238), channel_id=1, source_target_pairs={{0,2},{1,3},{2,0},{3,1},{4,6},{5,7},{6,4},{7,5},{8,10},{9,11},{10,... | collective-permute-start | bytes 24584 | tf_op jit(solution)/shard_map/ppermute | solution.py:54
  224.1 5.2 %collective-permute-start.15 = (f32[128,16]{0,1:T(8,128)S(1)}, f32[128,16]{0,1:T(8,128)S(1)}, u32[]{:S(2)}, u32[]{:S(2)}) collective-permute-start(f32[128,16]{0,1:T(8,128)S(1)} %add.241), channel_id=1, source_target_pairs={{0,2},{1,3},{2,0},{3,1},{4,6},{5,7},{6,4},{7,5},{8,10},{9,11},{10,... | collective-permute-start | bytes 24584 | tf_op jit(solution)/shard_map/ppermute | solution.py:54
Sparse Core Ops, SparseCore 0:
  22.9 60.0 all-gather.1

commit v8 on v7

--- a/solution.py
+++ b/solution.py
@@ -68,8 +68,7 @@
     repeats = local_heads // local_groups
     score_scale = 1.0 / math.sqrt(head_width)
     whole_kv = jnp.concatenate([key_vectors, value_vectors], axis=1)
-    whole_kv = lax.all_gather(whole_kv, CTX[1], axis=0, tiled=True)
-    whole_kv = lax.all_gather(whole_kv, CTX[0], axis=0, tiled=True)
+    whole_kv = lax.all_gather(whole_kv, CTX, axis=0, tiled=True)
     whole_kv, carried = lax.optimization_barrier((whole_kv, carried))
     whole_keys, whole_values = (whole_kv[:, :local_groups], whole_kv[:, local_groups:])
     all_tokens = whole_keys.shape[0]

time: 319 us -> 305 us (0.956)
  blocking collectives: 14.7 us -> 0 us
  starting transfers between devices: 118 us -> 114 us
  waiting for transfers between devices: 91.6 us -> 95.2 us
    all_gather x1 -> x0, blocking collectives: 14.7 us -> none  [attention_grads(): whole_kv = lax.all_gather(whole_kv, CTX[1], axis=0, tiled=True)]
    ppermute x6, waiting for transfers between devices: 4.77 us -> 9.15 us  [carried_both(): got_fwd = lax.ppermute(fwd_total, axis, up)]
where the time goes in v8:
time: 305 us; the launch traced here: 304 us
  starting transfers between devices  114 us (37%)
  waiting for transfers between devices  95.2 us (31%)
  local copies, waits for them, and re-layouts  29.4 us (10%)
  matrix products  26 us (9%)
  other arithmetic  23.8 us (8%)
  between operations  14.8 us (5%)
    all_to_all x1, waiting for transfers between devices, attention_grads(): parts = lax.all_to_all(parts, CTX, 0, 0, tiled=False)  77.5 us
    all_to_all x1, starting transfers between devices, attention_grads(): parts = lax.all_to_all(parts, CTX, 0, 0, tiled=False)  51.6 us
    ppermute x6, starting transfers between devices, carried_both(): got_fwd = lax.ppermute(fwd_total, axis, up)  49.1 us
    ppermute x6, waiting for transfers between devices, carried_both(): got_fwd = lax.ppermute(fwd_total, axis, up)  9.15 us
    unnamed x53, local copies, waits for them, and re-layouts  8.7 us
    ppermute x6, waiting for transfers between devices, carried_both(): got_bwd = lax.ppermute(bwd_total, axis, down)  7.97 us
    ppermute x6, starting transfers between devices, carried_both(): got_bwd = lax.ppermute(bwd_total, axis, down)  7.75 us
  transfers between devices with their start and end apart: 18, of which 8 were waited for; matrix products, arithmetic and copies ran while one was open for 14% of the time, Pallas kernels for 0%

profile of v8, /device:TPU:2, one launch (start us, length us, event | category | flops | bytes accessed | tf_op | source)
XLA Modules:
  0.0 303.5 jit_solution(3793082422875667276)
XLA Ops:
  7.2 1.4 pad_maximum_fusion.4
  8.7 0.8 copy.135
  10.3 1.3 copy.144
  11.6 1.3 copy.134
  13.2 4.2 %fusion.53 = f32[32,64,16]{0,2,1:T(8,128)S(1)} fusion(f32[128,32,64]{0,2,1:T(8,128)S(1)} %bitcast.279, f32[128,16]{0,1:T(8,128)S(1)} %copy-done.19), kind=kOutput, calls=%fused_computation.66 | convolution fusion | flops 50331648 | bytes 1187840 | tf_op jit(solution)/shard_map/cshp,csn->chpn/dot_general | solution.py:186
  17.6 4.2 %fusion.55 = f32[32,64,16]{0,2,1:T(8,128)S(1)} fusion(f32[128,32,64]{0,2,1:T(8,128)S(1)} %bitcast.278, f32[128,16]{0,1:T(8,128)S(1)} %copy-done.12), kind=kOutput, calls=%fused_computation.68 | convolution fusion | flops 50331648 | bytes 1187840 | tf_op jit(solution)/shard_map/cshp,csn->chpn/dot_general | solution.py:185
  22.1 1.3 collective-permute-start.6
  23.4 3.0 %collective-permute-start = (f32[32,1152]{1,0:T(8,128)S(1)}, f32[32,1152]{1,0:T(8,128)S(1)}, u32[]{:S(2)}, u32[]{:S(2)}) collective-permute-start(f32[32,1152]{1,0:T(8,128)S(1)} %get-tuple-element.341), channel_id=1, source_target_pairs={{0,4},{4,8},{8,12},{12,16},{16,20},{20,24},{24,28},{28,32},{32,36}... | collective-permute-start | bytes 442376 | tf_op jit(solution)/shard_map/ppermute | solution.py:36
  26.5 1.3 multiply_reduce_fusion.3
  27.8 0.7 copy.154
  28.5 1.8 copy_bitcast_fusion
  30.9 0.7 copy.196
  32.5 1.0 copy.195
  33.5 1.2 multiply_add_fusion
  35.1 0.7 fusion.76
  35.9 1.0 maximum_select_fusion.11
  36.9 1.3 collective-permute-start.7
  38.2 4.6 %collective-permute-start.1 = (f32[32,1152]{1,0:T(8,128)S(1)}, f32[32,1152]{1,0:T(8,128)S(1)}, u32[]{:S(2)}, u32[]{:S(2)}) collective-permute-start(f32[32,1152]{1,0:T(8,128)S(1)} %get-tuple-element.339), channel_id=1, source_target_pairs={{0,8},{4,12},{8,16},{12,20},{16,24},{20,28},{24,32},{28,36},{32,40... | collective-permute-start | bytes 442376 | tf_op jit(solution)/shard_map/ppermute | solution.py:36
  42.8 0.7 broadcast_in_dim.273
  43.5 0.7 broadcast_in_dim.251
  44.2 1.0 maximum_select_fusion.10
  45.2 1.7 collective-permute-done.1
  47.3 6.0 %collective-permute-start.2 = (f32[32,1152]{1,0:T(8,128)S(1)}, f32[32,1152]{1,0:T(8,128)S(1)}, u32[]{:S(2)}, u32[]{:S(2)}) collective-permute-start(f32[32,1152]{1,0:T(8,128)S(1)} %maximum_select_fusion.3), channel_id=1, source_target_pairs={{0,16},{4,20},{8,24},{12,28},{16,32},{20,36},{24,40},{28,44},{32,4... | collective-permute-start | bytes 442376 | tf_op jit(solution)/shard_map/ppermute | solution.py:36
  53.6 1.3 collective-permute-start.8
  55.1 1.6 collective-permute-done.2
  57.0 11.0 %collective-permute-start.3 = (f32[32,1152]{1,0:T(8,128)S(1)}, f32[32,1152]{1,0:T(8,128)S(1)}, u32[]{:S(2)}, u32[]{:S(2)}) collective-permute-start(f32[32,1152]{1,0:T(8,128)S(1)} %maximum_select_fusion.5), channel_id=1, source_target_pairs={{0,32},{4,36},{8,40},{12,44},{16,48},{20,52},{24,56},{28,60},{32,6... | collective-permute-start | bytes 442376 | tf_op jit(solution)/shard_map/ppermute | solution.py:36
  68.4 1.3 collective-permute-start.9
  69.9 2.7 collective-permute-done.3
  72.9 5.9 %collective-permute-start.4 = (f32[32,1152]{1,0:T(8,128)S(1)}, f32[32,1152]{1,0:T(8,128)S(1)}, u32[]{:S(2)}, u32[]{:S(2)}) collective-permute-start(f32[32,1152]{1,0:T(8,128)S(1)} %maximum_select_fusion.7), channel_id=1, source_target_pairs={{0,64},{4,68},{8,72},{12,76},{16,80},{20,84},{24,88},{28,92},{32,9... | collective-permute-start | bytes 442376 | tf_op jit(solution)/shard_map/ppermute | solution.py:36
  79.1 1.3 collective-permute-start.10
  80.6 2.2 collective-permute-done.4
  83.1 18.6 %collective-permute-start.5 = (f32[32,1152]{1,0:T(8,128)S(1)}, f32[32,1152]{1,0:T(8,128)S(1)}, u32[]{:S(2)}, u32[]{:S(2)}) collective-permute-start(f32[32,1152]{1,0:T(8,128)S(1)} %maximum_select_fusion.9), channel_id=1, source_target_pairs={{0,128},{4,132},{8,136},{12,140},{16,144},{20,148},{24,152},{28,15... | collective-permute-start | bytes 442376 | tf_op jit(solution)/shard_map/ppermute | solution.py:36
  102.1 1.3 collective-permute-start.11
  103.6 1.0 collective-permute-done.5
  104.9 1.0 copy.143
  105.9 8.0 %collective-permute-done.11 = f32[32,1152]{1,0:T(8,128)S(1)} collective-permute-done((f32[32,1152]{1,0:T(8,128)S(1)}, f32[32,1152]{1,0:T(8,128)S(1)}, u32[]{:S(2)}, u32[]{:S(2)}) %collective-permute-start.11) | collective-permute-done | bytes 147488 | tf_op jit(solution)/shard_map/ppermute | solution.py:37
  114.2 1.0 copy.151
  115.2 3.9 %fusion.79 = (bf16[8192,1,128]{2,0,1:T(8,128)(2,1)}, bf16[8192,1,128]{2,0,1:T(8,128)(2,1)S(1)}) fusion(bf16[8192,2,128]{2,0,1:T(8,128)(2,1)} %all-gather.2.cloned.1.call-done), kind=kLoop, calls=%fused_computation.196 | loop fusion | bytes 8388608 | tf_op jit(solution)/shard_map/slice | solution.py:73
  119.1 3.4 %while.26 = (s32[]{:T(128)}, f32[1,128,8]{1,2,0:T(8,128)S(1)}, f32[1,128,8]{1,2,0:T(8,128)S(1)}, s32[]{:T(128)}, bf16[8192,1,128]{2,0,1:T(8,128)(2,1)S(1)}, /*in...) while((s32[]{:T(128)}, f32[1,128,8]{1,2,0:T(8,128)S(1)}, ...), condition=%wide.region_4.5_spmd.clone, body=%wide.region_1.4_spmd.clone.sunk | while | flops 551817344 | bytes 18420912 | solution.py:113
  119.5 1.2 fusion.113
  120.7 1.7 exponential_reduce_fusion.2
  122.6 3.8 %broadcast_in_dim.139 = f32[8192,2,1,128]{3,0,2,1:T(8,128)} broadcast(f32[]{:T(128)} %constant.19.clone.1), dimensions={} | broadcast | bytes 8388612 | tf_op jit(solution)/shard_map/broadcast_in_dim | solution.py:143
  126.3 12.8 %while.27 = (s32[]{:T(128)}, f32[128,1,8,128]{0,3,2,1:T(8,128)S(1)}, f32[8192,2,1,128]{3,0,2,1:T(8,128)}, s32[]{:T(128)}, bf16[8192,1,128]{2,0,1:T(8,128)(2,1)S(...) while((s32[]{:T(128)}, ...), condition=%wide.region_7.8_spmd.clone, body=%wide.region_6.7_spmd.clone.sunk | while | flops 2708867072 | bytes 51672308 | solution.py:157
  126.3 1.2 fusion.124
  128.0 4.0 %fusion.125 = bf16[128,8,2048]{0,2,1:T(8,128)(2,1)S(1)} fusion(f32[2048,128,8]{1,0,2:T(8,128)S(1)} %fusion.124, f32[128,8]{0,1:T(8,128)S(1)} %get-tuple-element.542, f32[128,8]{0,1:T(8,128)S(1)} %bitcast.288, pred[128,2048]{0,1:T(8,128)(4,1)S(1)} %broadcast_compare_fusion.5, bf16[8192,1,128]{2,0,1:T(8,128)(2,1)} %get-tuple-element.540, ...), kind=kOutput, calls=%fused_computation.17.clone.1 | convolution fusion | flops 551550976 | bytes 13639684 | tf_op jit(solution)/shard_map/while/body/tgrd,kgd->gtrk/dot_general | solution.py:122
  132.0 0.8 fusion.126
  132.8 1.9 fusion.127
  134.7 1.3 convolution_bitcast_fusion.4
  136.0 3.2 %fusion.128 = f32[8192,2,1,128]{3,0,2,1:T(8,128)} fusion(f32[8192,2,1,128]{3,0,2,1:T(8,128)} %get-tuple-element.520, s32[]{:T(128)S(6)} %select_n.278, f32[2048,1,1,128]{3,0,2,1:T(8,128)S(1)} %fusion.127, f32[2048,1,1,128]{3,0,2,1:T(8,128)S(1)} %convolution_bitcast_fusion.4), kind=kLoop, calls=%fused_computation.27.clone.1 | loop fusion | flops 1048576 | bytes 6291460 | tf_op jit(solution)/shard_map/while/body/dynamic_update_slice | solution.py:153
  139.2 3.9 %bitcast_convert_fusion = bf16[8192,2,1,128]{3,0,1,2:T(8,128)(2,1)S(1)} fusion(f32[8192,2,1,128]{3,0,2,1:T(8,128)} %get-tuple-element.120), kind=kLoop, calls=%fused_computation.49 | loop fusion | flops 2097152 | bytes 12582912 | tf_op jit(solution)/shard_map/convert_element_type | solution.py:160
  143.1 2.3 copy.157
  145.4 51.6 %all-to-all-start = ((bf16[64,128,2,1,128]{4,1,2,3,0:T(8,128)(2,1)}), bf16[64,128,2,1,128]{4,1,2,3,0:T(8,128)(2,1)}, u32[]{:S(2)}, u32[]{:S(2)}) async-start(bf16[64,128,2,1,128]{4,1,2,3,0:T(8,128)(2,1)} %copy.157), calls=%async_computation | async-start | bytes 8388608 | tf_op jit(solution)/shard_map/all_to_all | solution.py:161
  197.4 1.7 multiply_reduce_fusion
  200.2 0.7 collective-permute-start.12
  201.9 1.4 collective-permute-start.14
  203.5 1.8 fusion.46
  205.5 1.8 fusion.50
  207.7 2.2 collective-permute-start.13
  209.9 1.5 collective-permute-start.15
  211.4 0.9 copy.155
  212.3 1.0 copy.166
  213.3 0.7 copy.167
  215.6 77.5 %all-to-all-done = bf16[64,128,2,1,128]{4,1,2,3,0:T(8,128)(2,1)} async-done(((bf16[64,128,2,1,128]{4,1,2,3,0:T(8,128)(2,1)}), bf16[64,128,2,1,128]{4,1,2,3,0:T(8,128)(2,1)}, u32[]{:S(2)}, u32[]{:S(2)}) %all-to-all-start) | async-done | bytes 4194336 | tf_op jit(solution)/shard_map/all_to_all | solution.py:161
  293.2 2.9 reduce.15
  (172 shorter events, 13.7 us)
Async XLA Ops:
  7.2 6.0 %copy-start.19 = (f32[128,16]{0,1:T(8,128)S(1)}, f32[128,16]{0,1:T(8,128)}, u32[]{:S(2)}) copy-start(f32[128,16]{0,1:T(8,128)} %param.22) | copy-start | bytes 24580
  7.2 10.4 %copy-start.12 = (f32[128,16]{0,1:T(8,128)S(1)}, f32[128,16]{0,1:T(8,128)}, u32[]{:S(2)}) copy-start(f32[128,16]{0,1:T(8,128)} %param.21) | copy-start | bytes 24580
  7.2 108.0 %all-gather.2.cloned.1.call-start = ((), (), s32[]{:S(2)}) async-start(), calls=%async_computation.1 | async-start | bytes 4259840 | tf_op jit(solution)/shard_map/all_gather | solution.py:71
  9.6 0.6 copy-start.8
  9.7 12.4 %copy-start.22 = (f32[32]{0:T(128)}, f32[32]{0:T(128)S(1)}, u32[]{:S(2)}) copy-start(f32[32]{0:T(128)S(1)} %fusion.78) | copy-start | bytes 388
  10.3 11.6 %copy-start.16 = (f32[1,128,32]{1,2,0:T(8,128)}, f32[1,128,32]{1,2,0:T(8,128)S(1)}, u32[]{:S(2)}) copy-start(f32[1,128,32]{1,2,0:T(8,128)S(1)} %copy.136) | copy-start | bytes 49156
  12.9 13.6 %copy-start = (bf16[128,2048]{0,1:T(8,128)(2,1)}, bf16[128,2048]{0,1:T(8,128)(2,1)S(1)}, u32[]{:S(2)}) copy-start(bf16[128,2048]{0,1:T(8,128)(2,1)S(1)} %copy.134) | copy-start | bytes 1572868
  13.0 14.8 %copy-start.14 = (f32[128,32]{0,1:T(8,128)}, f32[128,32]{0,1:T(8,128)S(1)}, u32[]{:S(2)}) copy-start(f32[128,32]{0,1:T(8,128)S(1)} %get-tuple-element.342) | copy-start | bytes 49156
  17.6 10.2 %copy-start.6 = (f32[32,1024]{1,0:T(8,128)}, f32[32,1024]{1,0:T(8,128)S(1)}, u32[]{:S(2)}) copy-start(f32[32,1024]{1,0:T(8,128)S(1)} %copy.146) | copy-start | bytes 393220
  22.0 5.8 %copy-start.7 = (f32[32,1024]{1,0:T(8,128)}, f32[32,1024]{1,0:T(8,128)S(1)}, u32[]{:S(2)}) copy-start(f32[32,1024]{1,0:T(8,128)S(1)} %copy.138) | copy-start | bytes 393220
  22.1 8.8 %copy-start.18 = (f32[32,128]{1,0:T(8,128)}, f32[32,128]{1,0:T(8,128)S(1)}, u32[]{:S(2)}) copy-start(f32[32,128]{1,0:T(8,128)S(1)} %broadcast_in_dim.140) | copy-start | bytes 49156
  22.1 8.2 %collective-permute-start.6 = (f32[32,1152]{1,0:T(8,128)S(1)}, f32[32,1152]{1,0:T(8,128)S(1)}, u32[]{:S(2)}, u32[]{:S(2)}) collective-permute-start(f32[32,1152]{1,0:T(8,128)S(1)} %get-tuple-element.340), channel_id=1, source_target_pairs={{4,0},{8,4},{12,8},{16,12},{20,16},{24,20},{28,24},{32,28},{36,32}... | collective-permute-start | bytes 442376 | tf_op jit(solution)/shard_map/ppermute | solution.py:37
  23.4 7.5 %collective-permute-start = (f32[32,1152]{1,0:T(8,128)S(1)}, f32[32,1152]{1,0:T(8,128)S(1)}, u32[]{:S(2)}, u32[]{:S(2)}) collective-permute-start(f32[32,1152]{1,0:T(8,128)S(1)} %get-tuple-element.341), channel_id=1, source_target_pairs={{0,4},{4,8},{8,12},{12,16},{16,20},{20,24},{24,28},{28,32},{32,36}... | collective-permute-start | bytes 442376 | tf_op jit(solution)/shard_map/ppermute | solution.py:36
  31.8 0.7 copy-start.4
  34.7 20.4 %copy-start.5 = (f32[32,1024]{1,0:T(8,128)S(1)}, f32[32,1024]{1,0:T(8,128)}, u32[]{:S(2)}) copy-start(f32[32,1024]{1,0:T(8,128)} %copy-done.4) | copy-start | bytes 393220
  34.7 20.4 %copy-start.10 = (f32[32,1152]{1,0:T(8,128)S(1)}, f32[32,1152]{1,0:T(8,128)}, u32[]{:S(2)}) copy-start(f32[32,1152]{1,0:T(8,128)} %constant.83.clone.1) | copy-start | bytes 442372
  36.9 16.4 %collective-permute-start.7 = (f32[32,1152]{1,0:T(8,128)S(1)}, f32[32,1152]{1,0:T(8,128)S(1)}, u32[]{:S(2)}, u32[]{:S(2)}) collective-permute-start(f32[32,1152]{1,0:T(8,128)S(1)} %get-tuple-element.338), channel_id=1, source_target_pairs={{8,0},{12,4},{16,8},{20,12},{24,16},{28,20},{32,24},{36,28},{40,32... | collective-permute-start | bytes 442376 | tf_op jit(solution)/shard_map/ppermute | solution.py:37
  38.2 8.7 %collective-permute-start.1 = (f32[32,1152]{1,0:T(8,128)S(1)}, f32[32,1152]{1,0:T(8,128)S(1)}, u32[]{:S(2)}, u32[]{:S(2)}) collective-permute-start(f32[32,1152]{1,0:T(8,128)S(1)} %get-tuple-element.339), channel_id=1, source_target_pairs={{0,8},{4,12},{8,16},{12,20},{16,24},{20,28},{24,32},{28,36},{32,40... | collective-permute-start | bytes 442376 | tf_op jit(solution)/shard_map/ppermute | solution.py:36
  47.3 9.4 %collective-permute-start.2 = (f32[32,1152]{1,0:T(8,128)S(1)}, f32[32,1152]{1,0:T(8,128)S(1)}, u32[]{:S(2)}, u32[]{:S(2)}) collective-permute-start(f32[32,1152]{1,0:T(8,128)S(1)} %maximum_select_fusion.3), channel_id=1, source_target_pairs={{0,16},{4,20},{8,24},{12,28},{16,32},{20,36},{24,40},{28,44},{32,4... | collective-permute-start | bytes 442376 | tf_op jit(solution)/shard_map/ppermute | solution.py:36
  53.6 14.4 %collective-permute-start.8 = (f32[32,1152]{1,0:T(8,128)S(1)}, f32[32,1152]{1,0:T(8,128)S(1)}, u32[]{:S(2)}, u32[]{:S(2)}) collective-permute-start(f32[32,1152]{1,0:T(8,128)S(1)} %maximum_select_fusion.13), channel_id=1, source_target_pairs={{16,0},{20,4},{24,8},{28,12},{32,16},{36,20},{40,24},{44,28},{48,3... | collective-permute-start | bytes 442376 | tf_op jit(solution)/shard_map/ppermute | solution.py:37
  57.0 15.5 %collective-permute-start.3 = (f32[32,1152]{1,0:T(8,128)S(1)}, f32[32,1152]{1,0:T(8,128)S(1)}, u32[]{:S(2)}, u32[]{:S(2)}) collective-permute-start(f32[32,1152]{1,0:T(8,128)S(1)} %maximum_select_fusion.5), channel_id=1, source_target_pairs={{0,32},{4,36},{8,40},{12,44},{16,48},{20,52},{24,56},{28,60},{32,6... | collective-permute-start | bytes 442376 | tf_op jit(solution)/shard_map/ppermute | solution.py:36
  68.4 10.4 %collective-permute-start.9 = (f32[32,1152]{1,0:T(8,128)S(1)}, f32[32,1152]{1,0:T(8,128)S(1)}, u32[]{:S(2)}, u32[]{:S(2)}) collective-permute-start(f32[32,1152]{1,0:T(8,128)S(1)} %maximum_select_fusion.15), channel_id=1, source_target_pairs={{32,0},{36,4},{40,8},{44,12},{48,16},{52,20},{56,24},{60,28},{64,3... | collective-permute-start | bytes 442376 | tf_op jit(solution)/shard_map/ppermute | solution.py:37
  72.9 9.9 %collective-permute-start.4 = (f32[32,1152]{1,0:T(8,128)S(1)}, f32[32,1152]{1,0:T(8,128)S(1)}, u32[]{:S(2)}, u32[]{:S(2)}) collective-permute-start(f32[32,1152]{1,0:T(8,128)S(1)} %maximum_select_fusion.7), channel_id=1, source_target_pairs={{0,64},{4,68},{8,72},{12,76},{16,80},{20,84},{24,88},{28,92},{32,9... | collective-permute-start | bytes 442376 | tf_op jit(solution)/shard_map/ppermute | solution.py:36
  79.1 22.7 %collective-permute-start.10 = (f32[32,1152]{1,0:T(8,128)S(1)}, f32[32,1152]{1,0:T(8,128)S(1)}, u32[]{:S(2)}, u32[]{:S(2)}) collective-permute-start(f32[32,1152]{1,0:T(8,128)S(1)} %maximum_select_fusion.17), channel_id=1, source_target_pairs={{64,0},{68,4},{72,8},{76,12},{80,16},{84,20},{88,24},{92,28},{96,3... | collective-permute-start | bytes 442376 | tf_op jit(solution)/shard_map/ppermute | solution.py:37
  83.1 21.5 %collective-permute-start.5 = (f32[32,1152]{1,0:T(8,128)S(1)}, f32[32,1152]{1,0:T(8,128)S(1)}, u32[]{:S(2)}, u32[]{:S(2)}) collective-permute-start(f32[32,1152]{1,0:T(8,128)S(1)} %maximum_select_fusion.9), channel_id=1, source_target_pairs={{0,128},{4,132},{8,136},{12,140},{16,144},{20,148},{24,152},{28,15... | collective-permute-start | bytes 442376 | tf_op jit(solution)/shard_map/ppermute | solution.py:36
  102.1 11.8 %collective-permute-start.11 = (f32[32,1152]{1,0:T(8,128)S(1)}, f32[32,1152]{1,0:T(8,128)S(1)}, u32[]{:S(2)}, u32[]{:S(2)}) collective-permute-start(f32[32,1152]{1,0:T(8,128)S(1)} %maximum_select_fusion.19), channel_id=1, source_target_pairs={{128,0},{132,4},{136,8},{140,12},{144,16},{148,20},{152,24},{156,2... | collective-permute-start | bytes 442376 | tf_op jit(solution)/shard_map/ppermute | solution.py:37
  122.5 3.8 %copy-start.21 = (f32[128,8]{0,1:T(8,128)S(1)}, f32[128,8]{0,1:T(8,128)}, u32[]{:S(2)}) copy-start(f32[128,8]{0,1:T(8,128)} %copy.154) | copy-start | bytes 12292
  126.3 1.6 copy-start.11
  145.4 51.6 %copy-start.9 = (f32[1,128,32]{2,1,0:T(8,128)S(1)}, f32[1,128,32]{2,1,0:T(8,128)}, u32[]{:S(2)}) copy-start(f32[1,128,32]{2,1,0:T(8,128)} %copy-done.8) | copy-start | bytes 49156
  145.4 51.7 %copy-start.13 = (f32[128,16]{0,1:T(8,128)S(1)}, f32[128,16]{0,1:T(8,128)}, u32[]{:S(2)}) copy-start(f32[128,16]{0,1:T(8,128)} %param.21) | copy-start | bytes 24580
  145.4 51.7 %copy-start.20 = (f32[128,16]{0,1:T(8,128)S(1)}, f32[128,16]{0,1:T(8,128)}, u32[]{:S(2)}) copy-start(f32[128,16]{0,1:T(8,128)} %param.22) | copy-start | bytes 24580
  145.4 52.0 %copy-start.1 = (bf16[128,2048]{0,1:T(8,128)(2,1)S(1)}, bf16[128,2048]{0,1:T(8,128)(2,1)}, u32[]{:S(2)}) copy-start(bf16[128,2048]{0,1:T(8,128)(2,1)} %copy-done) | copy-start | bytes 1572868
  145.4 147.8 %all-to-all-start = ((bf16[64,128,2,1,128]{4,1,2,3,0:T(8,128)(2,1)}), bf16[64,128,2,1,128]{4,1,2,3,0:T(8,128)(2,1)}, u32[]{:S(2)}, u32[]{:S(2)}) async-start(bf16[64,128,2,1,128]{4,1,2,3,0:T(8,128)(2,1)} %copy.157), calls=%async_computation | async-start | bytes 8388608 | tf_op jit(solution)/shard_map/all_to_all | solution.py:161
  196.9 2.2 copy-start.3
  197.0 3.9 %copy-start.2 = (f32[32,1024]{0,1:T(8,128)S(1)}, f32[32,1024]{0,1:T(8,128)}, u32[]{:S(2)}) copy-start(f32[32,1024]{0,1:T(8,128)} %copy.143) | copy-start | bytes 393220
  197.0 4.2 %copy-start.15 = (f32[128,32]{0,1:T(8,128)S(1)}, f32[128,32]{0,1:T(8,128)}, u32[]{:S(2)}) copy-start(f32[128,32]{0,1:T(8,128)} %copy-done.14) | copy-start | bytes 49156
  199.2 6.3 %copy-start.17 = (f32[1,128,32]{1,2,0:T(8,128)S(1)}, f32[1,128,32]{1,2,0:T(8,128)}, u32[]{:S(2)}) copy-start(f32[1,128,32]{1,2,0:T(8,128)} %copy-done.16) | copy-start | bytes 49156
  200.2 7.5 %collective-permute-start.12 = (f32[128,16]{0,1:T(8,128)S(1)}, f32[128,16]{0,1:T(8,128)S(1)}, u32[]{:S(2)}, u32[]{:S(2)}) collective-permute-start(f32[128,16]{0,1:T(8,128)S(1)} %convolution_add_fusion.1), channel_id=1, source_target_pairs={{0,1},{1,0},{2,3},{3,2},{4,5},{5,4},{6,7},{7,6},{8,9},{9,8},{10,11... | collective-permute-start | bytes 24584 | tf_op jit(solution)/shard_map/ppermute | solution.py:54
  201.9 8.0 %collective-permute-start.14 = (f32[128,16]{0,1:T(8,128)S(1)}, f32[128,16]{0,1:T(8,128)S(1)}, u32[]{:S(2)}, u32[]{:S(2)}) collective-permute-start(f32[128,16]{0,1:T(8,128)S(1)} %convolution_add_fusion), channel_id=1, source_target_pairs={{0,1},{1,0},{2,3},{3,2},{4,5},{5,4},{6,7},{7,6},{8,9},{9,8},{10,11... | collective-permute-start | bytes 24584 | tf_op jit(solution)/shard_map/ppermute | solution.py:54
  207.7 6.3 %collective-permute-start.13 = (f32[128,16]{0,1:T(8,128)S(1)}, f32[128,16]{0,1:T(8,128)S(1)}, u32[]{:S(2)}, u32[]{:S(2)}) collective-permute-start(f32[128,16]{0,1:T(8,128)S(1)} %add.238), channel_id=1, source_target_pairs={{0,2},{1,3},{2,0},{3,1},{4,6},{5,7},{6,4},{7,5},{8,10},{9,11},{10,... | collective-permute-start | bytes 24584 | tf_op jit(solution)/shard_map/ppermute | solution.py:54
  209.9 5.2 %collective-permute-start.15 = (f32[128,16]{0,1:T(8,128)S(1)}, f32[128,16]{0,1:T(8,128)S(1)}, u32[]{:S(2)}, u32[]{:S(2)}) collective-permute-start(f32[128,16]{0,1:T(8,128)S(1)} %add.241), channel_id=1, source_target_pairs={{0,2},{1,3},{2,0},{3,1},{4,6},{5,7},{6,4},{7,5},{8,10},{9,11},{10,... | collective-permute-start | bytes 24584 | tf_op jit(solution)/shard_map/ppermute | solution.py:54
Sparse Core Ops, SparseCore 0:
  10.8 89.0 all-gather.1

commit v9 on v8

--- a/solution.py
+++ b/solution.py
@@ -147,10 +147,9 @@
         query_acc, acc = carry
         first_row = block_index * key_block
         query_add, key_term = block_terms(entry, first_row, key_block)
-        current = lax.dynamic_slice_in_dim(acc, first_row, key_block, 0)
         return (
             query_acc + query_add,
-            lax.dynamic_update_slice_in_dim(acc, current + key_term, first_row, 0),
+            lax.dynamic_update_slice_in_dim(acc, key_term, first_row, 0),
         )
 
     query_start = jnp.zeros(entry[0].shape, jnp.float32)

time: 305 us -> 293 us (0.961)
  other arithmetic: 23.8 us -> 17.8 us
  starting transfers between devices: 114 us -> 108 us
    all_to_all x1, starting transfers between devices: 51.6 us -> 45.3 us  [attention_grads(): parts = lax.all_to_all(parts, CTX, 0, 0, tiled=False)]
    convert_element_type x1 -> x0, other arithmetic: 3.92 us -> none  [attention_grads(): buffer.reshape(ctx_size, local_rows, *buffer.shape[1:]).astype(jnp.bfloat16)]
  transfers between devices with their start and end apart: 18 -> 18, of which waited for: 8 -> 8; matrix products, arithmetic and copies ran while one was open for 14% -> 15% of each run, Pallas kernels for 0% -> 0%
where the time goes in v9:
time: 293 us; the launch traced here: 292 us
  starting transfers between devices  108 us (37%)
  waiting for transfers between devices  94.6 us (32%)
  local copies, waits for them, and re-layouts  30.5 us (10%)
  matrix products  26 us (9%)
  other arithmetic  17.8 us (6%)
  between operations  14.8 us (5%)
    all_to_all x1, waiting for transfers between devices, attention_grads(): parts = lax.all_to_all(parts, CTX, 0, 0, tiled=False)  77.3 us
    ppermute x6, starting transfers between devices, carried_both(): got_fwd = lax.ppermute(fwd_total, axis, up)  49.2 us
    all_to_all x1, starting transfers between devices, attention_grads(): parts = lax.all_to_all(parts, CTX, 0, 0, tiled=False)  45.3 us
    ppermute x6, waiting for transfers between devices, carried_both(): got_fwd = lax.ppermute(fwd_total, axis, up)  8.96 us
    unnamed x53, local copies, waits for them, and re-layouts  8.79 us
    ppermute x6, waiting for transfers between devices, carried_both(): got_bwd = lax.ppermute(bwd_total, axis, down)  7.87 us
    ppermute x6, starting transfers between devices, carried_both(): got_bwd = lax.ppermute(bwd_total, axis, down)  7.75 us
  transfers between devices with their start and end apart: 18, of which 8 were waited for; matrix products, arithmetic and copies ran while one was open for 15% of the time, Pallas kernels for 0%

profile of v9, /device:TPU:2, one launch (start us, length us, event | category | flops | bytes accessed | tf_op | source)
XLA Modules:
  0.0 292.0 jit_solution(3107826428492546797)
XLA Ops:
  7.2 1.4 pad_maximum_fusion.4
  8.7 0.8 copy.135
  10.3 1.3 copy.144
  11.6 1.3 copy.134
  13.2 4.2 %fusion.52 = f32[32,64,16]{0,2,1:T(8,128)S(1)} fusion(f32[128,32,64]{0,2,1:T(8,128)S(1)} %bitcast.280, f32[128,16]{0,1:T(8,128)S(1)} %copy-done.19), kind=kOutput, calls=%fused_computation.65 | convolution fusion | flops 50331648 | bytes 1187840 | tf_op jit(solution)/shard_map/cshp,csn->chpn/dot_general | solution.py:185
  17.6 4.2 %fusion.54 = f32[32,64,16]{0,2,1:T(8,128)S(1)} fusion(f32[128,32,64]{0,2,1:T(8,128)S(1)} %bitcast.279, f32[128,16]{0,1:T(8,128)S(1)} %copy-done.12), kind=kOutput, calls=%fused_computation.67 | convolution fusion | flops 50331648 | bytes 1187840 | tf_op jit(solution)/shard_map/cshp,csn->chpn/dot_general | solution.py:184
  22.2 1.3 collective-permute-start.6
  23.5 3.0 %collective-permute-start = (f32[32,1152]{1,0:T(8,128)S(1)}, f32[32,1152]{1,0:T(8,128)S(1)}, u32[]{:S(2)}, u32[]{:S(2)}) collective-permute-start(f32[32,1152]{1,0:T(8,128)S(1)} %get-tuple-element.341), channel_id=1, source_target_pairs={{0,4},{4,8},{8,12},{12,16},{16,20},{20,24},{24,28},{28,32},{32,36}... | collective-permute-start | bytes 442376 | tf_op jit(solution)/shard_map/ppermute | solution.py:36
  26.6 1.3 multiply_reduce_fusion.3
  27.8 0.7 copy.154
  28.5 1.8 copy_bitcast_fusion
  30.3 0.7 copy.198
  31.0 0.7 copy.196
  31.9 0.6 copy-done.4
  32.6 1.0 copy.195
  33.6 1.2 multiply_add_fusion
  35.2 0.7 fusion.75
  36.0 1.0 maximum_select_fusion.11
  37.1 1.3 collective-permute-start.7
  38.4 4.6 %collective-permute-start.1 = (f32[32,1152]{1,0:T(8,128)S(1)}, f32[32,1152]{1,0:T(8,128)S(1)}, u32[]{:S(2)}, u32[]{:S(2)}) collective-permute-start(f32[32,1152]{1,0:T(8,128)S(1)} %get-tuple-element.339), channel_id=1, source_target_pairs={{0,8},{4,12},{8,16},{12,20},{16,24},{20,28},{24,32},{28,36},{32,40... | collective-permute-start | bytes 442376 | tf_op jit(solution)/shard_map/ppermute | solution.py:36
  42.9 0.7 broadcast_in_dim.273
  43.7 0.7 broadcast_in_dim.251
  44.4 1.0 maximum_select_fusion.10
  45.4 1.6 collective-permute-done.1
  47.4 6.0 %collective-permute-start.2 = (f32[32,1152]{1,0:T(8,128)S(1)}, f32[32,1152]{1,0:T(8,128)S(1)}, u32[]{:S(2)}, u32[]{:S(2)}) collective-permute-start(f32[32,1152]{1,0:T(8,128)S(1)} %maximum_select_fusion.3), channel_id=1, source_target_pairs={{0,16},{4,20},{8,24},{12,28},{16,32},{20,36},{24,40},{28,44},{32,4... | collective-permute-start | bytes 442376 | tf_op jit(solution)/shard_map/ppermute | solution.py:36
  53.8 1.3 collective-permute-start.8
  55.3 1.6 collective-permute-done.2
  57.2 10.9 %collective-permute-start.3 = (f32[32,1152]{1,0:T(8,128)S(1)}, f32[32,1152]{1,0:T(8,128)S(1)}, u32[]{:S(2)}, u32[]{:S(2)}) collective-permute-start(f32[32,1152]{1,0:T(8,128)S(1)} %maximum_select_fusion.5), channel_id=1, source_target_pairs={{0,32},{4,36},{8,40},{12,44},{16,48},{20,52},{24,56},{28,60},{32,6... | collective-permute-start | bytes 442376 | tf_op jit(solution)/shard_map/ppermute | solution.py:36
  68.5 1.3 collective-permute-start.9
  69.9 2.6 collective-permute-done.3
  72.9 6.0 %collective-permute-start.4 = (f32[32,1152]{1,0:T(8,128)S(1)}, f32[32,1152]{1,0:T(8,128)S(1)}, u32[]{:S(2)}, u32[]{:S(2)}) collective-permute-start(f32[32,1152]{1,0:T(8,128)S(1)} %maximum_select_fusion.7), channel_id=1, source_target_pairs={{0,64},{4,68},{8,72},{12,76},{16,80},{20,84},{24,88},{28,92},{32,9... | collective-permute-start | bytes 442376 | tf_op jit(solution)/shard_map/ppermute | solution.py:36
  79.2 1.3 collective-permute-start.10
  80.7 2.1 collective-permute-done.4
  83.2 18.7 %collective-permute-start.5 = (f32[32,1152]{1,0:T(8,128)S(1)}, f32[32,1152]{1,0:T(8,128)S(1)}, u32[]{:S(2)}, u32[]{:S(2)}) collective-permute-start(f32[32,1152]{1,0:T(8,128)S(1)} %maximum_select_fusion.9), channel_id=1, source_target_pairs={{0,128},{4,132},{8,136},{12,140},{16,144},{20,148},{24,152},{28,15... | collective-permute-start | bytes 442376 | tf_op jit(solution)/shard_map/ppermute | solution.py:36
  102.2 1.3 collective-permute-start.11
  103.7 1.1 collective-permute-done.5
  105.0 1.0 copy.143
  106.0 7.9 %collective-permute-done.11 = f32[32,1152]{1,0:T(8,128)S(1)} collective-permute-done((f32[32,1152]{1,0:T(8,128)S(1)}, f32[32,1152]{1,0:T(8,128)S(1)}, u32[]{:S(2)}, u32[]{:S(2)}) %collective-permute-start.11) | collective-permute-done | bytes 147488 | tf_op jit(solution)/shard_map/ppermute | solution.py:37
  114.2 1.0 copy.151
  115.2 3.9 %fusion.78 = (bf16[8192,1,128]{2,0,1:T(8,128)(2,1)}, bf16[8192,1,128]{2,0,1:T(8,128)(2,1)S(1)}) fusion(bf16[8192,2,128]{2,0,1:T(8,128)(2,1)} %all-gather.2.cloned.1.call-done), kind=kLoop, calls=%fused_computation.195 | loop fusion | bytes 8388608 | tf_op jit(solution)/shard_map/slice | solution.py:73
  119.1 3.4 %while.26 = (s32[]{:T(128)}, f32[1,128,8]{1,2,0:T(8,128)S(1)}, f32[1,128,8]{1,2,0:T(8,128)S(1)}, s32[]{:T(128)}, bf16[8192,1,128]{2,0,1:T(8,128)(2,1)S(1)}, /*in...) while((s32[]{:T(128)}, f32[1,128,8]{1,2,0:T(8,128)S(1)}, ...), condition=%wide.region_4.5_spmd.clone, body=%wide.region_1.4_spmd.clone.sunk | while | flops 551817344 | bytes 18420912 | solution.py:113
  119.4 1.2 fusion.111
  120.7 1.7 exponential_reduce_fusion.2
  122.5 2.3 broadcast_in_dim.139
  124.8 10.8 %while.27 = (s32[]{:T(128)}, f32[128,1,8,128]{0,3,2,1:T(8,128)S(1)}, bf16[8192,2,1,128]{3,0,2,1:T(8,128)(2,1)}, s32[]{:T(128)}, bf16[8192,1,128]{2,0,1:T(8,128)(...) while((s32[]{:T(128)}, ...), condition=%wide.region_7.8_spmd.clone, body=%wide.region_6.7_spmd.clone.sunk | while | flops 2709915648 | bytes 46429428 | solution.py:156
  124.8 1.3 fusion.122
  126.4 4.0 %fusion.123 = bf16[128,8,2048]{0,2,1:T(8,128)(2,1)S(1)} fusion(f32[2048,128,8]{1,0,2:T(8,128)S(1)} %fusion.122, f32[128,8]{0,1:T(8,128)S(1)} %get-tuple-element.542, f32[128,8]{0,1:T(8,128)S(1)} %bitcast.289, pred[128,2048]{0,1:T(8,128)(4,1)S(1)} %broadcast_compare_fusion.5, bf16[8192,1,128]{2,0,1:T(8,128)(2,1)} %get-tuple-element.540, ...), kind=kOutput, calls=%fused_computation.17.clone.1 | convolution fusion | flops 551550976 | bytes 13639684 | tf_op jit(solution)/shard_map/while/body/tgrd,kgd->gtrk/dot_general | solution.py:122
  130.4 0.8 fusion.124
  131.2 2.0 fusion.125
  133.2 1.3 convolution_bitcast_fusion.4
  134.5 1.1 maximum_dynamic-update-slice_fusion.2
  135.5 4.8 %copy.157 = bf16[64,128,2,1,128]{4,1,2,3,0:T(8,128)(2,1)} copy(bf16[64,128,2,1,128]{4,1,0,2,3:T(8,128)(2,1)} %bitcast.267) | data formatting | bytes 8388608 | tf_op jit(solution)/shard_map/convert_element_type | solution.py:159
  140.3 45.3 %all-to-all-start = ((bf16[64,128,2,1,128]{4,1,2,3,0:T(8,128)(2,1)}), bf16[64,128,2,1,128]{4,1,2,3,0:T(8,128)(2,1)}, u32[]{:S(2)}, u32[]{:S(2)}) async-start(bf16[64,128,2,1,128]{4,1,2,3,0:T(8,128)(2,1)} %copy.157), calls=%async_computation | async-start | bytes 8388608 | tf_op jit(solution)/shard_map/all_to_all | solution.py:160
  186.1 1.7 multiply_reduce_fusion
  190.4 1.6 collective-permute-start.14
  192.2 1.8 fusion.45
  194.2 1.8 fusion.49
  196.4 2.2 collective-permute-start.13
  198.6 1.4 collective-permute-start.15
  200.0 0.9 copy.155
  201.0 1.0 copy.166
  202.0 0.7 copy.167
  204.4 77.3 %all-to-all-done = bf16[64,128,2,1,128]{4,1,2,3,0:T(8,128)(2,1)} async-done(((bf16[64,128,2,1,128]{4,1,2,3,0:T(8,128)(2,1)}), bf16[64,128,2,1,128]{4,1,2,3,0:T(8,128)(2,1)}, u32[]{:S(2)}, u32[]{:S(2)}) %all-to-all-start) | async-done | bytes 4194336 | tf_op jit(solution)/shard_map/all_to_all | solution.py:160
  281.7 2.9 reduce.15
  (171 shorter events, 12.9 us)
Async XLA Ops:
  7.2 6.0 %copy-start.19 = (f32[128,16]{0,1:T(8,128)S(1)}, f32[128,16]{0,1:T(8,128)}, u32[]{:S(2)}) copy-start(f32[128,16]{0,1:T(8,128)} %param.22) | copy-start | bytes 24580
  7.2 10.4 %copy-start.12 = (f32[128,16]{0,1:T(8,128)S(1)}, f32[128,16]{0,1:T(8,128)}, u32[]{:S(2)}) copy-start(f32[128,16]{0,1:T(8,128)} %param.21) | copy-start | bytes 24580
  7.2 108.0 %all-gather.2.cloned.1.call-start = ((), (), s32[]{:S(2)}) async-start(), calls=%async_computation.1 | async-start | bytes 4259840 | tf_op jit(solution)/shard_map/all_gather | solution.py:71
  9.7 0.6 copy-start.8
  9.7 12.4 %copy-start.22 = (f32[32]{0:T(128)}, f32[32]{0:T(128)S(1)}, u32[]{:S(2)}) copy-start(f32[32]{0:T(128)S(1)} %fusion.77) | copy-start | bytes 388
  10.3 11.6 %copy-start.16 = (f32[1,128,32]{1,2,0:T(8,128)}, f32[1,128,32]{1,2,0:T(8,128)S(1)}, u32[]{:S(2)}) copy-start(f32[1,128,32]{1,2,0:T(8,128)S(1)} %copy.136) | copy-start | bytes 49156
  12.9 13.6 %copy-start = (bf16[128,2048]{0,1:T(8,128)(2,1)}, bf16[128,2048]{0,1:T(8,128)(2,1)S(1)}, u32[]{:S(2)}) copy-start(bf16[128,2048]{0,1:T(8,128)(2,1)S(1)} %copy.134) | copy-start | bytes 1572868
  13.0 14.8 %copy-start.14 = (f32[128,32]{0,1:T(8,128)}, f32[128,32]{0,1:T(8,128)S(1)}, u32[]{:S(2)}) copy-start(f32[128,32]{0,1:T(8,128)S(1)} %get-tuple-element.342) | copy-start | bytes 49156
  17.6 10.2 %copy-start.6 = (f32[32,1024]{1,0:T(8,128)}, f32[32,1024]{1,0:T(8,128)S(1)}, u32[]{:S(2)}) copy-start(f32[32,1024]{1,0:T(8,128)S(1)} %copy.146) | copy-start | bytes 393220
  22.0 5.8 %copy-start.7 = (f32[32,1024]{1,0:T(8,128)}, f32[32,1024]{1,0:T(8,128)S(1)}, u32[]{:S(2)}) copy-start(f32[32,1024]{1,0:T(8,128)S(1)} %copy.138) | copy-start | bytes 393220
  22.1 8.9 %copy-start.18 = (f32[32,128]{1,0:T(8,128)}, f32[32,128]{1,0:T(8,128)S(1)}, u32[]{:S(2)}) copy-start(f32[32,128]{1,0:T(8,128)S(1)} %broadcast_in_dim.140) | copy-start | bytes 49156
  22.2 8.2 %collective-permute-start.6 = (f32[32,1152]{1,0:T(8,128)S(1)}, f32[32,1152]{1,0:T(8,128)S(1)}, u32[]{:S(2)}, u32[]{:S(2)}) collective-permute-start(f32[32,1152]{1,0:T(8,128)S(1)} %get-tuple-element.340), channel_id=1, source_target_pairs={{4,0},{8,4},{12,8},{16,12},{20,16},{24,20},{28,24},{32,28},{36,32}... | collective-permute-start | bytes 442376 | tf_op jit(solution)/shard_map/ppermute | solution.py:37
  23.5 7.5 %collective-permute-start = (f32[32,1152]{1,0:T(8,128)S(1)}, f32[32,1152]{1,0:T(8,128)S(1)}, u32[]{:S(2)}, u32[]{:S(2)}) collective-permute-start(f32[32,1152]{1,0:T(8,128)S(1)} %get-tuple-element.341), channel_id=1, source_target_pairs={{0,4},{4,8},{8,12},{12,16},{16,20},{20,24},{24,28},{28,32},{32,36}... | collective-permute-start | bytes 442376 | tf_op jit(solution)/shard_map/ppermute | solution.py:36
  31.9 0.7 copy-start.4
  34.8 20.4 %copy-start.5 = (f32[32,1024]{1,0:T(8,128)S(1)}, f32[32,1024]{1,0:T(8,128)}, u32[]{:S(2)}) copy-start(f32[32,1024]{1,0:T(8,128)} %copy-done.4) | copy-start | bytes 393220
  34.8 20.4 %copy-start.10 = (f32[32,1152]{1,0:T(8,128)S(1)}, f32[32,1152]{1,0:T(8,128)}, u32[]{:S(2)}) copy-start(f32[32,1152]{1,0:T(8,128)} %constant.83.clone.1) | copy-start | bytes 442372
  37.1 16.4 %collective-permute-start.7 = (f32[32,1152]{1,0:T(8,128)S(1)}, f32[32,1152]{1,0:T(8,128)S(1)}, u32[]{:S(2)}, u32[]{:S(2)}) collective-permute-start(f32[32,1152]{1,0:T(8,128)S(1)} %get-tuple-element.338), channel_id=1, source_target_pairs={{8,0},{12,4},{16,8},{20,12},{24,16},{28,20},{32,24},{36,28},{40,32... | collective-permute-start | bytes 442376 | tf_op jit(solution)/shard_map/ppermute | solution.py:37
  38.4 8.7 %collective-permute-start.1 = (f32[32,1152]{1,0:T(8,128)S(1)}, f32[32,1152]{1,0:T(8,128)S(1)}, u32[]{:S(2)}, u32[]{:S(2)}) collective-permute-start(f32[32,1152]{1,0:T(8,128)S(1)} %get-tuple-element.339), channel_id=1, source_target_pairs={{0,8},{4,12},{8,16},{12,20},{16,24},{20,28},{24,32},{28,36},{32,40... | collective-permute-start | bytes 442376 | tf_op jit(solution)/shard_map/ppermute | solution.py:36
  47.4 9.4 %collective-permute-start.2 = (f32[32,1152]{1,0:T(8,128)S(1)}, f32[32,1152]{1,0:T(8,128)S(1)}, u32[]{:S(2)}, u32[]{:S(2)}) collective-permute-start(f32[32,1152]{1,0:T(8,128)S(1)} %maximum_select_fusion.3), channel_id=1, source_target_pairs={{0,16},{4,20},{8,24},{12,28},{16,32},{20,36},{24,40},{28,44},{32,4... | collective-permute-start | bytes 442376 | tf_op jit(solution)/shard_map/ppermute | solution.py:36
  53.8 14.3 %collective-permute-start.8 = (f32[32,1152]{1,0:T(8,128)S(1)}, f32[32,1152]{1,0:T(8,128)S(1)}, u32[]{:S(2)}, u32[]{:S(2)}) collective-permute-start(f32[32,1152]{1,0:T(8,128)S(1)} %maximum_select_fusion.13), channel_id=1, source_target_pairs={{16,0},{20,4},{24,8},{28,12},{32,16},{36,20},{40,24},{44,28},{48,3... | collective-permute-start | bytes 442376 | tf_op jit(solution)/shard_map/ppermute | solution.py:37
  57.2 15.4 %collective-permute-start.3 = (f32[32,1152]{1,0:T(8,128)S(1)}, f32[32,1152]{1,0:T(8,128)S(1)}, u32[]{:S(2)}, u32[]{:S(2)}) collective-permute-start(f32[32,1152]{1,0:T(8,128)S(1)} %maximum_select_fusion.5), channel_id=1, source_target_pairs={{0,32},{4,36},{8,40},{12,44},{16,48},{20,52},{24,56},{28,60},{32,6... | collective-permute-start | bytes 442376 | tf_op jit(solution)/shard_map/ppermute | solution.py:36
  68.5 10.4 %collective-permute-start.9 = (f32[32,1152]{1,0:T(8,128)S(1)}, f32[32,1152]{1,0:T(8,128)S(1)}, u32[]{:S(2)}, u32[]{:S(2)}) collective-permute-start(f32[32,1152]{1,0:T(8,128)S(1)} %maximum_select_fusion.15), channel_id=1, source_target_pairs={{32,0},{36,4},{40,8},{44,12},{48,16},{52,20},{56,24},{60,28},{64,3... | collective-permute-start | bytes 442376 | tf_op jit(solution)/shard_map/ppermute | solution.py:37
  72.9 9.9 %collective-permute-start.4 = (f32[32,1152]{1,0:T(8,128)S(1)}, f32[32,1152]{1,0:T(8,128)S(1)}, u32[]{:S(2)}, u32[]{:S(2)}) collective-permute-start(f32[32,1152]{1,0:T(8,128)S(1)} %maximum_select_fusion.7), channel_id=1, source_target_pairs={{0,64},{4,68},{8,72},{12,76},{16,80},{20,84},{24,88},{28,92},{32,9... | collective-permute-start | bytes 442376 | tf_op jit(solution)/shard_map/ppermute | solution.py:36
  79.2 22.6 %collective-permute-start.10 = (f32[32,1152]{1,0:T(8,128)S(1)}, f32[32,1152]{1,0:T(8,128)S(1)}, u32[]{:S(2)}, u32[]{:S(2)}) collective-permute-start(f32[32,1152]{1,0:T(8,128)S(1)} %maximum_select_fusion.17), channel_id=1, source_target_pairs={{64,0},{68,4},{72,8},{76,12},{80,16},{84,20},{88,24},{92,28},{96,3... | collective-permute-start | bytes 442376 | tf_op jit(solution)/shard_map/ppermute | solution.py:37
  83.2 21.6 %collective-permute-start.5 = (f32[32,1152]{1,0:T(8,128)S(1)}, f32[32,1152]{1,0:T(8,128)S(1)}, u32[]{:S(2)}, u32[]{:S(2)}) collective-permute-start(f32[32,1152]{1,0:T(8,128)S(1)} %maximum_select_fusion.9), channel_id=1, source_target_pairs={{0,128},{4,132},{8,136},{12,140},{16,144},{20,148},{24,152},{28,15... | collective-permute-start | bytes 442376 | tf_op jit(solution)/shard_map/ppermute | solution.py:36
  102.2 11.7 %collective-permute-start.11 = (f32[32,1152]{1,0:T(8,128)S(1)}, f32[32,1152]{1,0:T(8,128)S(1)}, u32[]{:S(2)}, u32[]{:S(2)}) collective-permute-start(f32[32,1152]{1,0:T(8,128)S(1)} %maximum_select_fusion.19), channel_id=1, source_target_pairs={{128,0},{132,4},{136,8},{140,12},{144,16},{148,20},{152,24},{156,2... | collective-permute-start | bytes 442376 | tf_op jit(solution)/shard_map/ppermute | solution.py:37
  122.4 2.3 copy-start.21
  124.8 1.6 copy-start.11
  140.3 45.4 %copy-start.9 = (f32[1,128,32]{2,1,0:T(8,128)S(1)}, f32[1,128,32]{2,1,0:T(8,128)}, u32[]{:S(2)}) copy-start(f32[1,128,32]{2,1,0:T(8,128)} %copy-done.8) | copy-start | bytes 49156
  140.3 45.5 %copy-start.13 = (f32[128,16]{0,1:T(8,128)S(1)}, f32[128,16]{0,1:T(8,128)}, u32[]{:S(2)}) copy-start(f32[128,16]{0,1:T(8,128)} %param.21) | copy-start | bytes 24580
  140.3 45.5 %copy-start.20 = (f32[128,16]{0,1:T(8,128)S(1)}, f32[128,16]{0,1:T(8,128)}, u32[]{:S(2)}) copy-start(f32[128,16]{0,1:T(8,128)} %param.22) | copy-start | bytes 24580
  140.3 45.8 %copy-start.1 = (bf16[128,2048]{0,1:T(8,128)(2,1)S(1)}, bf16[128,2048]{0,1:T(8,128)(2,1)}, u32[]{:S(2)}) copy-start(bf16[128,2048]{0,1:T(8,128)(2,1)} %copy-done) | copy-start | bytes 1572868
  140.3 141.3 %all-to-all-start = ((bf16[64,128,2,1,128]{4,1,2,3,0:T(8,128)(2,1)}), bf16[64,128,2,1,128]{4,1,2,3,0:T(8,128)(2,1)}, u32[]{:S(2)}, u32[]{:S(2)}) async-start(bf16[64,128,2,1,128]{4,1,2,3,0:T(8,128)(2,1)} %copy.157), calls=%async_computation | async-start | bytes 8388608 | tf_op jit(solution)/shard_map/all_to_all | solution.py:160
  185.7 2.2 copy-start.3
  185.7 3.7 %copy-start.2 = (f32[32,1024]{0,1:T(8,128)S(1)}, f32[32,1024]{0,1:T(8,128)}, u32[]{:S(2)}) copy-start(f32[32,1024]{0,1:T(8,128)} %copy.143) | copy-start | bytes 393220
  185.7 4.0 %copy-start.15 = (f32[128,32]{0,1:T(8,128)S(1)}, f32[128,32]{0,1:T(8,128)}, u32[]{:S(2)}) copy-start(f32[128,32]{0,1:T(8,128)} %copy-done.14) | copy-start | bytes 49156
  187.9 6.3 %copy-start.17 = (f32[1,128,32]{1,2,0:T(8,128)S(1)}, f32[1,128,32]{1,2,0:T(8,128)}, u32[]{:S(2)}) copy-start(f32[1,128,32]{1,2,0:T(8,128)} %copy-done.16) | copy-start | bytes 49156
  188.9 7.5 %collective-permute-start.12 = (f32[128,16]{0,1:T(8,128)S(1)}, f32[128,16]{0,1:T(8,128)S(1)}, u32[]{:S(2)}, u32[]{:S(2)}) collective-permute-start(f32[128,16]{0,1:T(8,128)S(1)} %convolution_add_fusion.1), channel_id=1, source_target_pairs={{0,1},{1,0},{2,3},{3,2},{4,5},{5,4},{6,7},{7,6},{8,9},{9,8},{10,11... | collective-permute-start | bytes 24584 | tf_op jit(solution)/shard_map/ppermute | solution.py:54
  190.4 8.3 %collective-permute-start.14 = (f32[128,16]{0,1:T(8,128)S(1)}, f32[128,16]{0,1:T(8,128)S(1)}, u32[]{:S(2)}, u32[]{:S(2)}) collective-permute-start(f32[128,16]{0,1:T(8,128)S(1)} %convolution_add_fusion), channel_id=1, source_target_pairs={{0,1},{1,0},{2,3},{3,2},{4,5},{5,4},{6,7},{7,6},{8,9},{9,8},{10,11... | collective-permute-start | bytes 24584 | tf_op jit(solution)/shard_map/ppermute | solution.py:54
  196.4 6.3 %collective-permute-start.13 = (f32[128,16]{0,1:T(8,128)S(1)}, f32[128,16]{0,1:T(8,128)S(1)}, u32[]{:S(2)}, u32[]{:S(2)}) collective-permute-start(f32[128,16]{0,1:T(8,128)S(1)} %add.234), channel_id=1, source_target_pairs={{0,2},{1,3},{2,0},{3,1},{4,6},{5,7},{6,4},{7,5},{8,10},{9,11},{10,... | collective-permute-start | bytes 24584 | tf_op jit(solution)/shard_map/ppermute | solution.py:54
  198.6 5.2 %collective-permute-start.15 = (f32[128,16]{0,1:T(8,128)S(1)}, f32[128,16]{0,1:T(8,128)S(1)}, u32[]{:S(2)}, u32[]{:S(2)}) collective-permute-start(f32[128,16]{0,1:T(8,128)S(1)} %add.237), channel_id=1, source_target_pairs={{0,2},{1,3},{2,0},{3,1},{4,6},{5,7},{6,4},{7,5},{8,10},{9,11},{10,... | collective-permute-start | bytes 24584 | tf_op jit(solution)/shard_map/ppermute | solution.py:54
Sparse Core Ops, SparseCore 0:
  10.8 89.1 all-gather.1

commit v10 on v9

--- a/solution.py
+++ b/solution.py
@@ -69,7 +69,13 @@
     score_scale = 1.0 / math.sqrt(head_width)
     whole_kv = jnp.concatenate([key_vectors, value_vectors], axis=1)
     whole_kv = lax.all_gather(whole_kv, CTX, axis=0, tiled=True)
-    whole_kv, carried = lax.optimization_barrier((whole_kv, carried))
+    row_count = queries.shape[0]
+    out_dots = jnp.sum(
+        grad_attention.astype(jnp.float32) * attention_out.astype(jnp.float32), axis=-1
+    )
+    out_dots = out_dots.reshape(row_count, local_groups, repeats).transpose(1, 0, 2)
+    buffer = jnp.zeros((whole_kv.shape[0], 2, local_groups, head_width), jnp.float32)
+    whole_kv, carried, out_dots, buffer = lax.optimization_barrier((whole_kv, carried, out_dots, buffer))
     whole_keys, whole_values = (whole_kv[:, :local_groups], whole_kv[:, local_groups:])
     all_tokens = whole_keys.shape[0]
     key_block = math.gcd(all_tokens, 2048)
@@ -87,13 +93,8 @@
         return (jnp.where(allowed[None, :, None, :], scores, -jnp.inf), key_part)
 
     first_pos = here * local_rows
-    row_count = queries.shape[0]
     query_grp = queries.reshape(row_count, local_groups, repeats, head_width)
     grad_grp = grad_attention.reshape(row_count, local_groups, repeats, head_width)
-    out_dots = jnp.sum(
-        grad_attention.astype(jnp.float32) * attention_out.astype(jnp.float32), axis=-1
-    )
-    out_dots = out_dots.reshape(row_count, local_groups, repeats).transpose(1, 0, 2)
     query_pos = first_pos + jnp.arange(row_count)
     last_query = first_pos + row_count - 1
     live_blocks = last_query // key_block + 1
@@ -140,7 +141,6 @@
         key_term = jnp.stack([keys_term, value_term], axis=1)
         return (query_add, key_term)
 
-    buffer = jnp.zeros((all_tokens, 2, local_groups, head_width), jnp.float32)
     entry = entries
 
     def joint_step(block_index, carry, entry=entry):

time: 293 us -> 294 us (level)
  waiting for transfers between devices: 94.6 us -> 89.3 us
  matrix products: 26 us -> 29.4 us
    all_to_all x1, waiting for transfers between devices: 77.3 us -> 71.8 us  [attention_grads(): parts = lax.all_to_all(parts, CTX, 0, 0, tiled=False)]
    unnamed x53 -> x59, local copies, waits for them, and re-layouts: 8.79 us -> 8.11 us
  transfers between devices with their start and end apart: 18 -> 18, of which waited for: 8 -> 8; matrix products, arithmetic and copies ran while one was open for 15% -> 17% of each run, Pallas kernels for 0% -> 0%
where the time goes in v10:
time: 294 us; the launch traced here: 292 us
  starting transfers between devices  108 us (37%)
  waiting for transfers between devices  89.3 us (30%)
  local copies, waits for them, and re-layouts  29.7 us (10%)
  matrix products  29.4 us (10%)
  other arithmetic  20.6 us (7%)
  between operations  14.8 us (5%)
    all_to_all x1, waiting for transfers between devices, attention_grads(): parts = lax.all_to_all(parts, CTX, 0, 0, tiled=False)  71.8 us
    ppermute x6, starting transfers between devices, carried_both(): got_fwd = lax.ppermute(fwd_total, axis, up)  49.3 us
    all_to_all x1, starting transfers between devices, attention_grads(): parts = lax.all_to_all(parts, CTX, 0, 0, tiled=False)  45.3 us
    ppermute x6, waiting for transfers between devices, carried_both(): got_fwd = lax.ppermute(fwd_total, axis, up)  9.04 us
    unnamed x59, local copies, waits for them, and re-layouts  8.11 us
    ppermute x6, waiting for transfers between devices, carried_both(): got_bwd = lax.ppermute(bwd_total, axis, down)  7.89 us
    ppermute x6, starting transfers between devices, carried_both(): got_bwd = lax.ppermute(bwd_total, axis, down)  7.75 us
  transfers between devices with their start and end apart: 18, of which 8 were waited for; matrix products, arithmetic and copies ran while one was open for 17% of the time, Pallas kernels for 0%

profile of v10, /device:TPU:2, one launch (start us, length us, event | category | flops | bytes accessed | tf_op | source)
XLA Modules:
  0.0 291.9 jit_solution(2661538419833995301)
XLA Ops:
  7.2 1.4 pad_maximum_fusion.4
  8.7 0.8 copy.135
  10.3 1.3 copy.144
  11.6 1.3 copy.134
  13.2 4.2 %fusion.52 = f32[32,64,16]{0,2,1:T(8,128)S(1)} fusion(f32[128,32,64]{0,2,1:T(8,128)S(1)} %bitcast.284, f32[128,16]{0,1:T(8,128)S(1)} %copy-done.19), kind=kOutput, calls=%fused_computation.65 | convolution fusion | flops 50331648 | bytes 1187840 | tf_op jit(solution)/shard_map/cshp,csn->chpn/dot_general | solution.py:185
  17.6 4.2 %fusion.54 = f32[32,64,16]{0,2,1:T(8,128)S(1)} fusion(f32[128,32,64]{0,2,1:T(8,128)S(1)} %bitcast.283, f32[128,16]{0,1:T(8,128)S(1)} %copy-done.13), kind=kOutput, calls=%fused_computation.67 | convolution fusion | flops 50331648 | bytes 1187840 | tf_op jit(solution)/shard_map/cshp,csn->chpn/dot_general | solution.py:184
  22.2 1.3 collective-permute-start.6
  23.5 3.0 %collective-permute-start = (f32[32,1152]{1,0:T(8,128)S(1)}, f32[32,1152]{1,0:T(8,128)S(1)}, u32[]{:S(2)}, u32[]{:S(2)}) collective-permute-start(f32[32,1152]{1,0:T(8,128)S(1)} %get-tuple-element.345), channel_id=1, source_target_pairs={{0,4},{4,8},{8,12},{12,16},{16,20},{20,24},{24,28},{28,32},{32,36}... | collective-permute-start | bytes 442376 | tf_op jit(solution)/shard_map/ppermute | solution.py:36
  26.5 1.8 copy_bitcast_fusion
  28.4 1.9 multiply_reduce_fusion.3
  32.4 1.0 copy.195
  33.4 1.2 multiply_add_fusion
  35.0 0.7 fusion.75
  35.8 1.0 maximum_select_fusion.11
  36.8 1.3 collective-permute-start.7
  38.1 4.6 %collective-permute-start.1 = (f32[32,1152]{1,0:T(8,128)S(1)}, f32[32,1152]{1,0:T(8,128)S(1)}, u32[]{:S(2)}, u32[]{:S(2)}) collective-permute-start(f32[32,1152]{1,0:T(8,128)S(1)} %get-tuple-element.343), channel_id=1, source_target_pairs={{0,8},{4,12},{8,16},{12,20},{16,24},{20,28},{24,32},{28,36},{32,40... | collective-permute-start | bytes 442376 | tf_op jit(solution)/shard_map/ppermute | solution.py:36
  42.7 0.7 broadcast_in_dim.273
  43.4 0.7 broadcast_in_dim.142
  44.1 1.0 maximum_select_fusion.10
  45.1 1.7 collective-permute-done.1
  47.2 6.0 %collective-permute-start.2 = (f32[32,1152]{1,0:T(8,128)S(1)}, f32[32,1152]{1,0:T(8,128)S(1)}, u32[]{:S(2)}, u32[]{:S(2)}) collective-permute-start(f32[32,1152]{1,0:T(8,128)S(1)} %maximum_select_fusion.3), channel_id=1, source_target_pairs={{0,16},{4,20},{8,24},{12,28},{16,32},{20,36},{24,40},{28,44},{32,4... | collective-permute-start | bytes 442376 | tf_op jit(solution)/shard_map/ppermute | solution.py:36
  53.6 1.3 collective-permute-start.8
  55.0 1.6 collective-permute-done.2
  56.9 11.1 %collective-permute-start.3 = (f32[32,1152]{1,0:T(8,128)S(1)}, f32[32,1152]{1,0:T(8,128)S(1)}, u32[]{:S(2)}, u32[]{:S(2)}) collective-permute-start(f32[32,1152]{1,0:T(8,128)S(1)} %maximum_select_fusion.5), channel_id=1, source_target_pairs={{0,32},{4,36},{8,40},{12,44},{16,48},{20,52},{24,56},{28,60},{32,6... | collective-permute-start | bytes 442376 | tf_op jit(solution)/shard_map/ppermute | solution.py:36
  68.4 1.3 collective-permute-start.9
  69.9 2.5 collective-permute-done.3
  72.8 5.9 %collective-permute-start.4 = (f32[32,1152]{1,0:T(8,128)S(1)}, f32[32,1152]{1,0:T(8,128)S(1)}, u32[]{:S(2)}, u32[]{:S(2)}) collective-permute-start(f32[32,1152]{1,0:T(8,128)S(1)} %maximum_select_fusion.7), channel_id=1, source_target_pairs={{0,64},{4,68},{8,72},{12,76},{16,80},{20,84},{24,88},{28,92},{32,9... | collective-permute-start | bytes 442376 | tf_op jit(solution)/shard_map/ppermute | solution.py:36
  79.0 1.3 collective-permute-start.10
  80.5 2.2 collective-permute-done.4
  83.1 18.7 %collective-permute-start.5 = (f32[32,1152]{1,0:T(8,128)S(1)}, f32[32,1152]{1,0:T(8,128)S(1)}, u32[]{:S(2)}, u32[]{:S(2)}) collective-permute-start(f32[32,1152]{1,0:T(8,128)S(1)} %maximum_select_fusion.9), channel_id=1, source_target_pairs={{0,128},{4,132},{8,136},{12,140},{16,144},{20,148},{24,152},{28,15... | collective-permute-start | bytes 442376 | tf_op jit(solution)/shard_map/ppermute | solution.py:36
  102.2 1.3 collective-permute-start.11
  103.6 1.0 collective-permute-done.5
  105.0 1.0 copy.143
  106.0 7.9 %collective-permute-done.11 = f32[32,1152]{1,0:T(8,128)S(1)} collective-permute-done((f32[32,1152]{1,0:T(8,128)S(1)}, f32[32,1152]{1,0:T(8,128)S(1)}, u32[]{:S(2)}, u32[]{:S(2)}) %collective-permute-start.11) | collective-permute-done | bytes 147488 | tf_op jit(solution)/shard_map/ppermute | solution.py:37
  114.2 1.0 copy.151
  115.2 3.9 %fusion.78 = (bf16[8192,1,128]{2,0,1:T(8,128)(2,1)}, bf16[8192,1,128]{2,0,1:T(8,128)(2,1)S(1)}) fusion(bf16[8192,2,128]{2,0,1:T(8,128)(2,1)} %all-gather.2.cloned.1.call-done), kind=kLoop, calls=%fused_computation.195 | loop fusion | bytes 8388608 | tf_op jit(solution)/shard_map/slice | solution.py:79
  119.1 3.4 %while.26 = (s32[]{:T(128)}, f32[1,128,8]{1,2,0:T(8,128)S(1)}, f32[1,128,8]{1,2,0:T(8,128)S(1)}, s32[]{:T(128)}, bf16[8192,1,128]{2,0,1:T(8,128)(2,1)S(1)}, /*in...) while((s32[]{:T(128)}, f32[1,128,8]{1,2,0:T(8,128)S(1)}, ...), condition=%wide.region_5.6_spmd.clone, body=%wide.region_2.5_spmd.clone.sunk | while | flops 551817344 | bytes 18420912 | solution.py:114
  119.4 1.2 fusion.111
  120.7 1.7 exponential_reduce_fusion.2
  122.5 2.3 broadcast_in_dim.294
  124.8 10.8 %while.27 = (s32[]{:T(128)}, f32[128,1,8,128]{0,3,2,1:T(8,128)S(1)}, bf16[8192,2,1,128]{3,0,2,1:T(8,128)(2,1)}, s32[]{:T(128)}, bf16[8192,1,128]{2,0,1:T(8,128)(...) while((s32[]{:T(128)}, ...), condition=%wide.region_7.8_spmd.clone, body=%wide.region_6.7_spmd.clone.sunk | while | flops 2709915648 | bytes 46429428 | solution.py:156
  124.9 1.3 fusion.122
  126.5 4.0 %fusion.123 = bf16[128,8,2048]{0,2,1:T(8,128)(2,1)S(1)} fusion(f32[2048,128,8]{1,0,2:T(8,128)S(1)} %fusion.122, f32[128,8]{0,1:T(8,128)S(1)} %bitcast.294, f32[128,8]{0,1:T(8,128)S(1)} %bitcast.295, pred[128,2048]{0,1:T(8,128)(4,1)S(1)} %broadcast_compare_fusion.5, bf16[8192,1,128]{2,0,1:T(8,128)(2,1)} %get-tuple-element.544, s32[]{:T(128)S(6)} %select_n.277, ...), kind=kOutput, calls=%fused_computation.17.clone.1 | convolution fusion | flops 551550976 | bytes 13639684 | tf_op jit(solution)/shard_map/while/body/tgrd,kgd->gtrk/dot_general | solution.py:123
  130.5 0.8 fusion.124
  131.3 1.9 fusion.125
  133.3 1.3 convolution_bitcast_fusion.4
  134.5 1.1 maximum_dynamic-update-slice_fusion.2
  135.6 4.7 %copy.157 = bf16[64,128,2,1,128]{4,1,2,3,0:T(8,128)(2,1)} copy(bf16[64,128,2,1,128]{4,1,0,2,3:T(8,128)(2,1)} %bitcast.271) | data formatting | bytes 8388608 | tf_op jit(solution)/shard_map/convert_element_type | solution.py:159
  140.3 45.3 %all-to-all-start = ((bf16[64,128,2,1,128]{4,1,2,3,0:T(8,128)(2,1)}), bf16[64,128,2,1,128]{4,1,2,3,0:T(8,128)(2,1)}, u32[]{:S(2)}, u32[]{:S(2)}) async-start(bf16[64,128,2,1,128]{4,1,2,3,0:T(8,128)(2,1)} %copy.157), calls=%async_computation | async-start | bytes 8388608 | tf_op jit(solution)/shard_map/all_to_all | solution.py:160
  186.1 2.3 multiply_reduce_fusion
  189.3 0.8 convolution_add_fusion.1
  191.4 0.8 convolution_add_fusion
  192.2 1.5 collective-permute-start.14
  194.0 2.5 fusion.45
  196.7 0.8 fusion.67
  197.4 2.6 fusion.49
  200.5 0.7 add.234
  201.2 2.1 collective-permute-start.13
  203.3 0.7 add.237
  204.0 1.4 collective-permute-start.15
  205.4 0.9 copy.155
  206.4 1.0 copy.166
  209.8 71.8 %all-to-all-done = bf16[64,128,2,1,128]{4,1,2,3,0:T(8,128)(2,1)} async-done(((bf16[64,128,2,1,128]{4,1,2,3,0:T(8,128)(2,1)}), bf16[64,128,2,1,128]{4,1,2,3,0:T(8,128)(2,1)}, u32[]{:S(2)}, u32[]{:S(2)}) %all-to-all-start) | async-done | bytes 4194336 | tf_op jit(solution)/shard_map/all_to_all | solution.py:160
  281.6 2.9 reduce.15
  (177 shorter events, 15.3 us)
Async XLA Ops:
  7.2 6.0 %copy-start.19 = (f32[128,16]{0,1:T(8,128)S(1)}, f32[128,16]{0,1:T(8,128)}, u32[]{:S(2)}) copy-start(f32[128,16]{0,1:T(8,128)} %param.22) | copy-start | bytes 24580
  7.2 10.4 %copy-start.13 = (f32[128,16]{0,1:T(8,128)S(1)}, f32[128,16]{0,1:T(8,128)}, u32[]{:S(2)}) copy-start(f32[128,16]{0,1:T(8,128)} %param.21) | copy-start | bytes 24580
  7.2 108.0 %all-gather.2.cloned.1.call-start = ((), (), s32[]{:S(2)}) async-start(), calls=%async_computation.1 | async-start | bytes 4259840 | tf_op jit(solution)/shard_map/all_gather | solution.py:71
  9.6 0.6 copy-start.8
  9.7 12.4 %copy-start.25 = (f32[32]{0:T(128)}, f32[32]{0:T(128)S(1)}, u32[]{:S(2)}) copy-start(f32[32]{0:T(128)S(1)} %fusion.77) | copy-start | bytes 388
  10.3 11.6 %copy-start.17 = (f32[1,128,32]{1,2,0:T(8,128)}, f32[1,128,32]{1,2,0:T(8,128)S(1)}, u32[]{:S(2)}) copy-start(f32[1,128,32]{1,2,0:T(8,128)S(1)} %copy.136) | copy-start | bytes 49156
  12.9 15.5 %copy-start = (bf16[128,2048]{0,1:T(8,128)(2,1)}, bf16[128,2048]{0,1:T(8,128)(2,1)S(1)}, u32[]{:S(2)}) copy-start(bf16[128,2048]{0,1:T(8,128)(2,1)S(1)} %copy.134) | copy-start | bytes 1572868
  13.0 8.9 %copy-start.15 = (f32[128,32]{0,1:T(8,128)}, f32[128,32]{0,1:T(8,128)S(1)}, u32[]{:S(2)}) copy-start(f32[128,32]{0,1:T(8,128)S(1)} %get-tuple-element.346) | copy-start | bytes 49156
  17.6 5.9 %copy-start.6 = (f32[32,1024]{1,0:T(8,128)}, f32[32,1024]{1,0:T(8,128)S(1)}, u32[]{:S(2)}) copy-start(f32[32,1024]{1,0:T(8,128)S(1)} %copy.146) | copy-start | bytes 393220
  22.0 1.4 copy-start.7
  22.1 9.4 %copy-start.18 = (f32[32,128]{1,0:T(8,128)}, f32[32,128]{1,0:T(8,128)S(1)}, u32[]{:S(2)}) copy-start(f32[32,128]{1,0:T(8,128)S(1)} %broadcast_in_dim.140) | copy-start | bytes 49156
  22.2 8.1 %collective-permute-start.6 = (f32[32,1152]{1,0:T(8,128)S(1)}, f32[32,1152]{1,0:T(8,128)S(1)}, u32[]{:S(2)}, u32[]{:S(2)}) collective-permute-start(f32[32,1152]{1,0:T(8,128)S(1)} %get-tuple-element.344), channel_id=1, source_target_pairs={{4,0},{8,4},{12,8},{16,12},{20,16},{24,20},{28,24},{32,28},{36,32}... | collective-permute-start | bytes 442376 | tf_op jit(solution)/shard_map/ppermute | solution.py:37
  23.5 7.4 %collective-permute-start = (f32[32,1152]{1,0:T(8,128)S(1)}, f32[32,1152]{1,0:T(8,128)S(1)}, u32[]{:S(2)}, u32[]{:S(2)}) collective-permute-start(f32[32,1152]{1,0:T(8,128)S(1)} %get-tuple-element.345), channel_id=1, source_target_pairs={{0,4},{4,8},{8,12},{12,16},{16,20},{20,24},{24,28},{28,32},{32,36}... | collective-permute-start | bytes 442376 | tf_op jit(solution)/shard_map/ppermute | solution.py:36
  31.7 0.7 copy-start.4
  34.6 20.4 %copy-start.5 = (f32[32,1024]{1,0:T(8,128)S(1)}, f32[32,1024]{1,0:T(8,128)}, u32[]{:S(2)}) copy-start(f32[32,1024]{1,0:T(8,128)} %copy-done.4) | copy-start | bytes 393220
  34.6 20.4 %copy-start.10 = (f32[32,1152]{1,0:T(8,128)S(1)}, f32[32,1152]{1,0:T(8,128)}, u32[]{:S(2)}) copy-start(f32[32,1152]{1,0:T(8,128)} %constant.78.clone.1) | copy-start | bytes 442372
  36.8 16.4 %collective-permute-start.7 = (f32[32,1152]{1,0:T(8,128)S(1)}, f32[32,1152]{1,0:T(8,128)S(1)}, u32[]{:S(2)}, u32[]{:S(2)}) collective-permute-start(f32[32,1152]{1,0:T(8,128)S(1)} %get-tuple-element.342), channel_id=1, source_target_pairs={{8,0},{12,4},{16,8},{20,12},{24,16},{28,20},{32,24},{36,28},{40,32... | collective-permute-start | bytes 442376 | tf_op jit(solution)/shard_map/ppermute | solution.py:37
  38.1 8.7 %collective-permute-start.1 = (f32[32,1152]{1,0:T(8,128)S(1)}, f32[32,1152]{1,0:T(8,128)S(1)}, u32[]{:S(2)}, u32[]{:S(2)}) collective-permute-start(f32[32,1152]{1,0:T(8,128)S(1)} %get-tuple-element.343), channel_id=1, source_target_pairs={{0,8},{4,12},{8,16},{12,20},{16,24},{20,28},{24,32},{28,36},{32,40... | collective-permute-start | bytes 442376 | tf_op jit(solution)/shard_map/ppermute | solution.py:36
  47.2 9.4 %collective-permute-start.2 = (f32[32,1152]{1,0:T(8,128)S(1)}, f32[32,1152]{1,0:T(8,128)S(1)}, u32[]{:S(2)}, u32[]{:S(2)}) collective-permute-start(f32[32,1152]{1,0:T(8,128)S(1)} %maximum_select_fusion.3), channel_id=1, source_target_pairs={{0,16},{4,20},{8,24},{12,28},{16,32},{20,36},{24,40},{28,44},{32,4... | collective-permute-start | bytes 442376 | tf_op jit(solution)/shard_map/ppermute | solution.py:36
  53.6 14.5 %collective-permute-start.8 = (f32[32,1152]{1,0:T(8,128)S(1)}, f32[32,1152]{1,0:T(8,128)S(1)}, u32[]{:S(2)}, u32[]{:S(2)}) collective-permute-start(f32[32,1152]{1,0:T(8,128)S(1)} %maximum_select_fusion.13), channel_id=1, source_target_pairs={{16,0},{20,4},{24,8},{28,12},{32,16},{36,20},{40,24},{44,28},{48,3... | collective-permute-start | bytes 442376 | tf_op jit(solution)/shard_map/ppermute | solution.py:37
  56.9 15.5 %collective-permute-start.3 = (f32[32,1152]{1,0:T(8,128)S(1)}, f32[32,1152]{1,0:T(8,128)S(1)}, u32[]{:S(2)}, u32[]{:S(2)}) collective-permute-start(f32[32,1152]{1,0:T(8,128)S(1)} %maximum_select_fusion.5), channel_id=1, source_target_pairs={{0,32},{4,36},{8,40},{12,44},{16,48},{20,52},{24,56},{28,60},{32,6... | collective-permute-start | bytes 442376 | tf_op jit(solution)/shard_map/ppermute | solution.py:36
  68.4 10.3 %collective-permute-start.9 = (f32[32,1152]{1,0:T(8,128)S(1)}, f32[32,1152]{1,0:T(8,128)S(1)}, u32[]{:S(2)}, u32[]{:S(2)}) collective-permute-start(f32[32,1152]{1,0:T(8,128)S(1)} %maximum_select_fusion.15), channel_id=1, source_target_pairs={{32,0},{36,4},{40,8},{44,12},{48,16},{52,20},{56,24},{60,28},{64,3... | collective-permute-start | bytes 442376 | tf_op jit(solution)/shard_map/ppermute | solution.py:37
  72.8 9.9 %collective-permute-start.4 = (f32[32,1152]{1,0:T(8,128)S(1)}, f32[32,1152]{1,0:T(8,128)S(1)}, u32[]{:S(2)}, u32[]{:S(2)}) collective-permute-start(f32[32,1152]{1,0:T(8,128)S(1)} %maximum_select_fusion.7), channel_id=1, source_target_pairs={{0,64},{4,68},{8,72},{12,76},{16,80},{20,84},{24,88},{28,92},{32,9... | collective-permute-start | bytes 442376 | tf_op jit(solution)/shard_map/ppermute | solution.py:36
  79.0 22.8 %collective-permute-start.10 = (f32[32,1152]{1,0:T(8,128)S(1)}, f32[32,1152]{1,0:T(8,128)S(1)}, u32[]{:S(2)}, u32[]{:S(2)}) collective-permute-start(f32[32,1152]{1,0:T(8,128)S(1)} %maximum_select_fusion.17), channel_id=1, source_target_pairs={{64,0},{68,4},{72,8},{76,12},{80,16},{84,20},{88,24},{92,28},{96,3... | collective-permute-start | bytes 442376 | tf_op jit(solution)/shard_map/ppermute | solution.py:37
  83.1 21.6 %collective-permute-start.5 = (f32[32,1152]{1,0:T(8,128)S(1)}, f32[32,1152]{1,0:T(8,128)S(1)}, u32[]{:S(2)}, u32[]{:S(2)}) collective-permute-start(f32[32,1152]{1,0:T(8,128)S(1)} %maximum_select_fusion.9), channel_id=1, source_target_pairs={{0,128},{4,132},{8,136},{12,140},{16,144},{20,148},{24,152},{28,15... | collective-permute-start | bytes 442376 | tf_op jit(solution)/shard_map/ppermute | solution.py:36
  102.2 11.7 %collective-permute-start.11 = (f32[32,1152]{1,0:T(8,128)S(1)}, f32[32,1152]{1,0:T(8,128)S(1)}, u32[]{:S(2)}, u32[]{:S(2)}) collective-permute-start(f32[32,1152]{1,0:T(8,128)S(1)} %maximum_select_fusion.19), channel_id=1, source_target_pairs={{128,0},{132,4},{136,8},{140,12},{144,16},{148,20},{152,24},{156,2... | collective-permute-start | bytes 442376 | tf_op jit(solution)/shard_map/ppermute | solution.py:37
  119.1 3.4 %copy-start.11 = (f32[128,8]{1,0:T(8,128)S(1)}, f32[128,8]{1,0:T(8,128)}, u32[]{:S(2)}) copy-start(f32[128,8]{1,0:T(8,128)} %multiply_reduce_fusion.3) | copy-start | bytes 12292
  124.9 1.6 copy-start.12
  140.3 45.3 %copy-start.9 = (f32[1,128,32]{2,1,0:T(8,128)S(1)}, f32[1,128,32]{2,1,0:T(8,128)}, u32[]{:S(2)}) copy-start(f32[1,128,32]{2,1,0:T(8,128)} %copy-done.8) | copy-start | bytes 49156
  140.3 45.4 %copy-start.14 = (f32[128,16]{0,1:T(8,128)S(1)}, f32[128,16]{0,1:T(8,128)}, u32[]{:S(2)}) copy-start(f32[128,16]{0,1:T(8,128)} %param.21) | copy-start | bytes 24580
  140.3 45.4 %copy-start.20 = (f32[128,16]{0,1:T(8,128)S(1)}, f32[128,16]{0,1:T(8,128)}, u32[]{:S(2)}) copy-start(f32[128,16]{0,1:T(8,128)} %param.22) | copy-start | bytes 24580
  140.3 45.8 %copy-start.1 = (bf16[128,2048]{0,1:T(8,128)(2,1)S(1)}, bf16[128,2048]{0,1:T(8,128)(2,1)}, u32[]{:S(2)}) copy-start(bf16[128,2048]{0,1:T(8,128)(2,1)} %copy-done) | copy-start | bytes 1572868
  140.3 141.3 %all-to-all-start = ((bf16[64,128,2,1,128]{4,1,2,3,0:T(8,128)(2,1)}), bf16[64,128,2,1,128]{4,1,2,3,0:T(8,128)(2,1)}, u32[]{:S(2)}, u32[]{:S(2)}) async-start(bf16[64,128,2,1,128]{4,1,2,3,0:T(8,128)(2,1)} %copy.157), calls=%async_computation | async-start | bytes 8388608 | tf_op jit(solution)/shard_map/all_to_all | solution.py:160
  185.6 2.8 copy-start.3
  185.6 4.9 %copy-start.2 = (f32[32,1024]{0,1:T(8,128)S(1)}, f32[32,1024]{0,1:T(8,128)}, u32[]{:S(2)}) copy-start(f32[32,1024]{0,1:T(8,128)} %copy.143) | copy-start | bytes 393220
  185.6 5.2 %copy-start.16 = (f32[128,32]{0,1:T(8,128)S(1)}, f32[128,32]{0,1:T(8,128)}, u32[]{:S(2)}) copy-start(f32[128,32]{0,1:T(8,128)} %copy-done.15) | copy-start | bytes 49156
  185.7 2.7 copy-start.22
  185.8 5.6 %copy-start.24 = (pred[128,128]{1,0:T(8,128)(4,1)}, pred[128,128]{1,0:T(8,128)(4,1)S(1)}, u32[]{:S(2)}) copy-start(pred[128,128]{1,0:T(8,128)(4,1)S(1)} %iota_compare_fusion) | copy-start | bytes 49156
  186.1 5.3 %copy-start.21 = (f32[128,128]{1,0:T(8,128)}, f32[128,128]{1,0:T(8,128)S(1)}, u32[]{:S(2)}) copy-start(f32[128,128]{1,0:T(8,128)S(1)} %fusion.79) | copy-start | bytes 196612
  190.0 10.4 %collective-permute-start.12 = (f32[128,16]{0,1:T(8,128)}, f32[128,16]{0,1:T(8,128)}, u32[]{:S(2)}, u32[]{:S(2)}) collective-permute-start(f32[128,16]{0,1:T(8,128)} %convolution_add_fusion.1), channel_id=1, source_target_pairs={{0,1},{1,0},{2,3},{3,2},{4,5},{5,4},{6,7},{7,6},{8,9},{9,8},{10,11... | collective-permute-start | bytes 24584 | tf_op jit(solution)/shard_map/ppermute | solution.py:54
  190.9 6.6 %copy-start.23 = (f32[32,128]{1,0:T(8,128)S(1)}, f32[32,128]{1,0:T(8,128)}, u32[]{:S(2)}) copy-start(f32[32,128]{1,0:T(8,128)} %copy-done.22) | copy-start | bytes 49156
  192.2 11.1 %collective-permute-start.14 = (f32[128,16]{0,1:T(8,128)}, f32[128,16]{0,1:T(8,128)S(1)}, u32[]{:S(2)}, u32[]{:S(2)}) collective-permute-start(f32[128,16]{0,1:T(8,128)} %convolution_add_fusion), channel_id=1, source_target_pairs={{0,1},{1,0},{2,3},{3,2},{4,5},{5,4},{6,7},{7,6},{8,9},{9,8},{10,11... | collective-permute-start | bytes 24584 | tf_op jit(solution)/shard_map/ppermute | solution.py:54
  201.2 6.9 %collective-permute-start.13 = (f32[128,16]{0,1:T(8,128)S(1)}, f32[128,16]{0,1:T(8,128)S(1)}, u32[]{:S(2)}, u32[]{:S(2)}) collective-permute-start(f32[128,16]{0,1:T(8,128)S(1)} %add.234), channel_id=1, source_target_pairs={{0,2},{1,3},{2,0},{3,1},{4,6},{5,7},{6,4},{7,5},{8,10},{9,11},{10,... | collective-permute-start | bytes 24584 | tf_op jit(solution)/shard_map/ppermute | solution.py:54
  204.0 5.2 %collective-permute-start.15 = (f32[128,16]{0,1:T(8,128)S(1)}, f32[128,16]{0,1:T(8,128)S(1)}, u32[]{:S(2)}, u32[]{:S(2)}) collective-permute-start(f32[128,16]{0,1:T(8,128)S(1)} %add.237), channel_id=1, source_target_pairs={{0,2},{1,3},{2,0},{3,1},{4,6},{5,7},{6,4},{7,5},{8,10},{9,11},{10,... | collective-permute-start | bytes 24584 | tf_op jit(solution)/shard_map/ppermute | solution.py:54
Sparse Core Ops, SparseCore 0:
  10.8 89.1 all-gather.1
